TPU v7x, 512 devices: a whole 4x8x8 slice. The times are simulated.
512 devices in a mesh: mem: 128 (over z, y, core), dom: 4 (over x).
Axes of the slice: x: 4, y: 8, z: 8, core: 2. Of those that a mesh axis runs over, the one named last changes fastest.
Arguments:
- fcst_pert: float32 [2, 1024, 4, 16384], P(None, 'mem', 'dom'), may hold values from -6 to 6
- sensitivity: float32 [2, 64, 4, 16384], P(None, None, 'dom', 'mem'), may hold values from -6 to 6
- obs_pert: float32 [393216, 1024], P(('mem', 'dom')), may hold values from -6 to 6
- weighted_innovation: float32 [393216], P(('mem', 'dom')), may hold values from -8 to 8
- obs_lists: int32 [128, 16], replicated, may hold values from 0 to 3071, as said below
- block_taper: float32 [128, 16], replicated, may hold values from 0.2 to 1
- counts: int32 [128], replicated, may hold values from 8 to 16, as said below
Outputs:
- impact: float32 [393216, 128], P(('mem', 'dom'))
Inputs may be any that keep to these rules, and one draw needn't show every extreme that they name: `obs_lists`: each row's ids are distinct, and every id names an observation block whose column block is within one of the row's column block, cyclically. Observation block o belongs to column block o // 24 and region (o // 6) % 4. The first 8 slots of each row name, for every region, one block of the column block before and one of the column block after. `counts`: some column block uses all 16 slots.
All inputs are finite; a program needn't handle non-finite values.
Results may differ from a plain program's by a relative error of at most 0.0003.
Values sent between devices are 32-bit elements; how exact they have to be, the bound alone decides.
No kernel may reach another device: no remote copies, remote signals or barrier semaphores. Data moves between devices by JAX's collectives and lax.ppermute only.
A program may use at most 128 MiB of HBM per device.

v0:
```python
import jax
import jax.numpy as jnp
from jax import lax
from jax.sharding import PartitionSpec as P

M = 1024
OBSB = 128


def extended(cells, sides, width):
    for axis, dim in sides:
        count = lax.axis_size(axis)
        head = lax.slice_in_dim(cells, 0, width, axis=dim)
        tail = lax.slice_in_dim(cells, cells.shape[dim] - width, cells.shape[dim], axis=dim)
        cells = jnp.concatenate(
            [
                lax.ppermute(tail, axis, [(i, (i + 1) % count) for i in range(count)]),
                cells,
                lax.ppermute(head, axis, [((i + 1) % count, i) for i in range(count)]),
            ],
            axis=dim,
        )
    return cells


def from_behind(block, axis, distance):
    devices = range(lax.axis_size(axis))
    route = [((i - distance) % len(devices), i) for i in devices]
    return lax.ppermute(block, axis, route)


def block_weights(
    obs_lists, block_taper, counts, column_index, region_index, owned_blocks, regions
):
    row_ids = lax.dynamic_index_in_dim(obs_lists, column_index, 0, keepdims=False)
    row_taper = lax.dynamic_index_in_dim(block_taper, column_index, 0, keepdims=False)
    row_count = lax.dynamic_index_in_dim(counts, column_index, 0, keepdims=False)
    slot_live = jnp.arange(row_ids.shape[0], dtype=jnp.int32) < row_count
    column_count = obs_lists.shape[0]
    owner_columns = (column_index + jnp.arange(3, dtype=jnp.int32) - 1) % column_count
    owner_ids = (owner_columns[:, None] * regions + region_index) * owned_blocks + jnp.arange(
        owned_blocks, dtype=jnp.int32
    )[None, :]
    matched = (owner_ids[:, :, None] == row_ids[None, None, :]) & slot_live[None, None, :]
    return jnp.sum(
        jnp.where(matched, row_taper[None, None, :], jnp.zeros((), row_taper.dtype)), axis=2
    )


def body(fcst_pert, sensitivity, obs_pert, weighted_innovation, obs_lists, block_taper, counts):
    regrouped = lax.all_to_all(fcst_pert, "mem", split_axis=3, concat_axis=1, tiled=True)
    leads = regrouped.shape[0]
    members = regrouped.shape[1]
    targets = sensitivity.shape[1]
    per_lead = []
    for lead in range(leads):
        left = regrouped[lead].reshape(members, -1)
        right = sensitivity[lead].reshape(targets, -1)
        per_lead.append(
            lax.dot_general(left, right, (((1,), (1,)), ((), ())), precision=lax.Precision.HIGHEST)
        )
    partial_sums = jnp.concatenate(per_lead, axis=1)
    summed = lax.psum(partial_sums, "dom")
    regions = lax.axis_size("dom")
    column_index = lax.axis_index("mem")
    region_index = lax.axis_index("dom")
    owned_rows = obs_pert.shape[0]
    owned_blocks = owned_rows // OBSB
    row_scale = weighted_innovation / (M - 1)
    neighbour_rows = extended(obs_pert, (("mem", 0),), owned_rows)
    weight_rows = block_weights(
        obs_lists, block_taper, counts, column_index, region_index, owned_blocks, regions
    )
    products = jnp.dot(neighbour_rows, summed, precision=lax.Precision.HIGHEST)
    products = products.reshape(3, owned_blocks, OBSB, -1) * weight_rows[:, :, None, None]
    gathered = products[1]
    for direction in (1, -1):
        gathered = gathered + from_behind(products[1 + direction], "mem", direction)
    result = gathered.reshape(owned_rows, -1)
    return result * row_scale[:, None]


def solution(mesh):
    in_specs = (
        P(None, "mem", "dom", None),
        P(None, None, "dom", "mem"),
        P(("mem", "dom"), None),
        P(("mem", "dom")),
        P(),
        P(),
        P(),
    )
    out_specs = P(("mem", "dom"), None)
    return jax.shard_map(body, mesh=mesh, in_specs=in_specs, out_specs=out_specs, check_vma=False)
```

profile of v0, /device:TPU:249, one launch (start us, length us, event | category | flops | bytes accessed | tf_op | source)
XLA Modules:
  0.0 230.2 jit_solution(6720938939552736385)
XLA Ops:
  6.5 0.0 copy-start
  6.5 17.4 %copy.18 = f32[2,8,1,16384]{1,0,2,3:T(2,128)} copy(f32[2,8,1,16384]{3,2,1,0:T(1,128)} %param.7) | data formatting | bytes 2097152 | tf_op args[0]
  23.9 0.0 copy-start.4
  23.9 0.0 copy-start.2
  23.9 0.0 copy-start.1
  23.9 25.2 %reshape.66 = f32[128,1,2048]{2,1,0:T(1,128)} reshape(f32[16384,1,2,8]{3,2,1,0:T(2,128)} %bitcast.31) | data formatting | bytes 2097152
  49.2 14.6 %all-to-all-start = ((f32[128,1,2048]{2,1,0:T(1,128)}), f32[128,1,2048]{2,1,0:T(1,128)S(1)}, u32[]{:S(2)}, u32[]{:S(2)}) async-start(f32[128,1,2048]{2,1,0:T(1,128)} %reshape.66), calls=%async_computation | async-start | bytes 2097152 | tf_op jit(solution)/shard_map/all_to_all | solution.py:51
  63.7 0.0 all-reduce.2.cloned.1.call-start
  63.8 4.6 %collective-permute-start = (f32[768,1024]{1,0:T(8,128)}, f32[768,1024]{1,0:T(8,128)}, u32[]{:S(2)}, u32[]{:S(2)}) collective-permute-start(f32[768,1024]{1,0:T(8,128)} %param.9), channel_id=1, source_target_pairs={{0,4},{4,8},{8,12},{12,16},{16,20},{20,24},{24,28},{28,32},{32,36}... | collective-permute-start | bytes 9437192 | tf_op jit(solution)/shard_map/ppermute | solution.py:17
  68.4 2.1 collective-permute-start.1
  70.5 0.0 copy-done.4
  70.5 0.6 dynamic_slice.13
  71.1 0.0 copy-done
  71.1 0.2 dynamic-slice_reduce_fusion
  71.3 0.0 copy-done.2
  71.3 0.2 dynamic-slice_reduce_fusion.1
  71.5 0.0 copy-done.1
  71.5 19.6 %all-to-all-done = f32[128,1,2048]{2,1,0:T(1,128)S(1)} async-done(((f32[128,1,2048]{2,1,0:T(1,128)}), f32[128,1,2048]{2,1,0:T(1,128)S(1)}, u32[]{:S(2)}, u32[]{:S(2)}) %all-to-all-start) | async-done | bytes 1048608 | tf_op jit(solution)/shard_map/all_to_all | solution.py:51
  91.1 0.5 broadcast.88
  91.6 3.1 %reduce.4 = f32[128,2048]{1,0:T(8,128)S(1)} reduce(f32[128,1,2048]{2,1,0:T(1,128)S(1)} %all-to-all-done, f32[]{:T(128)} %broadcast.88), dimensions={1}, to_apply=%all_to_all.11.reduce_sub_computation | reduce | bytes 2097156 | tf_op jit(solution)/shard_map/all_to_all | solution.py:51
  94.7 26.7 %reshape.67 = f32[16384,1,2,8]{3,2,1,0:T(2,128)} reshape(f32[128,2048]{1,0:T(8,128)S(1)} %reduce.4) | data formatting | bytes 2097152
  121.4 17.6 %copy.19 = f32[2,8,1,16384]{3,2,1,0:T(1,128)S(1)} copy(f32[2,8,1,16384]{1,0,2,3:T(2,128)} %bitcast.30) | data formatting | bytes 2097152 | tf_op jit(solution)/shard_map/all_to_all | solution.py:51
  139.1 0.1 fusion.19
  139.1 1.0 fusion.6
  140.1 1.0 fusion.8
  141.1 0.8 pad_maximum_fusion
  141.9 0.0 all-reduce.2.cloned.1.call-update
  141.9 0.6 iota_compare_fusion
  142.6 0.1 iota_add_fusion
  142.7 0.2 select_reduce_fusion
  142.8 48.7 %all-reduce.2.cloned.1.call-done = f32[1024,128]{0,1:T(8,128)} async-done(((f32[1024,128]{0,1:T(8,128)}), f32[1024,128]{0,1:T(8,128)}) %all-reduce.2.cloned.1.call-update) | async-done | bytes 524304 | tf_op jit(solution)/shard_map/psum | solution.py:63
  191.5 0.0 collective-permute-done
  191.5 0.0 collective-permute-done.1
  191.5 11.3 %fusion = f32[2304,128]{1,0:T(8,128)S(1)} fusion(f32[1024,128]{0,1:T(8,128)} %all-reduce.2.cloned.1.call-done, f32[768,1024]{1,0:T(8,128)} %collective-permute-done.1, f32[768,1024]{1,0:T(8,128)} %param.9, f32[768,1024]{1,0:T(8,128)} %collective-permute-done), kind=kOutput, calls=%fused_computation | convolution fusion | flops 3628597248 | bytes 11141120 | tf_op jit(solution)/shard_map/dot_general | solution.py:74
  202.9 0.0 copy-start.3
  202.9 0.1 broadcast_multiply_fusion
  203.0 0.1 slice_bitcast_fusion.1
  203.1 6.9 %collective-permute-start.2 = (f32[6,128,128]{2,1,0:T(8,128)S(1)}, f32[6,128,128]{2,1,0:T(8,128)S(1)}, u32[]{:S(2)}, u32[]{:S(2)}) collective-permute-start(f32[6,128,128]{2,1,0:T(8,128)S(1)} %get-tuple-element.5), channel_id=1, source_target_pairs={{508,0},{0,4},{4,8},{8,12},{12,16},{16,20},{20,24},{24,28},{28,32}... | collective-permute-start | bytes 1179656 | tf_op jit(solution)/shard_map/ppermute | solution.py:29
  210.0 1.9 collective-permute-start.3
  211.9 0.0 copy-done.3
  211.9 2.8 %collective-permute-done.2 = f32[6,128,128]{2,1,0:T(8,128)S(1)} collective-permute-done((f32[6,128,128]{2,1,0:T(8,128)S(1)}, f32[6,128,128]{2,1,0:T(8,128)S(1)}, u32[]{:S(2)}, u32[]{:S(2)}) %collective-permute-start.2) | collective-permute-done | bytes 393248 | tf_op jit(solution)/shard_map/ppermute | solution.py:29
  214.7 7.7 %collective-permute-done.3 = f32[6,128,128]{2,1,0:T(8,128)S(1)} collective-permute-done((f32[6,128,128]{2,1,0:T(8,128)S(1)}, f32[6,128,128]{2,1,0:T(8,128)S(1)}, u32[]{:S(2)}, u32[]{:S(2)}) %collective-permute-start.3) | collective-permute-done | bytes 393248 | tf_op jit(solution)/shard_map/ppermute | solution.py:29
  222.4 0.1 fusion.13
  222.5 0.9 bitcast_multiply_fusion
  (3 shorter events, 0.0 us)
Async XLA Ops:
  6.5 64.6 %copy-start = (f32[128,16]{0,1:T(8,128)S(1)}, f32[128,16]{0,1:T(8,128)}, u32[]{:S(2)}) copy-start(f32[128,16]{0,1:T(8,128)} %param.12) | copy-start | bytes 24580
  23.9 46.6 %copy-start.4 = (s32[128]{0:T(128)S(1)}, s32[128]{0:T(128)}, u32[]{:S(2)}) copy-start(s32[128]{0:T(128)} %param.13) | copy-start | bytes 1540
  23.9 47.4 %copy-start.2 = (s32[128,16]{0,1:T(8,128)S(1)}, s32[128,16]{0,1:T(8,128)}, u32[]{:S(2)}) copy-start(s32[128,16]{0,1:T(8,128)} %param.11) | copy-start | bytes 24580
  23.9 47.6 %copy-start.1 = (f32[2,64,1,128]{3,2,1,0:T(1,128)S(1)}, f32[2,64,1,128]{3,2,1,0:T(1,128)}, u32[]{:S(2)}) copy-start(f32[2,64,1,128]{3,2,1,0:T(1,128)} %param.8) | copy-start | bytes 196612
  49.2 41.9 %all-to-all-start = ((f32[128,1,2048]{2,1,0:T(1,128)}), f32[128,1,2048]{2,1,0:T(1,128)S(1)}, u32[]{:S(2)}, u32[]{:S(2)}) async-start(f32[128,1,2048]{2,1,0:T(1,128)} %reshape.66), calls=%async_computation | async-start | bytes 2097152 | tf_op jit(solution)/shard_map/all_to_all | solution.py:51
  63.7 127.8 %all-reduce.2.cloned.1.call-start = ((), (), s32[]{:S(2)}) async-start(), calls=%async_computation.1 | async-start | bytes 1048576 | tf_op jit(solution)/shard_map/psum | solution.py:63
  63.8 127.7 %collective-permute-start = (f32[768,1024]{1,0:T(8,128)}, f32[768,1024]{1,0:T(8,128)}, u32[]{:S(2)}, u32[]{:S(2)}) collective-permute-start(f32[768,1024]{1,0:T(8,128)} %param.9), channel_id=1, source_target_pairs={{0,4},{4,8},{8,12},{12,16},{16,20},{20,24},{24,28},{28,32},{32,36}... | collective-permute-start | bytes 9437192 | tf_op jit(solution)/shard_map/ppermute | solution.py:17
  68.4 123.2 %collective-permute-start.1 = (f32[768,1024]{1,0:T(8,128)}, f32[768,1024]{1,0:T(8,128)}, u32[]{:S(2)}, u32[]{:S(2)}) collective-permute-start(f32[768,1024]{1,0:T(8,128)} %param.9), channel_id=1, source_target_pairs={{4,0},{8,4},{12,8},{16,12},{20,16},{24,20},{28,24},{32,28},{36,32}... | collective-permute-start | bytes 9437192 | tf_op jit(solution)/shard_map/ppermute | solution.py:19
  202.9 9.0 %copy-start.3 = (f32[768]{0:T(1024)S(1)}, f32[768]{0:T(1024)}, u32[]{:S(2)}) copy-start(f32[768]{0:T(1024)} %param.10) | copy-start | bytes 9220
  203.1 11.6 %collective-permute-start.2 = (f32[6,128,128]{2,1,0:T(8,128)S(1)}, f32[6,128,128]{2,1,0:T(8,128)S(1)}, u32[]{:S(2)}, u32[]{:S(2)}) collective-permute-start(f32[6,128,128]{2,1,0:T(8,128)S(1)} %get-tuple-element.5), channel_id=1, source_target_pairs={{508,0},{0,4},{4,8},{8,12},{12,16},{16,20},{20,24},{24,28},{28,32}... | collective-permute-start | bytes 1179656 | tf_op jit(solution)/shard_map/ppermute | solution.py:29
  210.0 12.4 %collective-permute-start.3 = (f32[6,128,128]{2,1,0:T(8,128)S(1)}, f32[6,128,128]{2,1,0:T(8,128)S(1)}, u32[]{:S(2)}, u32[]{:S(2)}) collective-permute-start(f32[6,128,128]{2,1,0:T(8,128)S(1)} %get-tuple-element.6), channel_id=1, source_target_pairs={{4,0},{8,4},{12,8},{16,12},{20,16},{24,20},{28,24},{32,28},{36,32}... | collective-permute-start | bytes 1179656 | tf_op jit(solution)/shard_map/ppermute | solution.py:29
Sparse Core Ops, SparseCore 0:
  142.0 49.4 all-reduce.1
where the time goes:
time: 233 us; the launch traced here: 230 us
  local copies, waits for them, and re-layouts  88.6 us (38%)
  waiting for transfers between devices  78.8 us (34%)
  starting transfers between devices  30.1 us (13%)
  between operations  13.6 us (6%)
  matrix products  13.3 us (6%)
  other arithmetic  5.99 us (3%)
    unnamed x13, local copies, waits for them, and re-layouts  69.3 us
    psum x1, waiting for transfers between devices, body(): summed = lax.psum(partial_sums, 'dom')  48.7 us
    all_to_all x1, waiting for transfers between devices, body(): lax.all_to_all(fcst_pert, 'mem', split_axis=3, concat_axis=1, tiled=True)  19.6 us
    all_to_all x2, local copies, waits for them, and re-layouts, body(): lax.all_to_all(fcst_pert, 'mem', split_axis=3, concat_axis=1, tiled=True)  18.1 us
    all_to_all x1, starting transfers between devices, body(): lax.all_to_all(fcst_pert, 'mem', split_axis=3, concat_axis=1, tiled=True)  14.6 us
    dot_general x1, matrix products, body(): products = jnp.dot(neighbour_rows, summed, precision=lax.Precision.HIGHEST)  11.3 us
    ppermute x2, waiting for transfers between devices, from_behind(): return lax.ppermute(block, axis, route)  10.5 us
    ppermute x2, starting transfers between devices, from_behind(): return lax.ppermute(block, axis, route)  8.8 us
  transfers between devices with their start and end apart: 6, of which 4 were waited for; matrix products, arithmetic and copies ran while one was open for 23% of the time, Pallas kernels for 0%

commit v1 on v0

v1 whole, which is shorter than its diff:
```python
import jax
import jax.numpy as jnp
from jax import lax
from jax.sharding import PartitionSpec as P

M = 1024
OBSB = 128
HIGHEST = lax.Precision.HIGHEST


def from_behind(block, axis, distance):
    devices = range(lax.axis_size(axis))
    route = [((i - distance) % len(devices), i) for i in devices]
    return lax.ppermute(block, axis, route)


def own_weights(obs_lists, block_taper, counts, column_index, region_index, owned_blocks, regions):
    column_count, slots = obs_lists.shape
    rows = (column_index + jnp.arange(3, dtype=jnp.int32) - 1) % column_count
    row_ids = obs_lists[rows]
    row_taper = block_taper[rows]
    row_count = counts[rows]
    slot_live = jnp.arange(slots, dtype=jnp.int32)[None, :] < row_count[:, None]
    own_ids = (column_index * regions + region_index) * owned_blocks + jnp.arange(
        owned_blocks, dtype=jnp.int32
    )
    matched = (row_ids[:, None, :] == own_ids[None, :, None]) & slot_live[:, None, :]
    return jnp.sum(
        jnp.where(matched, row_taper[:, None, :], jnp.zeros((), row_taper.dtype)), axis=2
    )


def body(fcst_pert, sensitivity, obs_pert, weighted_innovation, obs_lists, block_taper, counts):
    leads, local_members, _, columns = fcst_pert.shape
    column_blocks = lax.axis_size("mem")
    width = columns // column_blocks
    grid = fcst_pert.reshape(leads, local_members, column_blocks, width)
    grid = jnp.transpose(grid, (2, 0, 1, 3))
    regrouped = lax.all_to_all(grid, "mem", 0, 0, tiled=True)
    targets = sensitivity.shape[1]
    per_lead = []
    for lead in range(leads):
        left = regrouped[:, lead].reshape(-1, width)
        right = sensitivity[lead].reshape(targets, width)
        per_lead.append(
            lax.dot_general(left, right, (((1,), (1,)), ((), ())), precision=HIGHEST)
        )
    partial_sums = jnp.concatenate(per_lead, axis=1)
    summed = lax.psum(partial_sums, "dom")
    regions = lax.axis_size("dom")
    column_index = lax.axis_index("mem")
    region_index = lax.axis_index("dom")
    owned_rows = obs_pert.shape[0]
    owned_blocks = owned_rows // OBSB
    sources = (from_behind(summed, "mem", 1), summed, from_behind(summed, "mem", -1))
    weight_rows = own_weights(
        obs_lists, block_taper, counts, column_index, region_index, owned_blocks, regions
    )
    combined = sum(
        weight_rows[s][:, None, None] * sources[s][None] for s in range(len(sources))
    )
    rows = obs_pert.reshape(owned_blocks, OBSB, -1)
    result = jnp.einsum("irk,ikt->irt", rows, combined, precision=HIGHEST)
    result = result.reshape(owned_rows, -1)
    return result * (weighted_innovation / (M - 1))[:, None]


def solution(mesh):
    in_specs = (
        P(None, "mem", "dom", None),
        P(None, None, "dom", "mem"),
        P(("mem", "dom"), None),
        P(("mem", "dom")),
        P(),
        P(),
        P(),
    )
    out_specs = P(("mem", "dom"), None)
    return jax.shard_map(body, mesh=mesh, in_specs=in_specs, out_specs=out_specs, check_vma=False)
```

time: 233 us -> 142 us (0.61)
  the two profiles are of different devices: /device:TPU:249 before, /device:TPU:25 now
where the time goes in v1:
time: 142 us
  waiting for transfers between devices  79.5 us (56%)
  starting transfers between devices  26.9 us (19%)
  between operations  13.5 us (10%)
  local copies, waits for them, and re-layouts  11.1 us (8%)
  matrix products  9 us (6%)
  other arithmetic  1.99 us (1%)
    psum x1, waiting for transfers between devices, body(): summed = lax.psum(partial_sums, 'dom')  45.3 us
    all_to_all x1, waiting for transfers between devices, body(): regrouped = lax.all_to_all(grid, 'mem', 0, 0, tiled=True)  28.3 us
    all_to_all x1, starting transfers between devices, body(): regrouped = lax.all_to_all(grid, 'mem', 0, 0, tiled=True)  18 us
    ppermute x2, starting transfers between devices, from_behind(): return lax.ppermute(block, axis, route)  8.79 us
    ppermute x2, waiting for transfers between devices, from_behind(): return lax.ppermute(block, axis, route)  5.83 us
    dot_general x1, matrix products, body(): result = jnp.einsum('irk,ikt->irt', rows, combined, precision=HIGHEST)  5.53 us
    ppermute x2, local copies, waits for them, and re-layouts, from_behind(): return lax.ppermute(block, axis, route)  4.07 us
    dot_general x2, matrix products, body(): lax.dot_general(left, right, (((1,), (1,)), ((), ())), precision=HIGHEST)  3.48 us
  transfers between devices with their start and end apart: 4, of which 4 were waited for; matrix products, arithmetic and copies ran while one was open for 4% of the time, Pallas kernels for 0%

profile of v1, /device:TPU:25, one launch (start us, length us, event | category | flops | bytes accessed | tf_op | source)
XLA Modules:
  0.0 142.0 jit_solution(16191112976365428879)
XLA Ops:
  6.5 0.0 copy-start
  6.5 0.0 copy-start.3
  6.5 0.0 copy-start.4
  6.5 0.0 copy-start.2
  6.5 3.0 %copy.35 = f32[128,2,8,128]{3,2,1,0:T(8,128)} copy(f32[128,2,8,128]{3,0,2,1:T(8,128)} %bitcast.32) | data formatting | bytes 2097152 | tf_op jit(solution)/shard_map/transpose | solution.py:38
  9.6 0.0 copy-start.1
  9.6 0.0 copy-start.5
  9.6 18.0 %all-to-all-start = ((f32[128,2,8,128]{3,2,1,0:T(8,128)}), f32[128,2,8,128]{3,2,1,0:T(8,128)}, u32[]{:S(2)}, u32[]{:S(2)}) async-start(f32[128,2,8,128]{3,2,1,0:T(8,128)} %copy.35), calls=%async_computation | async-start | bytes 2097152 | tf_op jit(solution)/shard_map/all_to_all | solution.py:39
  27.6 0.0 all-reduce.2.cloned.1.call-start
  27.7 0.0 copy-done.3
  27.7 0.1 copy.33
  27.8 0.0 copy-done.4
  27.8 0.1 copy.34
  27.9 0.0 copy-done.2
  27.9 28.3 %all-to-all-done = f32[128,2,8,128]{3,2,1,0:T(8,128)} async-done(((f32[128,2,8,128]{3,2,1,0:T(8,128)}), f32[128,2,8,128]{3,2,1,0:T(8,128)}, u32[]{:S(2)}, u32[]{:S(2)}) %all-to-all-start) | async-done | bytes 1048608 | tf_op jit(solution)/shard_map/all_to_all | solution.py:39
  56.2 1.7 %fusion.12 = f32[1024,64]{0,1:T(8,128)S(1)} fusion(f32[64,128]{1,0:T(8,128)S(1)} %bitcast.34, f32[128,2,8,128]{3,2,1,0:T(8,128)} %all-to-all-done), kind=kOutput, calls=%fused_computation.16 | convolution fusion | flops 100663296 | bytes 819200 | tf_op jit(solution)/shard_map/dot_general | solution.py:46
  58.0 1.7 %fusion.13 = f32[1024,64]{0,1:T(8,128)S(1)} fusion(f32[64,128]{1,0:T(8,128)S(1)} %bitcast.33, f32[128,2,8,128]{3,2,1,0:T(8,128)} %all-to-all-done), kind=kOutput, calls=%fused_computation.18 | convolution fusion | flops 100663296 | bytes 819200 | tf_op jit(solution)/shard_map/dot_general | solution.py:46
  59.7 0.8 pad_maximum_fusion
  60.5 0.0 all-reduce.2.cloned.1.call-update
  60.6 0.6 gather_fusion
  61.1 0.6 gather_fusion.2
  61.7 0.0 copy-done.1
  61.7 0.6 gather_fusion.1
  62.3 0.1 iota_compare_fusion
  62.4 45.3 %all-reduce.2.cloned.1.call-done = f32[1024,128]{0,1:T(8,128)} async-done(((f32[1024,128]{0,1:T(8,128)}), f32[1024,128]{0,1:T(8,128)}) %all-reduce.2.cloned.1.call-update) | async-done | bytes 524304 | tf_op jit(solution)/shard_map/psum | solution.py:49
  107.7 6.9 %collective-permute-start = (f32[1024,128]{0,1:T(8,128)}, f32[1024,128]{0,1:T(8,128)}, u32[]{:S(2)}, u32[]{:S(2)}) collective-permute-start(f32[1024,128]{0,1:T(8,128)} %all-reduce.2.cloned.1.call-done), channel_id=1, source_target_pairs={{508,0},{0,4},{4,8},{8,12},{12,16},{16,20},{20,24},{24,28},{28,32}... | collective-permute-start | bytes 1572872 | tf_op jit(solution)/shard_map/ppermute | solution.py:14
  114.6 1.9 %collective-permute-start.1 = (f32[1024,128]{0,1:T(8,128)}, f32[1024,128]{0,1:T(8,128)}, u32[]{:S(2)}, u32[]{:S(2)}) collective-permute-start(f32[1024,128]{0,1:T(8,128)} %all-reduce.2.cloned.1.call-done), channel_id=1, source_target_pairs={{4,0},{8,4},{12,8},{16,12},{20,16},{24,20},{28,24},{32,28},{36,32}... | collective-permute-start | bytes 1572872 | tf_op jit(solution)/shard_map/ppermute | solution.py:14
  116.5 0.2 select_reduce_fusion
  116.7 0.0 copy-done.5
  116.7 2.1 %copy.39 = f32[1024,128]{1,0:T(8,128)} copy(f32[1024,128]{0,1:T(8,128)} %all-reduce.2.cloned.1.call-done) | data formatting | bytes 1048576 | tf_op jit(solution)/shard_map/psum | solution.py:49
  118.8 2.3 %collective-permute-done = f32[1024,128]{0,1:T(8,128)} collective-permute-done((f32[1024,128]{0,1:T(8,128)}, f32[1024,128]{0,1:T(8,128)}, u32[]{:S(2)}, u32[]{:S(2)}) %collective-permute-start) | collective-permute-done | bytes 524320 | tf_op jit(solution)/shard_map/ppermute | solution.py:14
  121.0 2.0 %copy.38 = f32[1024,128]{1,0:T(8,128)} copy(f32[1024,128]{0,1:T(8,128)} %collective-permute-done) | data formatting | bytes 1048576 | tf_op jit(solution)/shard_map/ppermute | solution.py:14
  123.1 3.6 %collective-permute-done.1 = f32[1024,128]{0,1:T(8,128)} collective-permute-done((f32[1024,128]{0,1:T(8,128)}, f32[1024,128]{0,1:T(8,128)}, u32[]{:S(2)}, u32[]{:S(2)}) %collective-permute-start.1) | collective-permute-done | bytes 524320 | tf_op jit(solution)/shard_map/ppermute | solution.py:14
  126.6 2.0 %copy.40 = f32[1024,128]{1,0:T(8,128)} copy(f32[1024,128]{0,1:T(8,128)} %collective-permute-done.1) | data formatting | bytes 1048576 | tf_op jit(solution)/shard_map/ppermute | solution.py:14
  128.7 0.0 copy-done
  128.7 5.5 %fusion = f32[6,128,128]{1,2,0:T(8,128)S(1)} fusion(f32[6,128,1024]{2,1,0:T(8,128)S(1)} %bitcast.31, f32[1024,128]{1,0:T(8,128)} %copy.40, f32[6]{0:T(128)S(1)} %get-tuple-element.8, f32[1024,128]{1,0:T(8,128)} %copy.39, f32[6]{0:T(128)S(1)} %get-tuple-element.9, f32[1024,128]{1,0:T(8,128)} %copy.38, f32[6]{0:T(128)S(1)} %get-tuple-element.7), kind=kOutput, calls=%fused_computation.3 | convolution fusion | flops 1211891712 | bytes 5111880 | tf_op jit(solution)/shard_map/irk,ikt->irt/dot_general | solution.py:63
  134.2 0.9 bitcast_multiply_fusion
  (6 shorter events, 0.0 us)
Async XLA Ops:
  6.5 122.1 %copy-start = (f32[768,1024]{1,0:T(8,128)S(1)}, f32[768,1024]{1,0:T(8,128)}, u32[]{:S(2)}) copy-start(f32[768,1024]{1,0:T(8,128)} %param.9) | copy-start | bytes 9437188
  6.5 21.1 %copy-start.3 = (s32[128,16]{0,1:T(8,128)S(1)}, s32[128,16]{0,1:T(8,128)}, u32[]{:S(2)}) copy-start(s32[128,16]{0,1:T(8,128)} %param.11) | copy-start | bytes 24580
  6.5 21.2 %copy-start.4 = (f32[128,16]{0,1:T(8,128)S(1)}, f32[128,16]{0,1:T(8,128)}, u32[]{:S(2)}) copy-start(f32[128,16]{0,1:T(8,128)} %param.12) | copy-start | bytes 24580
  6.5 21.3 %copy-start.2 = (f32[2,64,1,128]{3,2,1,0:T(1,128)S(1)}, f32[2,64,1,128]{3,2,1,0:T(1,128)}, u32[]{:S(2)}) copy-start(f32[2,64,1,128]{3,2,1,0:T(1,128)} %param.8) | copy-start | bytes 196612
  9.6 52.1 %copy-start.1 = (s32[128]{0:T(128)S(1)}, s32[128]{0:T(128)}, u32[]{:S(2)}) copy-start(s32[128]{0:T(128)} %param.13) | copy-start | bytes 1540
  9.6 107.2 %copy-start.5 = (f32[768]{0:T(1024)S(1)}, f32[768]{0:T(1024)}, u32[]{:S(2)}) copy-start(f32[768]{0:T(1024)} %param.10) | copy-start | bytes 9220
  9.6 46.7 %all-to-all-start = ((f32[128,2,8,128]{3,2,1,0:T(8,128)}), f32[128,2,8,128]{3,2,1,0:T(8,128)}, u32[]{:S(2)}, u32[]{:S(2)}) async-start(f32[128,2,8,128]{3,2,1,0:T(8,128)} %copy.35), calls=%async_computation | async-start | bytes 2097152 | tf_op jit(solution)/shard_map/all_to_all | solution.py:39
  27.6 80.1 %all-reduce.2.cloned.1.call-start = ((), (), s32[]{:S(2)}) async-start(), calls=%async_computation.1 | async-start | bytes 1048576 | tf_op jit(solution)/shard_map/psum | solution.py:49
  107.7 13.3 %collective-permute-start = (f32[1024,128]{0,1:T(8,128)}, f32[1024,128]{0,1:T(8,128)}, u32[]{:S(2)}, u32[]{:S(2)}) collective-permute-start(f32[1024,128]{0,1:T(8,128)} %all-reduce.2.cloned.1.call-done), channel_id=1, source_target_pairs={{508,0},{0,4},{4,8},{8,12},{12,16},{16,20},{20,24},{24,28},{28,32}... | collective-permute-start | bytes 1572872 | tf_op jit(solution)/shard_map/ppermute | solution.py:14
  114.6 12.0 %collective-permute-start.1 = (f32[1024,128]{0,1:T(8,128)}, f32[1024,128]{0,1:T(8,128)}, u32[]{:S(2)}, u32[]{:S(2)}) collective-permute-start(f32[1024,128]{0,1:T(8,128)} %all-reduce.2.cloned.1.call-done), channel_id=1, source_target_pairs={{4,0},{8,4},{12,8},{16,12},{20,16},{24,20},{28,24},{32,28},{36,32}... | collective-permute-start | bytes 1572872 | tf_op jit(solution)/shard_map/ppermute | solution.py:14
Sparse Core Ops, SparseCore 0:
  60.7 47.0 all-reduce.1

commit v2 on v1

--- a/solution.py
+++ b/solution.py
@@ -12,6 +12,14 @@
     devices = range(lax.axis_size(axis))
     route = [((i - distance) % len(devices), i) for i in devices]
     return lax.ppermute(block, axis, route)
+
+
+def gathered_sum(partial, axis):
+    count = lax.axis_size(axis)
+    pieces = partial.reshape(count, partial.shape[0] // count, partial.shape[1])
+    owned = lax.all_to_all(pieces, axis, 0, 0, tiled=True).sum(axis=0)
+    copies = jnp.broadcast_to(owned[None], (count,) + owned.shape)
+    return lax.all_to_all(copies, axis, 0, 0, tiled=True).reshape(partial.shape)
 
 
 def own_weights(obs_lists, block_taper, counts, column_index, region_index, owned_blocks, regions):
@@ -46,7 +54,7 @@
             lax.dot_general(left, right, (((1,), (1,)), ((), ())), precision=HIGHEST)
         )
     partial_sums = jnp.concatenate(per_lead, axis=1)
-    summed = lax.psum(partial_sums, "dom")
+    summed = gathered_sum(partial_sums, "dom")
     regions = lax.axis_size("dom")
     column_index = lax.axis_index("mem")
     region_index = lax.axis_index("dom")

time: 142 us -> 107 us (0.75)
  the two profiles are of different devices: /device:TPU:25 before, /device:TPU:2 now
where the time goes in v2:
time: 107 us
  waiting for transfers between devices  50.9 us (48%)
  starting transfers between devices  37.7 us (35%)
  matrix products  8.79 us (8%)
  local copies, waits for them, and re-layouts  6.73 us (6%)
  other arithmetic  2.3 us (2%)
    all_to_all x1, waiting for transfers between devices, body(): regrouped = lax.all_to_all(grid, 'mem', 0, 0, tiled=True)  29.8 us
    all_to_all x1, starting transfers between devices, body(): regrouped = lax.all_to_all(grid, 'mem', 0, 0, tiled=True)  18.5 us
    ppermute x2, starting transfers between devices, from_behind(): return lax.ppermute(block, axis, route)  8.87 us
    all_to_all x1, waiting for transfers between devices, gathered_sum(): owned = lax.all_to_all(pieces, axis, 0, 0, tiled=True).sum(axis=0)  8.38 us
    ppermute x2, waiting for transfers between devices, from_behind(): return lax.ppermute(block, axis, route)  6.82 us
    all_to_all x1, waiting for transfers between devices, gathered_sum(): return lax.all_to_all(copies, axis, 0, 0, tiled=True).reshape(partial.shape)  5.91 us
    all_to_all x1, starting transfers between devices, gathered_sum(): return lax.all_to_all(copies, axis, 0, 0, tiled=True).reshape(partial.shape)  5.55 us
    dot_general x1, matrix products, body(): result = jnp.einsum('irk,ikt->irt', rows, combined, precision=HIGHEST)  5.31 us
  transfers between devices with their start and end apart: 5, of which 5 were waited for; matrix products, arithmetic and copies ran while one was open for 2% of the time, Pallas kernels for 0%

profile of v2, /device:TPU:2, one launch (start us, length us, event | category | flops | bytes accessed | tf_op | source)
XLA Modules:
  0.0 106.6 jit_solution(5559720662889484537)
XLA Ops:
  0.0 0.0 copy-start
  0.0 0.0 copy-start.2
  0.0 3.0 %copy.26 = f32[128,2,8,128]{3,2,1,0:T(8,128)} copy(f32[128,2,8,128]{3,0,2,1:T(8,128)} %bitcast.39) | data formatting | bytes 2097152 | tf_op jit(solution)/shard_map/transpose | solution.py:46
  3.0 0.0 copy-start.3
  3.0 0.0 copy-start.4
  3.0 18.5 %all-to-all-start = ((f32[128,2,8,128]{3,2,1,0:T(8,128)}), f32[128,2,8,128]{3,2,1,0:T(8,128)}, u32[]{:S(2)}, u32[]{:S(2)}) async-start(f32[128,2,8,128]{3,2,1,0:T(8,128)} %copy.26), calls=%async_computation | async-start | bytes 2097152 | tf_op jit(solution)/shard_map/all_to_all | solution.py:47
  21.5 0.0 copy-done.2
  21.5 29.8 %all-to-all-done = f32[128,2,8,128]{3,2,1,0:T(8,128)} async-done(((f32[128,2,8,128]{3,2,1,0:T(8,128)}), f32[128,2,8,128]{3,2,1,0:T(8,128)}, u32[]{:S(2)}, u32[]{:S(2)}) %all-to-all-start) | async-done | bytes 1048608 | tf_op jit(solution)/shard_map/all_to_all | solution.py:47
  51.4 1.7 %fusion.12 = f32[1024,64]{0,1:T(8,128)S(1)} fusion(f32[64,128]{1,0:T(8,128)S(1)} %bitcast.41, f32[128,2,8,128]{3,2,1,0:T(8,128)} %all-to-all-done), kind=kOutput, calls=%fused_computation.17 | convolution fusion | flops 100663296 | bytes 819200 | tf_op jit(solution)/shard_map/dot_general | solution.py:54
  53.1 1.7 %fusion.13 = f32[1024,64]{0,1:T(8,128)S(1)} fusion(f32[64,128]{1,0:T(8,128)S(1)} %bitcast.40, f32[128,2,8,128]{3,2,1,0:T(8,128)} %all-to-all-done), kind=kOutput, calls=%fused_computation.19 | convolution fusion | flops 100663296 | bytes 819200 | tf_op jit(solution)/shard_map/dot_general | solution.py:54
  54.8 0.0 copy-start.1
  54.8 0.0 copy-start.5
  54.9 0.8 copy.37
  55.7 4.8 %all-to-all-start.1 = ((f32[4,256,128]{1,2,0:T(8,128)}), f32[4,256,128]{1,2,0:T(8,128)}, u32[]{:S(2)}, u32[]{:S(2)}) async-start(f32[4,256,128]{1,2,0:T(8,128)} %bitcast.37), calls=%async_computation.1 | async-start | bytes 1048576 | tf_op jit(solution)/shard_map/all_to_all | solution.py:20
  60.6 0.0 copy-done.3
  60.6 0.1 copy.24
  60.7 0.0 copy-done.4
  60.7 0.1 copy.25
  60.8 8.4 %all-to-all-done.1 = f32[4,256,128]{1,2,0:T(8,128)} async-done(((f32[4,256,128]{1,2,0:T(8,128)}), f32[4,256,128]{1,2,0:T(8,128)}, u32[]{:S(2)}, u32[]{:S(2)}) %all-to-all-start.1) | async-done | bytes 524320 | tf_op jit(solution)/shard_map/all_to_all | solution.py:20
  69.2 1.1 %reduce_sum.19 = f32[256,128]{0,1:T(8,128)S(1)} reduce(f32[4,256,128]{1,2,0:T(8,128)} %all-to-all-done.1, f32[]{:T(128)} %constant.36.clone.1), dimensions={0}, to_apply=%region_1.2 | reduce | flops 98304 | bytes 655364 | tf_op jit(solution)/shard_map/reduce_sum | solution.py:20
  70.3 0.1 copy.31
  70.3 0.8 broadcast_in_dim.12
  71.2 5.5 %all-to-all-start.2 = ((f32[4,256,128]{2,1,0:T(8,128)}), f32[4,256,128]{2,1,0:T(8,128)}, u32[]{:S(2)}, u32[]{:S(2)}) async-start(f32[4,256,128]{2,1,0:T(8,128)} %broadcast_in_dim.12), calls=%async_computation.2 | async-start | bytes 1048576 | tf_op jit(solution)/shard_map/all_to_all | solution.py:22
  76.7 0.6 gather_fusion
  77.3 0.6 gather_fusion.2
  77.8 0.0 copy-done.1
  77.8 0.6 gather_fusion.1
  78.5 0.1 iota_compare_fusion
  78.6 5.9 %all-to-all-done.2 = f32[4,256,128]{2,1,0:T(8,128)} async-done(((f32[4,256,128]{2,1,0:T(8,128)}), f32[4,256,128]{2,1,0:T(8,128)}, u32[]{:S(2)}, u32[]{:S(2)}) %all-to-all-start.2) | async-done | bytes 524320 | tf_op jit(solution)/shard_map/all_to_all | solution.py:22
  84.5 1.9 %collective-permute-start = (f32[1024,128]{1,0:T(8,128)}, f32[1024,128]{1,0:T(8,128)S(1)}, u32[]{:S(2)}, u32[]{:S(2)}) collective-permute-start(f32[1024,128]{1,0:T(8,128)} %bitcast.8), channel_id=1, source_target_pairs={{508,0},{0,4},{4,8},{8,12},{12,16},{16,20},{20,24},{24,28},{28,32}... | collective-permute-start | bytes 1572872 | tf_op jit(solution)/shard_map/ppermute | solution.py:14
  86.4 7.0 %collective-permute-start.1 = (f32[1024,128]{1,0:T(8,128)}, f32[1024,128]{1,0:T(8,128)S(1)}, u32[]{:S(2)}, u32[]{:S(2)}) collective-permute-start(f32[1024,128]{1,0:T(8,128)} %bitcast.8), channel_id=1, source_target_pairs={{4,0},{8,4},{12,8},{16,12},{20,16},{24,20},{28,24},{32,28},{36,32}... | collective-permute-start | bytes 1572872 | tf_op jit(solution)/shard_map/ppermute | solution.py:14
  93.4 0.2 select_reduce_fusion
  93.5 0.0 copy-done.5
  93.5 5.0 %collective-permute-done = f32[1024,128]{1,0:T(8,128)S(1)} collective-permute-done((f32[1024,128]{1,0:T(8,128)}, f32[1024,128]{1,0:T(8,128)S(1)}, u32[]{:S(2)}, u32[]{:S(2)}) %collective-permute-start) | collective-permute-done | bytes 524320 | tf_op jit(solution)/shard_map/ppermute | solution.py:14
  98.5 1.9 %collective-permute-done.1 = f32[1024,128]{1,0:T(8,128)S(1)} collective-permute-done((f32[1024,128]{1,0:T(8,128)}, f32[1024,128]{1,0:T(8,128)S(1)}, u32[]{:S(2)}, u32[]{:S(2)}) %collective-permute-start.1) | collective-permute-done | bytes 524320 | tf_op jit(solution)/shard_map/ppermute | solution.py:14
  100.4 0.0 copy-done
  100.4 5.3 %fusion = f32[6,128,128]{1,2,0:T(8,128)S(1)} fusion(f32[6,128,1024]{2,1,0:T(8,128)S(1)} %bitcast.36, f32[1024,128]{1,0:T(8,128)S(1)} %collective-permute-done.1, f32[6]{0:T(128)S(1)} %get-tuple-element.8, f32[1024,128]{1,0:T(8,128)} %bitcast.8, f32[6]{0:T(128)S(1)} %get-tuple-element.9, f32[1024,128]{1,0:T(8,128)S(1)} %collective-permute-done, ...), kind=kOutput, calls=%fused_computation.3 | convolution fusion | flops 1211891712 | bytes 5111880 | tf_op jit(solution)/shard_map/irk,ikt->irt/dot_general | solution.py:71
  105.7 0.9 bitcast_multiply_fusion
  (7 shorter events, 0.1 us)
Async XLA Ops:
  0.0 100.4 %copy-start = (f32[768,1024]{1,0:T(8,128)S(1)}, f32[768,1024]{1,0:T(8,128)}, u32[]{:S(2)}) copy-start(f32[768,1024]{1,0:T(8,128)} %param.9) | copy-start | bytes 9437188
  0.0 21.5 %copy-start.2 = (f32[2,64,1,128]{3,2,1,0:T(1,128)S(1)}, f32[2,64,1,128]{3,2,1,0:T(1,128)}, u32[]{:S(2)}) copy-start(f32[2,64,1,128]{3,2,1,0:T(1,128)} %param.8) | copy-start | bytes 196612
  3.0 57.5 %copy-start.3 = (s32[128,16]{0,1:T(8,128)S(1)}, s32[128,16]{0,1:T(8,128)}, u32[]{:S(2)}) copy-start(s32[128,16]{0,1:T(8,128)} %param.11) | copy-start | bytes 24580
  3.0 57.6 %copy-start.4 = (f32[128,16]{0,1:T(8,128)S(1)}, f32[128,16]{0,1:T(8,128)}, u32[]{:S(2)}) copy-start(f32[128,16]{0,1:T(8,128)} %param.12) | copy-start | bytes 24580
  3.0 48.3 %all-to-all-start = ((f32[128,2,8,128]{3,2,1,0:T(8,128)}), f32[128,2,8,128]{3,2,1,0:T(8,128)}, u32[]{:S(2)}, u32[]{:S(2)}) async-start(f32[128,2,8,128]{3,2,1,0:T(8,128)} %copy.26), calls=%async_computation | async-start | bytes 2097152 | tf_op jit(solution)/shard_map/all_to_all | solution.py:47
  54.8 23.0 %copy-start.1 = (s32[128]{0:T(128)S(1)}, s32[128]{0:T(128)}, u32[]{:S(2)}) copy-start(s32[128]{0:T(128)} %param.13) | copy-start | bytes 1540
  54.8 38.7 %copy-start.5 = (f32[768]{0:T(1024)S(1)}, f32[768]{0:T(1024)}, u32[]{:S(2)}) copy-start(f32[768]{0:T(1024)} %param.10) | copy-start | bytes 9220
  55.7 13.4 %all-to-all-start.1 = ((f32[4,256,128]{1,2,0:T(8,128)}), f32[4,256,128]{1,2,0:T(8,128)}, u32[]{:S(2)}, u32[]{:S(2)}) async-start(f32[4,256,128]{1,2,0:T(8,128)} %bitcast.37), calls=%async_computation.1 | async-start | bytes 1048576 | tf_op jit(solution)/shard_map/all_to_all | solution.py:20
  71.2 13.3 %all-to-all-start.2 = ((f32[4,256,128]{2,1,0:T(8,128)}), f32[4,256,128]{2,1,0:T(8,128)}, u32[]{:S(2)}, u32[]{:S(2)}) async-start(f32[4,256,128]{2,1,0:T(8,128)} %broadcast_in_dim.12), calls=%async_computation.2 | async-start | bytes 1048576 | tf_op jit(solution)/shard_map/all_to_all | solution.py:22
  84.5 14.0 %collective-permute-start = (f32[1024,128]{1,0:T(8,128)}, f32[1024,128]{1,0:T(8,128)S(1)}, u32[]{:S(2)}, u32[]{:S(2)}) collective-permute-start(f32[1024,128]{1,0:T(8,128)} %bitcast.8), channel_id=1, source_target_pairs={{508,0},{0,4},{4,8},{8,12},{12,16},{16,20},{20,24},{24,28},{28,32}... | collective-permute-start | bytes 1572872 | tf_op jit(solution)/shard_map/ppermute | solution.py:14
  86.4 14.0 %collective-permute-start.1 = (f32[1024,128]{1,0:T(8,128)}, f32[1024,128]{1,0:T(8,128)S(1)}, u32[]{:S(2)}, u32[]{:S(2)}) collective-permute-start(f32[1024,128]{1,0:T(8,128)} %bitcast.8), channel_id=1, source_target_pairs={{4,0},{8,4},{12,8},{16,12},{20,16},{24,20},{28,24},{32,28},{36,32}... | collective-permute-start | bytes 1572872 | tf_op jit(solution)/shard_map/ppermute | solution.py:14

commit v3 on v2

--- a/solution.py
+++ b/solution.py
@@ -5,7 +5,7 @@
 
 M = 1024
 OBSB = 128
-HIGHEST = lax.Precision.HIGHEST
+HIGH = lax.Precision.HIGH
 
 
 def from_behind(block, axis, distance):
@@ -51,7 +51,7 @@
         left = regrouped[:, lead].reshape(-1, width)
         right = sensitivity[lead].reshape(targets, width)
         per_lead.append(
-            lax.dot_general(left, right, (((1,), (1,)), ((), ())), precision=HIGHEST)
+            lax.dot_general(left, right, (((1,), (1,)), ((), ())), precision=HIGH)
         )
     partial_sums = jnp.concatenate(per_lead, axis=1)
     summed = gathered_sum(partial_sums, "dom")
@@ -68,7 +68,7 @@
         weight_rows[s][:, None, None] * sources[s][None] for s in range(len(sources))
     )
     rows = obs_pert.reshape(owned_blocks, OBSB, -1)
-    result = jnp.einsum("irk,ikt->irt", rows, combined, precision=HIGHEST)
+    result = jnp.einsum("irk,ikt->irt", rows, combined, precision=HIGH)
     result = result.reshape(owned_rows, -1)
     return result * (weighted_innovation / (M - 1))[:, None]
 

time: 107 us -> 105 us (0.981)
  matrix products: 8.79 us -> 6.35 us
    dot_general x3, matrix products: 8.79 us -> 6.35 us  [the longest x1 3.46 us: body(): result = jnp.einsum('irk,ikt->irt', rows, combined, precision=HIGH)]
where the time goes in v3:
time: 105 us; the launch traced here: 104 us
  waiting for transfers between devices  50.9 us (48%)
  starting transfers between devices  37.7 us (36%)
  local copies, waits for them, and re-layouts  6.73 us (6%)
  matrix products  6.35 us (6%)
  other arithmetic  2.3 us (2%)
    all_to_all x1, waiting for transfers between devices, body(): regrouped = lax.all_to_all(grid, 'mem', 0, 0, tiled=True)  29.8 us
    all_to_all x1, starting transfers between devices, body(): regrouped = lax.all_to_all(grid, 'mem', 0, 0, tiled=True)  18.5 us
    ppermute x2, starting transfers between devices, from_behind(): return lax.ppermute(block, axis, route)  8.87 us
    all_to_all x1, waiting for transfers between devices, gathered_sum(): owned = lax.all_to_all(pieces, axis, 0, 0, tiled=True).sum(axis=0)  8.38 us
    ppermute x2, waiting for transfers between devices, from_behind(): return lax.ppermute(block, axis, route)  6.82 us
    all_to_all x1, waiting for transfers between devices, gathered_sum(): return lax.all_to_all(copies, axis, 0, 0, tiled=True).reshape(partial.shape)  5.91 us
    all_to_all x1, starting transfers between devices, gathered_sum(): return lax.all_to_all(copies, axis, 0, 0, tiled=True).reshape(partial.shape)  5.55 us
    all_to_all x1, starting transfers between devices, gathered_sum(): owned = lax.all_to_all(pieces, axis, 0, 0, tiled=True).sum(axis=0)  4.82 us
  transfers between devices with their start and end apart: 5, of which 5 were waited for; matrix products, arithmetic and copies ran while one was open for 2% of the time, Pallas kernels for 0%

profile of v3, /device:TPU:2, one launch (start us, length us, event | category | flops | bytes accessed | tf_op | source)
XLA Modules:
  0.0 104.2 jit_solution(11850899503699324993)
XLA Ops:
  0.0 0.0 copy-start
  0.0 0.0 copy-start.2
  0.0 3.0 %copy.26 = f32[128,2,8,128]{3,2,1,0:T(8,128)} copy(f32[128,2,8,128]{3,0,2,1:T(8,128)} %bitcast.39) | data formatting | bytes 2097152 | tf_op jit(solution)/shard_map/transpose | solution.py:46
  3.0 0.0 copy-start.3
  3.0 0.0 copy-start.4
  3.0 18.5 %all-to-all-start = ((f32[128,2,8,128]{3,2,1,0:T(8,128)}), f32[128,2,8,128]{3,2,1,0:T(8,128)}, u32[]{:S(2)}, u32[]{:S(2)}) async-start(f32[128,2,8,128]{3,2,1,0:T(8,128)} %copy.26), calls=%async_computation | async-start | bytes 2097152 | tf_op jit(solution)/shard_map/all_to_all | solution.py:47
  21.5 0.0 copy-done.2
  21.5 29.8 %all-to-all-done = f32[128,2,8,128]{3,2,1,0:T(8,128)} async-done(((f32[128,2,8,128]{3,2,1,0:T(8,128)}), f32[128,2,8,128]{3,2,1,0:T(8,128)}, u32[]{:S(2)}, u32[]{:S(2)}) %all-to-all-start) | async-done | bytes 1048608 | tf_op jit(solution)/shard_map/all_to_all | solution.py:47
  51.4 1.4 %fusion.12 = f32[1024,64]{0,1:T(8,128)S(1)} fusion(f32[64,128]{1,0:T(8,128)S(1)} %bitcast.41, f32[128,2,8,128]{3,2,1,0:T(8,128)} %all-to-all-done), kind=kOutput, calls=%fused_computation.17 | convolution fusion | flops 50331648 | bytes 819200 | tf_op jit(solution)/shard_map/dot_general | solution.py:54
  52.8 1.4 %fusion.13 = f32[1024,64]{0,1:T(8,128)S(1)} fusion(f32[64,128]{1,0:T(8,128)S(1)} %bitcast.40, f32[128,2,8,128]{3,2,1,0:T(8,128)} %all-to-all-done), kind=kOutput, calls=%fused_computation.19 | convolution fusion | flops 50331648 | bytes 819200 | tf_op jit(solution)/shard_map/dot_general | solution.py:54
  54.3 0.0 copy-start.1
  54.3 0.0 copy-start.5
  54.3 0.8 copy.37
  55.1 4.8 %all-to-all-start.1 = ((f32[4,256,128]{1,2,0:T(8,128)}), f32[4,256,128]{1,2,0:T(8,128)}, u32[]{:S(2)}, u32[]{:S(2)}) async-start(f32[4,256,128]{1,2,0:T(8,128)} %bitcast.37), calls=%async_computation.1 | async-start | bytes 1048576 | tf_op jit(solution)/shard_map/all_to_all | solution.py:20
  60.0 0.0 copy-done.3
  60.0 0.1 copy.24
  60.1 0.0 copy-done.4
  60.1 0.1 copy.25
  60.2 8.4 %all-to-all-done.1 = f32[4,256,128]{1,2,0:T(8,128)} async-done(((f32[4,256,128]{1,2,0:T(8,128)}), f32[4,256,128]{1,2,0:T(8,128)}, u32[]{:S(2)}, u32[]{:S(2)}) %all-to-all-start.1) | async-done | bytes 524320 | tf_op jit(solution)/shard_map/all_to_all | solution.py:20
  68.6 1.1 %reduce_sum.19 = f32[256,128]{0,1:T(8,128)S(1)} reduce(f32[4,256,128]{1,2,0:T(8,128)} %all-to-all-done.1, f32[]{:T(128)} %constant.36.clone.1), dimensions={0}, to_apply=%region_1.2 | reduce | flops 98304 | bytes 655364 | tf_op jit(solution)/shard_map/reduce_sum | solution.py:20
  69.7 0.1 copy.31
  69.8 0.8 broadcast_in_dim.12
  70.6 5.5 %all-to-all-start.2 = ((f32[4,256,128]{2,1,0:T(8,128)}), f32[4,256,128]{2,1,0:T(8,128)}, u32[]{:S(2)}, u32[]{:S(2)}) async-start(f32[4,256,128]{2,1,0:T(8,128)} %broadcast_in_dim.12), calls=%async_computation.2 | async-start | bytes 1048576 | tf_op jit(solution)/shard_map/all_to_all | solution.py:22
  76.1 0.6 gather_fusion
  76.7 0.6 gather_fusion.2
  77.3 0.0 copy-done.1
  77.3 0.6 gather_fusion.1
  77.9 0.1 iota_compare_fusion
  78.0 5.9 %all-to-all-done.2 = f32[4,256,128]{2,1,0:T(8,128)} async-done(((f32[4,256,128]{2,1,0:T(8,128)}), f32[4,256,128]{2,1,0:T(8,128)}, u32[]{:S(2)}, u32[]{:S(2)}) %all-to-all-start.2) | async-done | bytes 524320 | tf_op jit(solution)/shard_map/all_to_all | solution.py:22
  83.9 1.9 %collective-permute-start = (f32[1024,128]{1,0:T(8,128)}, f32[1024,128]{1,0:T(8,128)S(1)}, u32[]{:S(2)}, u32[]{:S(2)}) collective-permute-start(f32[1024,128]{1,0:T(8,128)} %bitcast.8), channel_id=1, source_target_pairs={{508,0},{0,4},{4,8},{8,12},{12,16},{16,20},{20,24},{24,28},{28,32}... | collective-permute-start | bytes 1572872 | tf_op jit(solution)/shard_map/ppermute | solution.py:14
  85.8 7.0 %collective-permute-start.1 = (f32[1024,128]{1,0:T(8,128)}, f32[1024,128]{1,0:T(8,128)S(1)}, u32[]{:S(2)}, u32[]{:S(2)}) collective-permute-start(f32[1024,128]{1,0:T(8,128)} %bitcast.8), channel_id=1, source_target_pairs={{4,0},{8,4},{12,8},{16,12},{20,16},{24,20},{28,24},{32,28},{36,32}... | collective-permute-start | bytes 1572872 | tf_op jit(solution)/shard_map/ppermute | solution.py:14
  92.8 0.2 select_reduce_fusion
  92.9 0.0 copy-done.5
  93.0 5.0 %collective-permute-done = f32[1024,128]{1,0:T(8,128)S(1)} collective-permute-done((f32[1024,128]{1,0:T(8,128)}, f32[1024,128]{1,0:T(8,128)S(1)}, u32[]{:S(2)}, u32[]{:S(2)}) %collective-permute-start) | collective-permute-done | bytes 524320 | tf_op jit(solution)/shard_map/ppermute | solution.py:14
  97.9 1.9 %collective-permute-done.1 = f32[1024,128]{1,0:T(8,128)S(1)} collective-permute-done((f32[1024,128]{1,0:T(8,128)}, f32[1024,128]{1,0:T(8,128)S(1)}, u32[]{:S(2)}, u32[]{:S(2)}) %collective-permute-start.1) | collective-permute-done | bytes 524320 | tf_op jit(solution)/shard_map/ppermute | solution.py:14
  99.8 0.0 copy-done
  99.8 3.5 %fusion = f32[6,128,128]{1,2,0:T(8,128)S(1)} fusion(f32[6,128,1024]{2,1,0:T(8,128)S(1)} %bitcast.36, f32[1024,128]{1,0:T(8,128)S(1)} %collective-permute-done.1, f32[6]{0:T(128)S(1)} %get-tuple-element.8, f32[1024,128]{1,0:T(8,128)} %bitcast.8, f32[6]{0:T(128)S(1)} %get-tuple-element.9, f32[1024,128]{1,0:T(8,128)S(1)} %collective-permute-done, ...), kind=kOutput, calls=%fused_computation.3 | convolution fusion | flops 607911936 | bytes 5111880 | tf_op jit(solution)/shard_map/irk,ikt->irt/dot_general | solution.py:71
  103.2 0.9 bitcast_multiply_fusion
  (7 shorter events, 0.1 us)
Async XLA Ops:
  0.0 99.8 %copy-start = (f32[768,1024]{1,0:T(8,128)S(1)}, f32[768,1024]{1,0:T(8,128)}, u32[]{:S(2)}) copy-start(f32[768,1024]{1,0:T(8,128)} %param.9) | copy-start | bytes 9437188
  0.0 21.5 %copy-start.2 = (f32[2,64,1,128]{3,2,1,0:T(1,128)S(1)}, f32[2,64,1,128]{3,2,1,0:T(1,128)}, u32[]{:S(2)}) copy-start(f32[2,64,1,128]{3,2,1,0:T(1,128)} %param.8) | copy-start | bytes 196612
  3.0 57.0 %copy-start.3 = (s32[128,16]{0,1:T(8,128)S(1)}, s32[128,16]{0,1:T(8,128)}, u32[]{:S(2)}) copy-start(s32[128,16]{0,1:T(8,128)} %param.11) | copy-start | bytes 24580
  3.0 57.1 %copy-start.4 = (f32[128,16]{0,1:T(8,128)S(1)}, f32[128,16]{0,1:T(8,128)}, u32[]{:S(2)}) copy-start(f32[128,16]{0,1:T(8,128)} %param.12) | copy-start | bytes 24580
  3.0 48.3 %all-to-all-start = ((f32[128,2,8,128]{3,2,1,0:T(8,128)}), f32[128,2,8,128]{3,2,1,0:T(8,128)}, u32[]{:S(2)}, u32[]{:S(2)}) async-start(f32[128,2,8,128]{3,2,1,0:T(8,128)} %copy.26), calls=%async_computation | async-start | bytes 2097152 | tf_op jit(solution)/shard_map/all_to_all | solution.py:47
  54.3 23.0 %copy-start.1 = (s32[128]{0:T(128)S(1)}, s32[128]{0:T(128)}, u32[]{:S(2)}) copy-start(s32[128]{0:T(128)} %param.13) | copy-start | bytes 1540
  54.3 38.7 %copy-start.5 = (f32[768]{0:T(1024)S(1)}, f32[768]{0:T(1024)}, u32[]{:S(2)}) copy-start(f32[768]{0:T(1024)} %param.10) | copy-start | bytes 9220
  55.1 13.4 %all-to-all-start.1 = ((f32[4,256,128]{1,2,0:T(8,128)}), f32[4,256,128]{1,2,0:T(8,128)}, u32[]{:S(2)}, u32[]{:S(2)}) async-start(f32[4,256,128]{1,2,0:T(8,128)} %bitcast.37), calls=%async_computation.1 | async-start | bytes 1048576 | tf_op jit(solution)/shard_map/all_to_all | solution.py:20
  70.6 13.3 %all-to-all-start.2 = ((f32[4,256,128]{2,1,0:T(8,128)}), f32[4,256,128]{2,1,0:T(8,128)}, u32[]{:S(2)}, u32[]{:S(2)}) async-start(f32[4,256,128]{2,1,0:T(8,128)} %broadcast_in_dim.12), calls=%async_computation.2 | async-start | bytes 1048576 | tf_op jit(solution)/shard_map/all_to_all | solution.py:22
  83.9 14.0 %collective-permute-start = (f32[1024,128]{1,0:T(8,128)}, f32[1024,128]{1,0:T(8,128)S(1)}, u32[]{:S(2)}, u32[]{:S(2)}) collective-permute-start(f32[1024,128]{1,0:T(8,128)} %bitcast.8), channel_id=1, source_target_pairs={{508,0},{0,4},{4,8},{8,12},{12,16},{16,20},{20,24},{24,28},{28,32}... | collective-permute-start | bytes 1572872 | tf_op jit(solution)/shard_map/ppermute | solution.py:14
  85.8 14.0 %collective-permute-start.1 = (f32[1024,128]{1,0:T(8,128)}, f32[1024,128]{1,0:T(8,128)S(1)}, u32[]{:S(2)}, u32[]{:S(2)}) collective-permute-start(f32[1024,128]{1,0:T(8,128)} %bitcast.8), channel_id=1, source_target_pairs={{4,0},{8,4},{12,8},{16,12},{20,16},{24,20},{28,24},{32,28},{36,32}... | collective-permute-start | bytes 1572872 | tf_op jit(solution)/shard_map/ppermute | solution.py:14

commit v4 on v3

--- a/solution.py
+++ b/solution.py
@@ -14,12 +14,10 @@
     return lax.ppermute(block, axis, route)
 
 
-def gathered_sum(partial, axis):
+def gathered(piece, axis):
     count = lax.axis_size(axis)
-    pieces = partial.reshape(count, partial.shape[0] // count, partial.shape[1])
-    owned = lax.all_to_all(pieces, axis, 0, 0, tiled=True).sum(axis=0)
-    copies = jnp.broadcast_to(owned[None], (count,) + owned.shape)
-    return lax.all_to_all(copies, axis, 0, 0, tiled=True).reshape(partial.shape)
+    copies = jnp.broadcast_to(piece[None], (count,) + piece.shape)
+    return lax.all_to_all(copies, axis, 0, 0, tiled=True)
 
 
 def own_weights(obs_lists, block_taper, counts, column_index, region_index, owned_blocks, regions):
@@ -41,21 +39,19 @@
 def body(fcst_pert, sensitivity, obs_pert, weighted_innovation, obs_lists, block_taper, counts):
     leads, local_members, _, columns = fcst_pert.shape
     column_blocks = lax.axis_size("mem")
+    regions = lax.axis_size("dom")
     width = columns // column_blocks
-    grid = fcst_pert.reshape(leads, local_members, column_blocks, width)
-    grid = jnp.transpose(grid, (2, 0, 1, 3))
-    regrouped = lax.all_to_all(grid, "mem", 0, 0, tiled=True)
+    pair = local_members // regions
+    grid = fcst_pert.reshape(leads, regions, pair, column_blocks, width)
+    grid = jnp.transpose(grid, (3, 1, 0, 2, 4)).reshape(column_blocks * regions, -1)
+    arrived = lax.all_to_all(grid, ("mem", "dom"), 0, 0, tiled=True)
+    arrived = arrived.reshape(column_blocks, regions, leads, pair, width)
     targets = sensitivity.shape[1]
-    per_lead = []
-    for lead in range(leads):
-        left = regrouped[:, lead].reshape(-1, width)
-        right = sensitivity[lead].reshape(targets, width)
-        per_lead.append(
-            lax.dot_general(left, right, (((1,), (1,)), ((), ())), precision=HIGH)
-        )
-    partial_sums = jnp.concatenate(per_lead, axis=1)
-    summed = gathered_sum(partial_sums, "dom")
-    regions = lax.axis_size("dom")
+    levels = gathered(sensitivity[:, :, 0, :], "dom")
+    quarter = jnp.einsum("mdljc,dltc->mjlt", arrived, levels, precision=HIGH)
+    quarter = quarter.reshape(column_blocks * pair, leads * targets)
+    full = gathered(quarter, "dom").reshape(regions, column_blocks, pair, -1)
+    summed = jnp.transpose(full, (1, 0, 2, 3)).reshape(column_blocks * local_members, -1)
     column_index = lax.axis_index("mem")
     region_index = lax.axis_index("dom")
     owned_rows = obs_pert.shape[0]

time: 105 us -> 102 us (0.971)
  local copies, waits for them, and re-layouts: 6.73 us -> 12.1 us
  waiting for transfers between devices: 50.9 us -> 46 us
  matrix products: 6.35 us -> 4.44 us
  other arithmetic: 2.3 us -> 1.17 us
    all_to_all x3, waiting for transfers between devices: 44.1 us -> 34.7 us  [the longest x1 27.5 us: body(): arrived = lax.all_to_all(grid, ('mem', 'dom'), 0, 0, tiled=True)]
    ppermute x2, starting transfers between devices: 8.87 us -> 4.33 us  [from_behind(): return lax.ppermute(block, axis, route)]
    ppermute x2, waiting for transfers between devices: 6.82 us -> 11.2 us  [from_behind(): return lax.ppermute(block, axis, route)]
    all_to_all x3, starting transfers between devices: 28.8 us -> 33.2 us  [the longest x1 17.9 us: body(): arrived = lax.all_to_all(grid, ('mem', 'dom'), 0, 0, tiled=True)]
    reshape x1, local copies, waits for them, and re-layouts: 0.82 us -> 3.03 us  [body(): grid = fcst_pert.reshape(leads, regions, pair, column_blocks, width)]
    broadcast_in_dim x1 -> x3, local copies, waits for them, and re-layouts: 0.82 us -> 2.71 us  [gathered(): copies = jnp.broadcast_to(piece[None], (count,) + piece.shape)]
    transpose x1 -> x2, local copies, waits for them, and re-layouts: 3.01 us -> 1.42 us  [the longest x1 1.22 us: body(): jnp.transpose(full, (1, 0, 2, 3)).reshape(column_blocks * local_members, -1)]
    unnamed x14 -> x12, local copies, waits for them, and re-layouts: 0.22 us -> 1.47 us
  transfers between devices with their start and end apart: 5 -> 5, of which waited for: 5 -> 5; matrix products, arithmetic and copies ran while one was open for 2% -> 8% of each run, Pallas kernels for 0% -> 0%
where the time goes in v4:
time: 102 us; the launch traced here: 101 us
  waiting for transfers between devices  46 us (45%)
  starting transfers between devices  37.5 us (37%)
  local copies, waits for them, and re-layouts  12.1 us (12%)
  matrix products  4.44 us (4%)
  other arithmetic  1.17 us (1%)
    all_to_all x1, waiting for transfers between devices, body(): arrived = lax.all_to_all(grid, ('mem', 'dom'), 0, 0, tiled=True)  27.5 us
    all_to_all x1, starting transfers between devices, body(): arrived = lax.all_to_all(grid, ('mem', 'dom'), 0, 0, tiled=True)  17.9 us
    all_to_all x2, starting transfers between devices, gathered(): return lax.all_to_all(copies, axis, 0, 0, tiled=True)  15.3 us
    ppermute x2, waiting for transfers between devices, from_behind(): return lax.ppermute(block, axis, route)  11.2 us
    all_to_all x2, waiting for transfers between devices, gathered(): return lax.all_to_all(copies, axis, 0, 0, tiled=True)  7.27 us
    ppermute x2, starting transfers between devices, from_behind(): return lax.ppermute(block, axis, route)  4.33 us
    reshape x1, local copies, waits for them, and re-layouts, body(): grid = fcst_pert.reshape(leads, regions, pair, column_blocks, width)  3.03 us
    broadcast_in_dim x3, local copies, waits for them, and re-layouts, gathered(): copies = jnp.broadcast_to(piece[None], (count,) + piece.shape)  2.71 us
  transfers between devices with their start and end apart: 5, of which 5 were waited for; matrix products, arithmetic and copies ran while one was open for 8% of the time, Pallas kernels for 0%

profile of v4, /device:TPU:2, one launch (start us, length us, event | category | flops | bytes accessed | tf_op | source)
XLA Modules:
  0.0 101.3 jit_solution(7260283106726733267)
XLA Ops:
  0.0 0.0 copy-start
  0.0 0.0 copy-start.2
  0.0 0.0 copy-start.3
  0.0 1.7 %broadcast_in_dim.23 = f32[4,2,64,128]{3,2,1,0:T(8,128)} broadcast(f32[2,64,128]{2,1,0:T(8,128)} %bitcast.39), dimensions={1,2,3} | broadcast | bytes 327680 | tf_op jit(solution)/shard_map/broadcast_in_dim | solution.py:19
  1.7 9.3 %all-to-all-start = ((f32[4,2,64,128]{3,2,1,0:T(8,128)}), f32[4,2,64,128]{3,2,1,0:T(8,128)S(1)}, u32[]{:S(2)}, u32[]{:S(2)}) async-start(f32[4,2,64,128]{3,2,1,0:T(8,128)} %broadcast_in_dim.23), calls=%async_computation | async-start | bytes 524288 | tf_op jit(solution)/shard_map/all_to_all | solution.py:20
  11.0 3.0 %copy.31 = f32[2,4,2,128,128]{4,2,0,1,3:T(2,128)} copy(f32[2,4,2,128,128]{4,3,2,1,0:T(8,128)} %bitcast.38) | data formatting | bytes 2097152 | tf_op jit(solution)/shard_map/reshape | solution.py:45
  14.0 0.0 copy-start.1
  14.0 2.2 %all-to-all-done = f32[4,2,64,128]{3,2,1,0:T(8,128)S(1)} async-done(((f32[4,2,64,128]{3,2,1,0:T(8,128)}), f32[4,2,64,128]{3,2,1,0:T(8,128)S(1)}, u32[]{:S(2)}, u32[]{:S(2)}) %all-to-all-start) | async-done | bytes 262176 | tf_op jit(solution)/shard_map/all_to_all | solution.py:20
  16.2 17.9 %all-to-all-start.1 = ((f32[512,1,512]{2,1,0:T(1,128)}), f32[512,1,512]{2,1,0:T(1,128)}, u32[]{:S(2)}, u32[]{:S(2)}) async-start(f32[512,1,512]{2,1,0:T(1,128)} %bitcast.34), calls=%async_computation.1 | async-start | bytes 2097152 | tf_op jit(solution)/shard_map/all_to_all | solution.py:47
  34.1 0.0 copy-start.4
  34.1 0.0 copy-done.2
  34.1 0.7 copy.30
  34.9 0.0 copy-done.3
  34.9 0.7 copy.29
  35.6 27.5 %all-to-all-done.1 = f32[512,1,512]{2,1,0:T(1,128)} async-done(((f32[512,1,512]{2,1,0:T(1,128)}), f32[512,1,512]{2,1,0:T(1,128)}, u32[]{:S(2)}, u32[]{:S(2)}) %all-to-all-start.1) | async-done | bytes 1048608 | tf_op jit(solution)/shard_map/all_to_all | solution.py:47
  63.1 2.1 %convolution_bitcast_fusion = f32[128,2,2,64]{0,3,1,2:T(8,128)S(1)} fusion(f32[128,4,2,2,128]{4,3,2,1,0:T(2,128)} %bitcast.7, f32[4,2,64,128]{3,2,1,0:T(8,128)S(1)} %all-to-all-done), kind=kOutput, calls=%fused_computation.15 | convolution fusion | flops 100663296 | bytes 1441792 | tf_op jit(solution)/shard_map/mdljc,dltc->mjlt/dot_general | solution.py:51
  65.1 0.2 copy.35
  65.3 0.2 broadcast_in_dim.24
  65.5 0.8 broadcast_in_dim.25
  66.3 6.1 %all-to-all-start.2 = ((f32[4,256,128]{2,1,0:T(8,128)}), f32[4,256,128]{2,1,0:T(8,128)}, u32[]{:S(2)}, u32[]{:S(2)}) async-start(f32[4,256,128]{2,1,0:T(8,128)} %broadcast_in_dim.25), calls=%async_computation.2 | async-start | bytes 1048576 | tf_op jit(solution)/shard_map/all_to_all | solution.py:20
  72.4 1.4 %gather_fusion.2 = f32[3,16]{1,0:T(4,128)S(1)} fusion(f32[128,16]{1,0:T(8,128)} %copy.30, s32[1024]{0:T(1024)S(1)} %pad_clamp_fusion), kind=kCustom, calls=%fused_computation.2 | custom fusion | bytes 396 | tf_op jit(solution)/shard_map/gather | solution.py:27
  73.8 1.4 %gather_fusion = s32[3,16]{1,0:T(4,128)S(1)} fusion(s32[128,16]{1,0:T(8,128)} %copy.29, s32[1024]{0:T(1024)S(1)} %pad_clamp_fusion), kind=kCustom, calls=%fused_computation | custom fusion | bytes 396 | tf_op jit(solution)/shard_map/gather | solution.py:26
  75.2 0.0 copy-done.1
  75.2 0.6 gather_fusion.1
  75.8 0.1 iota_compare_fusion
  75.9 5.1 %all-to-all-done.2 = f32[4,256,128]{2,1,0:T(8,128)} async-done(((f32[4,256,128]{2,1,0:T(8,128)}), f32[4,256,128]{2,1,0:T(8,128)}, u32[]{:S(2)}, u32[]{:S(2)}) %all-to-all-start.2) | async-done | bytes 524320 | tf_op jit(solution)/shard_map/all_to_all | solution.py:20
  81.0 1.2 %copy.36 = f32[128,4,2,128]{3,2,1,0:T(2,128)S(1)} copy(f32[128,4,2,128]{3,2,0,1:T(2,128)} %bitcast.12) | data formatting | bytes 1048576 | tf_op jit(solution)/shard_map/transpose | solution.py:54
  82.2 1.9 %collective-permute-start.1 = (f32[1024,128]{1,0:T(8,128)S(1)}, f32[1024,128]{1,0:T(8,128)S(1)}, u32[]{:S(2)}, u32[]{:S(2)}) collective-permute-start(f32[1024,128]{1,0:T(8,128)S(1)} %bitcast.35), channel_id=1, source_target_pairs={{4,0},{8,4},{12,8},{16,12},{20,16},{24,20},{28,24},{32,28},{36,32}... | collective-permute-start | bytes 1572872 | tf_op jit(solution)/shard_map/ppermute | solution.py:14
  84.2 2.4 %collective-permute-start = (f32[1024,128]{1,0:T(8,128)S(1)}, f32[1024,128]{1,0:T(8,128)S(1)}, u32[]{:S(2)}, u32[]{:S(2)}) collective-permute-start(f32[1024,128]{1,0:T(8,128)S(1)} %bitcast.36), channel_id=1, source_target_pairs={{508,0},{0,4},{4,8},{8,12},{12,16},{16,20},{20,24},{24,28},{28,32}... | collective-permute-start | bytes 1572872 | tf_op jit(solution)/shard_map/ppermute | solution.py:14
  86.6 0.2 select_reduce_fusion
  86.7 0.0 copy-done.4
  86.7 4.1 %collective-permute-done.1 = f32[1024,128]{1,0:T(8,128)S(1)} collective-permute-done((f32[1024,128]{1,0:T(8,128)S(1)}, f32[1024,128]{1,0:T(8,128)S(1)}, u32[]{:S(2)}, u32[]{:S(2)}) %collective-permute-start.1) | collective-permute-done | bytes 524320 | tf_op jit(solution)/shard_map/ppermute | solution.py:14
  90.8 7.1 %collective-permute-done = f32[1024,128]{1,0:T(8,128)S(1)} collective-permute-done((f32[1024,128]{1,0:T(8,128)S(1)}, f32[1024,128]{1,0:T(8,128)S(1)}, u32[]{:S(2)}, u32[]{:S(2)}) %collective-permute-start) | collective-permute-done | bytes 524320 | tf_op jit(solution)/shard_map/ppermute | solution.py:14
  98.0 0.0 copy-done
  98.0 2.4 %fusion = f32[6,128,128]{1,2,0:T(8,128)S(1)} fusion(f32[6,128,1024]{2,1,0:T(8,128)S(1)} %bitcast.33, f32[1024,128]{1,0:T(8,128)S(1)} %collective-permute-done.1, f32[6]{0:T(128)S(1)} %get-tuple-element.6, f32[1024,128]{1,0:T(8,128)S(1)} %bitcast.37, f32[6]{0:T(128)S(1)} %get-tuple-element.7, f32[1024,128]{1,0:T(8,128)S(1)} %collective-permute-done, ...), kind=kOutput, calls=%fused_computation.3 | convolution fusion | flops 607911936 | bytes 5111880 | tf_op jit(solution)/shard_map/irk,ikt->irt/dot_general | solution.py:67
  100.4 0.9 bitcast_multiply_fusion
  (5 shorter events, 0.0 us)
Async XLA Ops:
  0.0 98.0 %copy-start = (f32[768,1024]{1,0:T(8,128)S(1)}, f32[768,1024]{1,0:T(8,128)}, u32[]{:S(2)}) copy-start(f32[768,1024]{1,0:T(8,128)} %param.9) | copy-start | bytes 9437188
  0.0 34.1 %copy-start.2 = (f32[128,16]{0,1:T(8,128)S(1)}, f32[128,16]{0,1:T(8,128)}, u32[]{:S(2)}) copy-start(f32[128,16]{0,1:T(8,128)} %param.12) | copy-start | bytes 24580
  0.0 34.9 %copy-start.3 = (s32[128,16]{0,1:T(8,128)S(1)}, s32[128,16]{0,1:T(8,128)}, u32[]{:S(2)}) copy-start(s32[128,16]{0,1:T(8,128)} %param.11) | copy-start | bytes 24580
  1.7 14.5 %all-to-all-start = ((f32[4,2,64,128]{3,2,1,0:T(8,128)}), f32[4,2,64,128]{3,2,1,0:T(8,128)S(1)}, u32[]{:S(2)}, u32[]{:S(2)}) async-start(f32[4,2,64,128]{3,2,1,0:T(8,128)} %broadcast_in_dim.23), calls=%async_computation | async-start | bytes 524288 | tf_op jit(solution)/shard_map/all_to_all | solution.py:20
  14.0 61.2 %copy-start.1 = (s32[128]{0:T(128)S(1)}, s32[128]{0:T(128)}, u32[]{:S(2)}) copy-start(s32[128]{0:T(128)} %param.13) | copy-start | bytes 1540
  16.2 46.8 %all-to-all-start.1 = ((f32[512,1,512]{2,1,0:T(1,128)}), f32[512,1,512]{2,1,0:T(1,128)}, u32[]{:S(2)}, u32[]{:S(2)}) async-start(f32[512,1,512]{2,1,0:T(1,128)} %bitcast.34), calls=%async_computation.1 | async-start | bytes 2097152 | tf_op jit(solution)/shard_map/all_to_all | solution.py:47
  34.1 52.6 %copy-start.4 = (f32[768]{0:T(1024)S(1)}, f32[768]{0:T(1024)}, u32[]{:S(2)}) copy-start(f32[768]{0:T(1024)} %param.10) | copy-start | bytes 9220
  66.3 14.7 %all-to-all-start.2 = ((f32[4,256,128]{2,1,0:T(8,128)}), f32[4,256,128]{2,1,0:T(8,128)}, u32[]{:S(2)}, u32[]{:S(2)}) async-start(f32[4,256,128]{2,1,0:T(8,128)} %broadcast_in_dim.25), calls=%async_computation.2 | async-start | bytes 1048576 | tf_op jit(solution)/shard_map/all_to_all | solution.py:20
  82.2 8.6 %collective-permute-start.1 = (f32[1024,128]{1,0:T(8,128)S(1)}, f32[1024,128]{1,0:T(8,128)S(1)}, u32[]{:S(2)}, u32[]{:S(2)}) collective-permute-start(f32[1024,128]{1,0:T(8,128)S(1)} %bitcast.35), channel_id=1, source_target_pairs={{4,0},{8,4},{12,8},{16,12},{20,16},{24,20},{28,24},{32,28},{36,32}... | collective-permute-start | bytes 1572872 | tf_op jit(solution)/shard_map/ppermute | solution.py:14
  84.2 13.8 %collective-permute-start = (f32[1024,128]{1,0:T(8,128)S(1)}, f32[1024,128]{1,0:T(8,128)S(1)}, u32[]{:S(2)}, u32[]{:S(2)}) collective-permute-start(f32[1024,128]{1,0:T(8,128)S(1)} %bitcast.36), channel_id=1, source_target_pairs={{508,0},{0,4},{4,8},{8,12},{12,16},{16,20},{20,24},{24,28},{28,32}... | collective-permute-start | bytes 1572872 | tf_op jit(solution)/shard_map/ppermute | solution.py:14

commit v5 on v4

--- a/solution.py
+++ b/solution.py
@@ -18,6 +18,15 @@
     count = lax.axis_size(axis)
     copies = jnp.broadcast_to(piece[None], (count,) + piece.shape)
     return lax.all_to_all(copies, axis, 0, 0, tiled=True)
+
+
+def shifted_copies(piece, axis):
+    count = lax.axis_size(axis)
+    index = lax.axis_index(axis)
+    arrived = [piece] + [from_behind(piece, axis, step) for step in range(1, count)]
+    order = (index - jnp.arange(count, dtype=jnp.int32)) % count
+    slots = jnp.zeros((count,) + piece.shape, piece.dtype)
+    return slots.at[order].set(jnp.stack(arrived))
 
 
 def own_weights(obs_lists, block_taper, counts, column_index, region_index, owned_blocks, regions):
@@ -47,7 +56,7 @@
     arrived = lax.all_to_all(grid, ("mem", "dom"), 0, 0, tiled=True)
     arrived = arrived.reshape(column_blocks, regions, leads, pair, width)
     targets = sensitivity.shape[1]
-    levels = gathered(sensitivity[:, :, 0, :], "dom")
+    levels = shifted_copies(sensitivity[:, :, 0, :], "dom")
     quarter = jnp.einsum("mdljc,dltc->mjlt", arrived, levels, precision=HIGH)
     quarter = quarter.reshape(column_blocks * pair, leads * targets)
     full = gathered(quarter, "dom").reshape(regions, column_blocks, pair, -1)

time: 102 us -> 94.2 us (0.924)
  waiting for transfers between devices: 46 us -> 29.8 us
  starting transfers between devices: 37.5 us -> 45.2 us
    all_to_all x1, waiting for transfers between devices: 27.5 us -> 11.9 us  [body(): arrived = lax.all_to_all(grid, ('mem', 'dom'), 0, 0, tiled=True)]
    ppermute x2 -> x5, starting transfers between devices: 4.33 us -> 15.9 us  [from_behind(): return lax.ppermute(block, axis, route)]
    all_to_all x2 -> x1, starting transfers between devices: 15.3 us -> 6.06 us  [gathered(): return lax.all_to_all(copies, axis, 0, 0, tiled=True)]
    all_to_all x1, starting transfers between devices: 17.9 us -> 23.3 us  [body(): arrived = lax.all_to_all(grid, ('mem', 'dom'), 0, 0, tiled=True)]
    all_to_all x2 -> x1, waiting for transfers between devices: 7.27 us -> 5.07 us  [gathered(): return lax.all_to_all(copies, axis, 0, 0, tiled=True)]
    broadcast_in_dim x3 -> x2, local copies, waits for them, and re-layouts: 2.71 us -> 1 us  [gathered(): copies = jnp.broadcast_to(piece[None], (count,) + piece.shape)]
    ppermute x2 -> x5, waiting for transfers between devices: 11.2 us -> 12.9 us  [from_behind(): return lax.ppermute(block, axis, route)]
    scatter x0 -> x1, local copies, waits for them, and re-layouts: none -> 1.58 us  [shifted_copies(): return slots.at[order].set(jnp.stack(arrived))]
  transfers between devices with their start and end apart: 5 -> 7, of which waited for: 5 -> 6; matrix products, arithmetic and copies ran while one was open for 8% -> 8% of each run, Pallas kernels for 0% -> 0%
where the time goes in v5:
time: 94.2 us; the launch traced here: 93.6 us
  starting transfers between devices  45.2 us (48%)
  waiting for transfers between devices  29.8 us (32%)
  local copies, waits for them, and re-layouts  12.1 us (13%)
  matrix products  4.42 us (5%)
  other arithmetic  1.9 us (2%)
    all_to_all x1, starting transfers between devices, body(): arrived = lax.all_to_all(grid, ('mem', 'dom'), 0, 0, tiled=True)  23.3 us
    ppermute x5, starting transfers between devices, from_behind(): return lax.ppermute(block, axis, route)  15.9 us
    ppermute x5, waiting for transfers between devices, from_behind(): return lax.ppermute(block, axis, route)  12.9 us
    all_to_all x1, waiting for transfers between devices, body(): arrived = lax.all_to_all(grid, ('mem', 'dom'), 0, 0, tiled=True)  11.9 us
    all_to_all x1, starting transfers between devices, gathered(): return lax.all_to_all(copies, axis, 0, 0, tiled=True)  6.06 us
    all_to_all x1, waiting for transfers between devices, gathered(): return lax.all_to_all(copies, axis, 0, 0, tiled=True)  5.07 us
    reshape x1, local copies, waits for them, and re-layouts, body(): grid = fcst_pert.reshape(leads, regions, pair, column_blocks, width)  3.18 us
    dot_general x1, matrix products, body(): result = jnp.einsum('irk,ikt->irt', rows, combined, precision=HIGH)  2.36 us
  transfers between devices with their start and end apart: 7, of which 6 were waited for; matrix products, arithmetic and copies ran while one was open for 8% of the time, Pallas kernels for 0%

profile of v5, /device:TPU:2, one launch (start us, length us, event | category | flops | bytes accessed | tf_op | source)
XLA Modules:
  0.0 93.6 jit_solution(15535713335377733949)
XLA Ops:
  0.0 0.0 copy-start
  0.0 0.0 copy-start.2
  0.0 0.0 copy-start.3
  0.0 0.0 copy-start.4
  0.0 3.2 %copy.33 = f32[2,4,2,128,128]{4,2,0,1,3:T(2,128)} copy(f32[2,4,2,128,128]{4,3,2,1,0:T(8,128)} %bitcast.44) | data formatting | bytes 2097152 | tf_op jit(solution)/shard_map/reshape | solution.py:54
  3.2 23.3 %all-to-all-start = ((f32[512,1,512]{2,1,0:T(1,128)}), f32[512,1,512]{2,1,0:T(1,128)}, u32[]{:S(2)}, u32[]{:S(2)}) async-start(f32[512,1,512]{2,1,0:T(1,128)} %bitcast.40), calls=%async_computation | async-start | bytes 2097152 | tf_op jit(solution)/shard_map/all_to_all | solution.py:56
  26.5 0.0 copy-start.1
  26.5 0.0 copy-done.2
  26.5 6.3 %collective-permute-start.2 = (f32[2,64,128]{2,1,0:T(8,128)S(1)}, f32[2,64,128]{2,1,0:T(8,128)S(1)}, u32[]{:S(2)}, u32[]{:S(2)}) collective-permute-start(f32[2,64,128]{2,1,0:T(8,128)S(1)} %bitcast.45), channel_id=1, source_target_pairs={{1,0},{2,1},{3,2},{0,3},{5,4},{6,5},{7,6},{4,7},{9,8},{10,9},{11,1... | collective-permute-start | bytes 196616 | tf_op jit(solution)/shard_map/ppermute | solution.py:14
  32.8 1.9 %collective-permute-start.1 = (f32[2,64,128]{2,1,0:T(8,128)S(1)}, f32[2,64,128]{2,1,0:T(8,128)S(1)}, u32[]{:S(2)}, u32[]{:S(2)}) collective-permute-start(f32[2,64,128]{2,1,0:T(8,128)S(1)} %bitcast.46), channel_id=1, source_target_pairs={{2,0},{3,1},{0,2},{1,3},{6,4},{7,5},{4,6},{5,7},{10,8},{11,9},{8,1... | collective-permute-start | bytes 196616 | tf_op jit(solution)/shard_map/ppermute | solution.py:14
  34.7 3.4 %collective-permute-start = (f32[2,64,128]{2,1,0:T(8,128)S(1)}, f32[2,64,128]{2,1,0:T(8,128)S(1)}, u32[]{:S(2)}, u32[]{:S(2)}) collective-permute-start(f32[2,64,128]{2,1,0:T(8,128)S(1)} %bitcast.47), channel_id=1, source_target_pairs={{3,0},{0,1},{1,2},{2,3},{7,4},{4,5},{5,6},{6,7},{11,8},{8,9},{9,10... | collective-permute-start | bytes 196616 | tf_op jit(solution)/shard_map/ppermute | solution.py:14
  38.1 0.0 copy-done.3
  38.1 0.7 copy.32
  38.8 0.0 copy-done.4
  38.8 0.7 copy.31
  39.6 0.0 collective-permute-done.2
  39.6 1.4 %collective-permute-done.1 = f32[2,64,128]{2,1,0:T(8,128)S(1)} collective-permute-done((f32[2,64,128]{2,1,0:T(8,128)S(1)}, f32[2,64,128]{2,1,0:T(8,128)S(1)}, u32[]{:S(2)}, u32[]{:S(2)}) %collective-permute-start.1) | collective-permute-done | bytes 65568 | tf_op jit(solution)/shard_map/ppermute | solution.py:14
  41.0 0.2 collective-permute-done
  41.2 0.7 pad_maximum_fusion
  42.0 0.0 copy-start.5
  42.0 1.6 %scatter_fusion = f32[4,2,64,128]{3,2,1,0:T(8,128)S(1)} fusion(f32[4,2,64,128]{3,2,1,0:T(8,128)S(1)} %broadcast_in_dim.16, s32[4]{0:T(128)S(1)} %fusion.17, f32[4,2,64,128]{3,2,1,0:T(8,128)} %pad_maximum_fusion), kind=kCustom, calls=%fused_computation.3 | custom fusion | bytes 786448 | tf_op jit(solution)/shard_map/scatter | solution.py:29
  43.6 11.9 %all-to-all-done = f32[512,1,512]{2,1,0:T(1,128)} async-done(((f32[512,1,512]{2,1,0:T(1,128)}), f32[512,1,512]{2,1,0:T(1,128)}, u32[]{:S(2)}, u32[]{:S(2)}) %all-to-all-start) | async-done | bytes 1048608 | tf_op jit(solution)/shard_map/all_to_all | solution.py:56
  55.4 2.1 %convolution_bitcast_fusion = f32[128,2,2,64]{0,3,1,2:T(8,128)S(1)} fusion(f32[128,4,2,2,128]{4,3,2,1,0:T(2,128)} %bitcast.12, f32[4,2,64,128]{3,2,1,0:T(8,128)S(1)} %scatter_fusion), kind=kOutput, calls=%fused_computation.16 | convolution fusion | flops 100663296 | bytes 1441792 | tf_op jit(solution)/shard_map/mdljc,dltc->mjlt/dot_general | solution.py:60
  57.5 0.2 copy.37
  57.7 0.2 broadcast_in_dim.17
  57.9 0.8 broadcast_in_dim.22
  58.7 6.1 %all-to-all-start.1 = ((f32[4,256,128]{2,1,0:T(8,128)}), f32[4,256,128]{2,1,0:T(8,128)}, u32[]{:S(2)}, u32[]{:S(2)}) async-start(f32[4,256,128]{2,1,0:T(8,128)} %broadcast_in_dim.22), calls=%async_computation.1 | async-start | bytes 1048576 | tf_op jit(solution)/shard_map/all_to_all | solution.py:20
  64.8 1.4 %gather_fusion.2 = f32[3,16]{1,0:T(4,128)S(1)} fusion(f32[128,16]{1,0:T(8,128)} %copy.32, s32[1024]{0:T(1024)S(1)} %pad_clamp_fusion), kind=kCustom, calls=%fused_computation.2 | custom fusion | bytes 396 | tf_op jit(solution)/shard_map/gather | solution.py:36
  66.2 1.4 %gather_fusion = s32[3,16]{1,0:T(4,128)S(1)} fusion(s32[128,16]{1,0:T(8,128)} %copy.31, s32[1024]{0:T(1024)S(1)} %pad_clamp_fusion), kind=kCustom, calls=%fused_computation | custom fusion | bytes 396 | tf_op jit(solution)/shard_map/gather | solution.py:35
  67.6 0.0 copy-done.1
  67.6 0.6 gather_fusion.1
  68.2 0.1 iota_compare_fusion
  68.3 5.1 %all-to-all-done.1 = f32[4,256,128]{2,1,0:T(8,128)} async-done(((f32[4,256,128]{2,1,0:T(8,128)}), f32[4,256,128]{2,1,0:T(8,128)}, u32[]{:S(2)}, u32[]{:S(2)}) %all-to-all-start.1) | async-done | bytes 524320 | tf_op jit(solution)/shard_map/all_to_all | solution.py:20
  73.4 1.2 %copy.38 = f32[128,4,2,128]{3,2,1,0:T(2,128)S(1)} copy(f32[128,4,2,128]{3,2,0,1:T(2,128)} %bitcast.17) | data formatting | bytes 1048576 | tf_op jit(solution)/shard_map/transpose | solution.py:63
  74.6 1.9 %collective-permute-start.4 = (f32[1024,128]{1,0:T(8,128)S(1)}, f32[1024,128]{1,0:T(8,128)S(1)}, u32[]{:S(2)}, u32[]{:S(2)}) collective-permute-start(f32[1024,128]{1,0:T(8,128)S(1)} %bitcast.41), channel_id=1, source_target_pairs={{4,0},{8,4},{12,8},{16,12},{20,16},{24,20},{28,24},{32,28},{36,32}... | collective-permute-start | bytes 1572872 | tf_op jit(solution)/shard_map/ppermute | solution.py:14
  76.5 2.4 %collective-permute-start.3 = (f32[1024,128]{1,0:T(8,128)S(1)}, f32[1024,128]{1,0:T(8,128)S(1)}, u32[]{:S(2)}, u32[]{:S(2)}) collective-permute-start(f32[1024,128]{1,0:T(8,128)S(1)} %bitcast.42), channel_id=1, source_target_pairs={{508,0},{0,4},{4,8},{8,12},{12,16},{16,20},{20,24},{24,28},{28,32}... | collective-permute-start | bytes 1572872 | tf_op jit(solution)/shard_map/ppermute | solution.py:14
  78.9 0.2 select_reduce_fusion
  79.1 0.0 copy-done.5
  79.1 4.1 %collective-permute-done.4 = f32[1024,128]{1,0:T(8,128)S(1)} collective-permute-done((f32[1024,128]{1,0:T(8,128)S(1)}, f32[1024,128]{1,0:T(8,128)S(1)}, u32[]{:S(2)}, u32[]{:S(2)}) %collective-permute-start.4) | collective-permute-done | bytes 524320 | tf_op jit(solution)/shard_map/ppermute | solution.py:14
  83.2 7.1 %collective-permute-done.3 = f32[1024,128]{1,0:T(8,128)S(1)} collective-permute-done((f32[1024,128]{1,0:T(8,128)S(1)}, f32[1024,128]{1,0:T(8,128)S(1)}, u32[]{:S(2)}, u32[]{:S(2)}) %collective-permute-start.3) | collective-permute-done | bytes 524320 | tf_op jit(solution)/shard_map/ppermute | solution.py:14
  90.3 0.0 copy-done
  90.3 2.4 %fusion = f32[6,128,128]{1,2,0:T(8,128)S(1)} fusion(f32[6,128,1024]{2,1,0:T(8,128)S(1)} %bitcast.39, f32[1024,128]{1,0:T(8,128)S(1)} %collective-permute-done.4, f32[6]{0:T(128)S(1)} %get-tuple-element.6, f32[1024,128]{1,0:T(8,128)S(1)} %bitcast.43, f32[6]{0:T(128)S(1)} %get-tuple-element.7, f32[1024,128]{1,0:T(8,128)S(1)} %collective-permute-done.3, ...), kind=kOutput, calls=%fused_computation.4 | convolution fusion | flops 607911936 | bytes 5111880 | tf_op jit(solution)/shard_map/irk,ikt->irt/dot_general | solution.py:76
  92.7 0.9 bitcast_multiply_fusion
  (7 shorter events, 0.1 us)
Async XLA Ops:
  0.0 90.3 %copy-start = (f32[768,1024]{1,0:T(8,128)S(1)}, f32[768,1024]{1,0:T(8,128)}, u32[]{:S(2)}) copy-start(f32[768,1024]{1,0:T(8,128)} %param.9) | copy-start | bytes 9437188
  0.0 26.5 %copy-start.2 = (f32[2,64,1,128]{3,2,1,0:T(1,128)S(1)}, f32[2,64,1,128]{3,2,1,0:T(1,128)}, u32[]{:S(2)}) copy-start(f32[2,64,1,128]{3,2,1,0:T(1,128)} %param.8) | copy-start | bytes 196612
  0.0 38.1 %copy-start.3 = (f32[128,16]{0,1:T(8,128)S(1)}, f32[128,16]{0,1:T(8,128)}, u32[]{:S(2)}) copy-start(f32[128,16]{0,1:T(8,128)} %param.12) | copy-start | bytes 24580
  0.0 38.8 %copy-start.4 = (s32[128,16]{0,1:T(8,128)S(1)}, s32[128,16]{0,1:T(8,128)}, u32[]{:S(2)}) copy-start(s32[128,16]{0,1:T(8,128)} %param.11) | copy-start | bytes 24580
  3.2 52.2 %all-to-all-start = ((f32[512,1,512]{2,1,0:T(1,128)}), f32[512,1,512]{2,1,0:T(1,128)}, u32[]{:S(2)}, u32[]{:S(2)}) async-start(f32[512,1,512]{2,1,0:T(1,128)} %bitcast.40), calls=%async_computation | async-start | bytes 2097152 | tf_op jit(solution)/shard_map/all_to_all | solution.py:56
  26.5 41.1 %copy-start.1 = (s32[128]{0:T(128)S(1)}, s32[128]{0:T(128)}, u32[]{:S(2)}) copy-start(s32[128]{0:T(128)} %param.13) | copy-start | bytes 1540
  26.5 13.1 %collective-permute-start.2 = (f32[2,64,128]{2,1,0:T(8,128)S(1)}, f32[2,64,128]{2,1,0:T(8,128)S(1)}, u32[]{:S(2)}, u32[]{:S(2)}) collective-permute-start(f32[2,64,128]{2,1,0:T(8,128)S(1)} %bitcast.45), channel_id=1, source_target_pairs={{1,0},{2,1},{3,2},{0,3},{5,4},{6,5},{7,6},{4,7},{9,8},{10,9},{11,1... | collective-permute-start | bytes 196616 | tf_op jit(solution)/shard_map/ppermute | solution.py:14
  32.8 8.2 %collective-permute-start.1 = (f32[2,64,128]{2,1,0:T(8,128)S(1)}, f32[2,64,128]{2,1,0:T(8,128)S(1)}, u32[]{:S(2)}, u32[]{:S(2)}) collective-permute-start(f32[2,64,128]{2,1,0:T(8,128)S(1)} %bitcast.46), channel_id=1, source_target_pairs={{2,0},{3,1},{0,2},{1,3},{6,4},{7,5},{4,6},{5,7},{10,8},{11,9},{8,1... | collective-permute-start | bytes 196616 | tf_op jit(solution)/shard_map/ppermute | solution.py:14
  34.7 6.5 %collective-permute-start = (f32[2,64,128]{2,1,0:T(8,128)S(1)}, f32[2,64,128]{2,1,0:T(8,128)S(1)}, u32[]{:S(2)}, u32[]{:S(2)}) collective-permute-start(f32[2,64,128]{2,1,0:T(8,128)S(1)} %bitcast.47), channel_id=1, source_target_pairs={{3,0},{0,1},{1,2},{2,3},{7,4},{4,5},{5,6},{6,7},{11,8},{8,9},{9,10... | collective-permute-start | bytes 196616 | tf_op jit(solution)/shard_map/ppermute | solution.py:14
  42.0 37.1 %copy-start.5 = (f32[768]{0:T(1024)S(1)}, f32[768]{0:T(1024)}, u32[]{:S(2)}) copy-start(f32[768]{0:T(1024)} %param.10) | copy-start | bytes 9220
  58.7 14.7 %all-to-all-start.1 = ((f32[4,256,128]{2,1,0:T(8,128)}), f32[4,256,128]{2,1,0:T(8,128)}, u32[]{:S(2)}, u32[]{:S(2)}) async-start(f32[4,256,128]{2,1,0:T(8,128)} %broadcast_in_dim.22), calls=%async_computation.1 | async-start | bytes 1048576 | tf_op jit(solution)/shard_map/all_to_all | solution.py:20
  74.6 8.6 %collective-permute-start.4 = (f32[1024,128]{1,0:T(8,128)S(1)}, f32[1024,128]{1,0:T(8,128)S(1)}, u32[]{:S(2)}, u32[]{:S(2)}) collective-permute-start(f32[1024,128]{1,0:T(8,128)S(1)} %bitcast.41), channel_id=1, source_target_pairs={{4,0},{8,4},{12,8},{16,12},{20,16},{24,20},{28,24},{32,28},{36,32}... | collective-permute-start | bytes 1572872 | tf_op jit(solution)/shard_map/ppermute | solution.py:14
  76.5 13.8 %collective-permute-start.3 = (f32[1024,128]{1,0:T(8,128)S(1)}, f32[1024,128]{1,0:T(8,128)S(1)}, u32[]{:S(2)}, u32[]{:S(2)}) collective-permute-start(f32[1024,128]{1,0:T(8,128)S(1)} %bitcast.42), channel_id=1, source_target_pairs={{508,0},{0,4},{4,8},{8,12},{12,16},{16,20},{20,24},{24,28},{28,32}... | collective-permute-start | bytes 1572872 | tf_op jit(solution)/shard_map/ppermute | solution.py:14

commit v6 on v5

--- a/solution.py
+++ b/solution.py
@@ -59,13 +59,14 @@
     levels = shifted_copies(sensitivity[:, :, 0, :], "dom")
     quarter = jnp.einsum("mdljc,dltc->mjlt", arrived, levels, precision=HIGH)
     quarter = quarter.reshape(column_blocks * pair, leads * targets)
-    full = gathered(quarter, "dom").reshape(regions, column_blocks, pair, -1)
-    summed = jnp.transpose(full, (1, 0, 2, 3)).reshape(column_blocks * local_members, -1)
+    trio = jnp.stack([from_behind(quarter, "mem", 1), quarter, from_behind(quarter, "mem", -1)])
+    full = gathered(trio, "dom").reshape(regions, len(trio), column_blocks, pair, -1)
+    full = jnp.transpose(full, (1, 2, 0, 3, 4)).reshape(len(trio), column_blocks * local_members, -1)
     column_index = lax.axis_index("mem")
     region_index = lax.axis_index("dom")
     owned_rows = obs_pert.shape[0]
     owned_blocks = owned_rows // OBSB
-    sources = (from_behind(summed, "mem", 1), summed, from_behind(summed, "mem", -1))
+    sources = [full[s] for s in range(len(trio))]
     weight_rows = own_weights(
         obs_lists, block_taper, counts, column_index, region_index, owned_blocks, regions
     )

time: 94.2 us -> 103 us (1.093)
  the two profiles are of different devices: /device:TPU:2 before, /device:TPU:17 now
where the time goes in v6:
time: 103 us
  starting transfers between devices  43.2 us (42%)
  waiting for transfers between devices  40.5 us (39%)
  local copies, waits for them, and re-layouts  11.3 us (11%)
  matrix products  4.43 us (4%)
  other arithmetic  2.91 us (3%)
    all_to_all x1, starting transfers between devices, body(): arrived = lax.all_to_all(grid, ('mem', 'dom'), 0, 0, tiled=True)  23.4 us
    all_to_all x1, waiting for transfers between devices, gathered(): return lax.all_to_all(copies, axis, 0, 0, tiled=True)  18.9 us
    ppermute x5, starting transfers between devices, from_behind(): return lax.ppermute(block, axis, route)  15.5 us
    all_to_all x1, waiting for transfers between devices, body(): arrived = lax.all_to_all(grid, ('mem', 'dom'), 0, 0, tiled=True)  14.2 us
    ppermute x5, waiting for transfers between devices, from_behind(): return lax.ppermute(block, axis, route)  7.41 us
    all_to_all x1, starting transfers between devices, gathered(): return lax.all_to_all(copies, axis, 0, 0, tiled=True)  4.34 us
    reshape x1, local copies, waits for them, and re-layouts, body(): grid = fcst_pert.reshape(leads, regions, pair, column_blocks, width)  3.19 us
    dot_general x1, matrix products, body(): result = jnp.einsum('irk,ikt->irt', rows, combined, precision=HIGH)  2.37 us
  transfers between devices with their start and end apart: 7, of which 6 were waited for; matrix products, arithmetic and copies ran while one was open for 5% of the time, Pallas kernels for 0%

profile of v6, /device:TPU:17, one launch (start us, length us, event | category | flops | bytes accessed | tf_op | source)
XLA Modules:
  0.0 102.5 jit_solution(5868810063938757177)
XLA Ops:
  0.0 0.0 copy-start
  0.0 0.0 copy-start.2
  0.0 3.2 %copy.40 = f32[2,4,2,128,128]{4,2,0,1,3:T(2,128)} copy(f32[2,4,2,128,128]{4,3,2,1,0:T(8,128)} %bitcast.48) | data formatting | bytes 2097152 | tf_op jit(solution)/shard_map/reshape | solution.py:54
  3.2 23.4 %all-to-all-start = ((f32[512,1,512]{2,1,0:T(1,128)}), f32[512,1,512]{2,1,0:T(1,128)}, u32[]{:S(2)}, u32[]{:S(2)}) async-start(f32[512,1,512]{2,1,0:T(1,128)} %bitcast.44), calls=%async_computation | async-start | bytes 2097152 | tf_op jit(solution)/shard_map/all_to_all | solution.py:56
  26.6 0.0 copy-done.2
  26.6 3.1 %collective-permute-start = (f32[2,64,128]{2,1,0:T(8,128)S(1)}, f32[2,64,128]{2,1,0:T(8,128)S(1)}, u32[]{:S(2)}, u32[]{:S(2)}) collective-permute-start(f32[2,64,128]{2,1,0:T(8,128)S(1)} %bitcast.49), channel_id=1, source_target_pairs={{3,0},{0,1},{1,2},{2,3},{7,4},{4,5},{5,6},{6,7},{11,8},{8,9},{9,10... | collective-permute-start | bytes 196616 | tf_op jit(solution)/shard_map/ppermute | solution.py:14
  29.7 4.3 %collective-permute-start.1 = (f32[2,64,128]{2,1,0:T(8,128)S(1)}, f32[2,64,128]{2,1,0:T(8,128)S(1)}, u32[]{:S(2)}, u32[]{:S(2)}) collective-permute-start(f32[2,64,128]{2,1,0:T(8,128)S(1)} %bitcast.50), channel_id=1, source_target_pairs={{2,0},{3,1},{0,2},{1,3},{6,4},{7,5},{4,6},{5,7},{10,8},{11,9},{8,1... | collective-permute-start | bytes 196616 | tf_op jit(solution)/shard_map/ppermute | solution.py:14
  34.0 3.1 %collective-permute-start.2 = (f32[2,64,128]{2,1,0:T(8,128)S(1)}, f32[2,64,128]{2,1,0:T(8,128)S(1)}, u32[]{:S(2)}, u32[]{:S(2)}) collective-permute-start(f32[2,64,128]{2,1,0:T(8,128)S(1)} %bitcast.51), channel_id=1, source_target_pairs={{1,0},{2,1},{3,2},{0,3},{5,4},{6,5},{7,6},{4,7},{9,8},{10,9},{11,1... | collective-permute-start | bytes 196616 | tf_op jit(solution)/shard_map/ppermute | solution.py:14
  37.1 0.0 collective-permute-done
  37.2 1.4 %collective-permute-done.1 = f32[2,64,128]{2,1,0:T(8,128)S(1)} collective-permute-done((f32[2,64,128]{2,1,0:T(8,128)S(1)}, f32[2,64,128]{2,1,0:T(8,128)S(1)}, u32[]{:S(2)}, u32[]{:S(2)}) %collective-permute-start.1) | collective-permute-done | bytes 65568 | tf_op jit(solution)/shard_map/ppermute | solution.py:14
  38.6 1.5 %collective-permute-done.2 = f32[2,64,128]{2,1,0:T(8,128)S(1)} collective-permute-done((f32[2,64,128]{2,1,0:T(8,128)S(1)}, f32[2,64,128]{2,1,0:T(8,128)S(1)}, u32[]{:S(2)}, u32[]{:S(2)}) %collective-permute-start.2) | collective-permute-done | bytes 65568 | tf_op jit(solution)/shard_map/ppermute | solution.py:14
  40.1 0.7 pad_maximum_fusion.1
  40.8 1.6 %scatter_fusion = f32[4,2,64,128]{3,2,1,0:T(8,128)S(1)} fusion(f32[4,2,64,128]{3,2,1,0:T(8,128)S(1)} %broadcast_in_dim.14, s32[4]{0:T(128)S(1)} %fusion.17, f32[4,2,64,128]{3,2,1,0:T(8,128)} %pad_maximum_fusion.1), kind=kCustom, calls=%fused_computation.3 | custom fusion | bytes 786448 | tf_op jit(solution)/shard_map/scatter | solution.py:29
  42.4 14.2 %all-to-all-done = f32[512,1,512]{2,1,0:T(1,128)} async-done(((f32[512,1,512]{2,1,0:T(1,128)}), f32[512,1,512]{2,1,0:T(1,128)}, u32[]{:S(2)}, u32[]{:S(2)}) %all-to-all-start) | async-done | bytes 1048608 | tf_op jit(solution)/shard_map/all_to_all | solution.py:56
  56.7 2.1 %convolution_bitcast_fusion = f32[128,2,2,64]{0,3,1,2:T(8,128)S(1)} fusion(f32[128,4,2,2,128]{4,3,2,1,0:T(2,128)} %bitcast.12, f32[4,2,64,128]{3,2,1,0:T(8,128)S(1)} %scatter_fusion), kind=kOutput, calls=%fused_computation.16 | convolution fusion | flops 100663296 | bytes 1441792 | tf_op jit(solution)/shard_map/mdljc,dltc->mjlt/dot_general | solution.py:60
  58.7 0.2 copy.44
  58.9 0.8 reshape.161
  59.8 0.0 copy-start.3
  59.8 0.0 copy-start.4
  59.8 3.0 %collective-permute-start.3 = (f32[256,128]{1,0:T(8,128)}, f32[256,128]{1,0:T(8,128)}, u32[]{:S(2)}, u32[]{:S(2)}) collective-permute-start(f32[256,128]{1,0:T(8,128)} %reshape.161), channel_id=1, source_target_pairs={{508,0},{0,4},{4,8},{8,12},{12,16},{16,20},{20,24},{24,28},{28,32}... | collective-permute-start | bytes 393224 | tf_op jit(solution)/shard_map/ppermute | solution.py:14
  62.8 1.9 %collective-permute-start.4 = (f32[256,128]{1,0:T(8,128)}, f32[256,128]{1,0:T(8,128)}, u32[]{:S(2)}, u32[]{:S(2)}) collective-permute-start(f32[256,128]{1,0:T(8,128)} %reshape.161), channel_id=1, source_target_pairs={{4,0},{8,4},{12,8},{16,12},{20,16},{24,20},{28,24},{32,28},{36,32}... | collective-permute-start | bytes 393224 | tf_op jit(solution)/shard_map/ppermute | solution.py:14
  64.8 0.2 stack_reshape.3
  64.9 0.0 copy-start.1
  64.9 0.1 collective-permute-done.3
  65.1 4.4 %collective-permute-done.4 = f32[256,128]{1,0:T(8,128)} collective-permute-done((f32[256,128]{1,0:T(8,128)}, f32[256,128]{1,0:T(8,128)}, u32[]{:S(2)}, u32[]{:S(2)}) %collective-permute-start.4) | collective-permute-done | bytes 131104 | tf_op jit(solution)/shard_map/ppermute | solution.py:14
  69.4 0.0 copy-start.5
  69.4 1.0 pad_maximum_fusion
  70.4 1.3 %broadcast_in_dim.15 = f32[4,3,256,128]{3,2,1,0:T(8,128)} broadcast(f32[3,256,128]{2,1,0:T(8,128)S(1)} %pad_maximum_fusion), dimensions={1,2,3} | broadcast | bytes 1966080 | tf_op jit(solution)/shard_map/broadcast_in_dim | solution.py:19
  71.7 4.3 %all-to-all-start.1 = ((f32[4,3,256,128]{3,2,1,0:T(8,128)}), f32[4,3,256,128]{3,2,1,0:T(8,128)}, u32[]{:S(2)}, u32[]{:S(2)}) async-start(f32[4,3,256,128]{3,2,1,0:T(8,128)} %broadcast_in_dim.15), calls=%async_computation.1 | async-start | bytes 3145728 | tf_op jit(solution)/shard_map/all_to_all | solution.py:20
  76.1 0.0 copy-done.3
  76.1 0.1 copy.38
  76.2 0.0 copy-done.4
  76.2 0.1 copy.39
  76.3 0.6 gather_fusion
  76.9 0.6 gather_fusion.2
  77.4 0.0 copy-done.1
  77.4 0.6 gather_fusion.1
  78.1 0.1 iota_compare_fusion
  78.2 0.2 select_reduce_fusion
  78.3 0.0 copy-done.5
  78.3 18.9 %all-to-all-done.1 = f32[4,3,256,128]{3,2,1,0:T(8,128)} async-done(((f32[4,3,256,128]{3,2,1,0:T(8,128)}), f32[4,3,256,128]{3,2,1,0:T(8,128)}, u32[]{:S(2)}, u32[]{:S(2)}) %all-to-all-start.1) | async-done | bytes 1572896 | tf_op jit(solution)/shard_map/all_to_all | solution.py:20
  97.2 1.5 %fusion.18 = (f32[1,128,4,2,128]{4,3,1,0,2:T(2,128)S(1)}, f32[1,128,4,2,128]{4,3,1,0,2:T(2,128)S(1)}, f32[1,128,4,2,128]{4,3,1,0,2:T(2,128)S(1)}) fusion(f32[3,128,4,2,128]{4,3,1,0,2:T(2,128)} %bitcast.20), kind=kLoop, calls=%fused_computation.42 | loop fusion | bytes 3145728 | tf_op jit(solution)/shard_map/slice | solution.py:69
  98.7 0.2 copy.46
  98.9 0.2 copy.47
  99.0 0.2 copy.48
  99.2 0.0 copy-done
  99.2 2.4 %fusion = f32[6,128,128]{1,2,0:T(8,128)S(1)} fusion(f32[6,128,1024]{2,1,0:T(8,128)S(1)} %bitcast.43, f32[1024,128]{1,0:T(8,128)S(1)} %bitcast.47, f32[6]{0:T(128)S(1)} %get-tuple-element.9, f32[1024,128]{1,0:T(8,128)S(1)} %bitcast.46, f32[6]{0:T(128)S(1)} %get-tuple-element.10, f32[1024,128]{1,0:T(8,128)S(1)} %bitcast.45, f32[6]{0:T(128)S(1)} %get-tuple-element.8), kind=kOutput, calls=%fused_computation.4 | convolution fusion | flops 607911936 | bytes 5111880 | tf_op jit(solution)/shard_map/irk,ikt->irt/dot_general | solution.py:77
  101.6 0.9 bitcast_multiply_fusion
  (7 shorter events, 0.1 us)
Async XLA Ops:
  0.0 99.2 %copy-start = (f32[768,1024]{1,0:T(8,128)S(1)}, f32[768,1024]{1,0:T(8,128)}, u32[]{:S(2)}) copy-start(f32[768,1024]{1,0:T(8,128)} %param.9) | copy-start | bytes 9437188
  0.0 26.6 %copy-start.2 = (f32[2,64,1,128]{3,2,1,0:T(1,128)S(1)}, f32[2,64,1,128]{3,2,1,0:T(1,128)}, u32[]{:S(2)}) copy-start(f32[2,64,1,128]{3,2,1,0:T(1,128)} %param.8) | copy-start | bytes 196612
  3.2 53.5 %all-to-all-start = ((f32[512,1,512]{2,1,0:T(1,128)}), f32[512,1,512]{2,1,0:T(1,128)}, u32[]{:S(2)}, u32[]{:S(2)}) async-start(f32[512,1,512]{2,1,0:T(1,128)} %bitcast.44), calls=%async_computation | async-start | bytes 2097152 | tf_op jit(solution)/shard_map/all_to_all | solution.py:56
  26.6 10.5 %collective-permute-start = (f32[2,64,128]{2,1,0:T(8,128)S(1)}, f32[2,64,128]{2,1,0:T(8,128)S(1)}, u32[]{:S(2)}, u32[]{:S(2)}) collective-permute-start(f32[2,64,128]{2,1,0:T(8,128)S(1)} %bitcast.49), channel_id=1, source_target_pairs={{3,0},{0,1},{1,2},{2,3},{7,4},{4,5},{5,6},{6,7},{11,8},{8,9},{9,10... | collective-permute-start | bytes 196616 | tf_op jit(solution)/shard_map/ppermute | solution.py:14
  29.7 8.9 %collective-permute-start.1 = (f32[2,64,128]{2,1,0:T(8,128)S(1)}, f32[2,64,128]{2,1,0:T(8,128)S(1)}, u32[]{:S(2)}, u32[]{:S(2)}) collective-permute-start(f32[2,64,128]{2,1,0:T(8,128)S(1)} %bitcast.50), channel_id=1, source_target_pairs={{2,0},{3,1},{0,2},{1,3},{6,4},{7,5},{4,6},{5,7},{10,8},{11,9},{8,1... | collective-permute-start | bytes 196616 | tf_op jit(solution)/shard_map/ppermute | solution.py:14
  34.0 6.0 %collective-permute-start.2 = (f32[2,64,128]{2,1,0:T(8,128)S(1)}, f32[2,64,128]{2,1,0:T(8,128)S(1)}, u32[]{:S(2)}, u32[]{:S(2)}) collective-permute-start(f32[2,64,128]{2,1,0:T(8,128)S(1)} %bitcast.51), channel_id=1, source_target_pairs={{1,0},{2,1},{3,2},{0,3},{5,4},{6,5},{7,6},{4,7},{9,8},{10,9},{11,1... | collective-permute-start | bytes 196616 | tf_op jit(solution)/shard_map/ppermute | solution.py:14
  59.8 16.3 %copy-start.3 = (s32[128,16]{0,1:T(8,128)S(1)}, s32[128,16]{0,1:T(8,128)}, u32[]{:S(2)}) copy-start(s32[128,16]{0,1:T(8,128)} %param.11) | copy-start | bytes 24580
  59.8 16.4 %copy-start.4 = (f32[128,16]{0,1:T(8,128)S(1)}, f32[128,16]{0,1:T(8,128)}, u32[]{:S(2)}) copy-start(f32[128,16]{0,1:T(8,128)} %param.12) | copy-start | bytes 24580
  59.8 5.3 %collective-permute-start.3 = (f32[256,128]{1,0:T(8,128)}, f32[256,128]{1,0:T(8,128)}, u32[]{:S(2)}, u32[]{:S(2)}) collective-permute-start(f32[256,128]{1,0:T(8,128)} %reshape.161), channel_id=1, source_target_pairs={{508,0},{0,4},{4,8},{8,12},{12,16},{16,20},{20,24},{24,28},{28,32}... | collective-permute-start | bytes 393224 | tf_op jit(solution)/shard_map/ppermute | solution.py:14
  62.8 6.6 %collective-permute-start.4 = (f32[256,128]{1,0:T(8,128)}, f32[256,128]{1,0:T(8,128)}, u32[]{:S(2)}, u32[]{:S(2)}) collective-permute-start(f32[256,128]{1,0:T(8,128)} %reshape.161), channel_id=1, source_target_pairs={{4,0},{8,4},{12,8},{16,12},{20,16},{24,20},{28,24},{32,28},{36,32}... | collective-permute-start | bytes 393224 | tf_op jit(solution)/shard_map/ppermute | solution.py:14
  64.9 12.5 %copy-start.1 = (s32[128]{0:T(128)S(1)}, s32[128]{0:T(128)}, u32[]{:S(2)}) copy-start(s32[128]{0:T(128)} %param.13) | copy-start | bytes 1540
  69.4 8.9 %copy-start.5 = (f32[768]{0:T(1024)S(1)}, f32[768]{0:T(1024)}, u32[]{:S(2)}) copy-start(f32[768]{0:T(1024)} %param.10) | copy-start | bytes 9220
  71.7 25.5 %all-to-all-start.1 = ((f32[4,3,256,128]{3,2,1,0:T(8,128)}), f32[4,3,256,128]{3,2,1,0:T(8,128)}, u32[]{:S(2)}, u32[]{:S(2)}) async-start(f32[4,3,256,128]{3,2,1,0:T(8,128)} %broadcast_in_dim.15), calls=%async_computation.1 | async-start | bytes 3145728 | tf_op jit(solution)/shard_map/all_to_all | solution.py:20

commit v7 on v5

--- a/solution.py
+++ b/solution.py
@@ -65,17 +65,20 @@
     region_index = lax.axis_index("dom")
     owned_rows = obs_pert.shape[0]
     owned_blocks = owned_rows // OBSB
-    sources = (from_behind(summed, "mem", 1), summed, from_behind(summed, "mem", -1))
+    behind = from_behind(summed, "mem", 1)
+    ahead = from_behind(summed, "mem", -1)
     weight_rows = own_weights(
         obs_lists, block_taper, counts, column_index, region_index, owned_blocks, regions
     )
-    combined = sum(
-        weight_rows[s][:, None, None] * sources[s][None] for s in range(len(sources))
+    scale = (weighted_innovation / (M - 1))[:, None]
+    rows = obs_pert * scale
+    own = jnp.dot(rows, summed, precision=HIGH).reshape(owned_blocks, OBSB, -1)
+    rows = rows.reshape(owned_blocks, OBSB, -1)
+    others = weight_rows[0][:, None, None] * behind[None] + weight_rows[2][:, None, None] * ahead[None]
+    result = own * weight_rows[1][:, None, None] + jnp.einsum(
+        "irk,ikt->irt", rows, others, precision=HIGH
     )
-    rows = obs_pert.reshape(owned_blocks, OBSB, -1)
-    result = jnp.einsum("irk,ikt->irt", rows, combined, precision=HIGH)
-    result = result.reshape(owned_rows, -1)
-    return result * (weighted_innovation / (M - 1))[:, None]
+    return result.reshape(owned_rows, -1)
 
 
 def solution(mesh):

time: 94.2 us -> 92.5 us (0.982)
  the two profiles are of different devices: /device:TPU:2 before, /device:TPU:57 now
where the time goes in v7:
time: 92.5 us; the launch traced here: 92.1 us
  starting transfers between devices  41.3 us (45%)
  waiting for transfers between devices  34.9 us (38%)
  local copies, waits for them, and re-layouts  8.15 us (9%)
  matrix products  5.08 us (5%)
  other arithmetic  2.45 us (3%)
    all_to_all x1, starting transfers between devices, body(): arrived = lax.all_to_all(grid, ('mem', 'dom'), 0, 0, tiled=True)  21.1 us
    ppermute x5, starting transfers between devices, from_behind(): return lax.ppermute(block, axis, route)  16.1 us
    all_to_all x1, waiting for transfers between devices, body(): arrived = lax.all_to_all(grid, ('mem', 'dom'), 0, 0, tiled=True)  13.9 us
    ppermute x5, waiting for transfers between devices, from_behind(): return lax.ppermute(block, axis, route)  13.5 us
    all_to_all x1, waiting for transfers between devices, gathered(): return lax.all_to_all(copies, axis, 0, 0, tiled=True)  7.51 us
    all_to_all x1, starting transfers between devices, gathered(): return lax.all_to_all(copies, axis, 0, 0, tiled=True)  4.13 us
    reshape x1, local copies, waits for them, and re-layouts, body(): grid = fcst_pert.reshape(leads, regions, pair, column_blocks, width)  3.07 us
    dot_general x1, matrix products, body(): jnp.einsum('irk,ikt->irt', rows, others, precision=HIGH)  2.84 us
  transfers between devices with their start and end apart: 7, of which 6 were waited for; matrix products, arithmetic and copies ran while one was open for 7% of the time, Pallas kernels for 0%

profile of v7, /device:TPU:57, one launch (start us, length us, event | category | flops | bytes accessed | tf_op | source)
XLA Modules:
  0.0 92.1 jit_solution(16277361301489434511)
XLA Ops:
  0.0 0.0 copy-start
  0.0 0.0 copy-start.1
  0.0 0.0 copy-start.2
  0.0 0.0 copy-start.3
  0.0 0.0 copy-start.4
  0.0 3.1 %copy.25 = f32[2,4,2,128,128]{4,2,0,1,3:T(2,128)} copy(f32[2,4,2,128,128]{4,3,2,1,0:T(8,128)} %bitcast.47) | data formatting | bytes 2097152 | tf_op jit(solution)/shard_map/reshape | solution.py:54
  3.1 21.1 %all-to-all-start = ((f32[512,1,512]{2,1,0:T(1,128)}), f32[512,1,512]{2,1,0:T(1,128)S(1)}, u32[]{:S(2)}, u32[]{:S(2)}) async-start(f32[512,1,512]{2,1,0:T(1,128)} %bitcast.10), calls=%async_computation | async-start | bytes 2097152 | tf_op jit(solution)/shard_map/all_to_all | solution.py:56
  24.2 0.0 copy-done.1
  24.2 4.4 %collective-permute-start.2 = (f32[2,64,128]{2,1,0:T(8,128)S(1)}, f32[2,64,128]{2,1,0:T(8,128)S(1)}, u32[]{:S(2)}, u32[]{:S(2)}) collective-permute-start(f32[2,64,128]{2,1,0:T(8,128)S(1)} %bitcast.48), channel_id=1, source_target_pairs={{1,0},{2,1},{3,2},{0,3},{5,4},{6,5},{7,6},{4,7},{9,8},{10,9},{11,1... | collective-permute-start | bytes 196616 | tf_op jit(solution)/shard_map/ppermute | solution.py:14
  28.5 2.5 %collective-permute-start.1 = (f32[2,64,128]{2,1,0:T(8,128)S(1)}, f32[2,64,128]{2,1,0:T(8,128)S(1)}, u32[]{:S(2)}, u32[]{:S(2)}) collective-permute-start(f32[2,64,128]{2,1,0:T(8,128)S(1)} %bitcast.49), channel_id=1, source_target_pairs={{2,0},{3,1},{0,2},{1,3},{6,4},{7,5},{4,6},{5,7},{10,8},{11,9},{8,1... | collective-permute-start | bytes 196616 | tf_op jit(solution)/shard_map/ppermute | solution.py:14
  31.0 2.5 %collective-permute-start = (f32[2,64,128]{2,1,0:T(8,128)S(1)}, f32[2,64,128]{2,1,0:T(8,128)S(1)}, u32[]{:S(2)}, u32[]{:S(2)}) collective-permute-start(f32[2,64,128]{2,1,0:T(8,128)S(1)} %bitcast.50), channel_id=1, source_target_pairs={{3,0},{0,1},{1,2},{2,3},{7,4},{4,5},{5,6},{6,7},{11,8},{8,9},{9,10... | collective-permute-start | bytes 196616 | tf_op jit(solution)/shard_map/ppermute | solution.py:14
  33.5 0.0 copy-done.2
  33.5 0.1 copy.31
  33.7 0.0 copy-done
  33.7 0.6 gather_fusion.1
  34.3 0.6 gather_fusion
  34.9 0.0 copy-done.3
  34.9 0.1 copy.32
  35.0 0.6 gather_fusion.2
  35.6 0.1 iota_compare_fusion
  35.6 0.0 copy-done.4
  35.6 0.0 collective-permute-done.2
  35.7 0.7 collective-permute-done.1
  36.4 3.5 %collective-permute-done = f32[2,64,128]{2,1,0:T(8,128)S(1)} collective-permute-done((f32[2,64,128]{2,1,0:T(8,128)S(1)}, f32[2,64,128]{2,1,0:T(8,128)S(1)}, u32[]{:S(2)}, u32[]{:S(2)}) %collective-permute-start) | collective-permute-done | bytes 65568 | tf_op jit(solution)/shard_map/ppermute | solution.py:14
  39.9 0.7 scatter_fusion
  40.6 13.9 %all-to-all-done = f32[512,1,512]{2,1,0:T(1,128)S(1)} async-done(((f32[512,1,512]{2,1,0:T(1,128)}), f32[512,1,512]{2,1,0:T(1,128)S(1)}, u32[]{:S(2)}, u32[]{:S(2)}) %all-to-all-start) | async-done | bytes 1048608 | tf_op jit(solution)/shard_map/all_to_all | solution.py:56
  54.5 0.8 convolution_bitcast_fusion
  55.3 0.2 copy.29
  55.5 0.2 broadcast_in_dim.15
  55.7 0.8 broadcast_in_dim.16
  56.5 4.1 %all-to-all-start.1 = ((f32[4,256,128]{2,1,0:T(8,128)}), f32[4,256,128]{2,1,0:T(8,128)}, u32[]{:S(2)}, u32[]{:S(2)}) async-start(f32[4,256,128]{2,1,0:T(8,128)} %broadcast_in_dim.16), calls=%async_computation.1 | async-start | bytes 1048576 | tf_op jit(solution)/shard_map/all_to_all | solution.py:20
  60.7 0.2 select_reduce_fusion
  60.8 2.2 %broadcast_multiply_fusion = f32[768,1024]{1,0:T(8,128)S(1)} fusion(f32[768,1024]{1,0:T(8,128)} %param.9, f32[768]{0:T(1024)S(1)} %broadcast_multiply_fusion.1), kind=kLoop, calls=%fused_computation.12 | loop fusion | flops 786432 | bytes 6294528 | tf_op jit(solution)/shard_map/mul | solution.py:74
  63.0 7.5 %all-to-all-done.1 = f32[4,256,128]{2,1,0:T(8,128)} async-done(((f32[4,256,128]{2,1,0:T(8,128)}), f32[4,256,128]{2,1,0:T(8,128)}, u32[]{:S(2)}, u32[]{:S(2)}) %all-to-all-start.1) | async-done | bytes 524320 | tf_op jit(solution)/shard_map/all_to_all | solution.py:20
  70.5 1.2 %copy.30 = f32[128,4,2,128]{3,2,1,0:T(2,128)S(1)} copy(f32[128,4,2,128]{3,2,0,1:T(2,128)} %bitcast.16) | data formatting | bytes 1048576 | tf_op jit(solution)/shard_map/transpose | solution.py:63
  71.7 4.9 %collective-permute-start.3 = (f32[1024,128]{1,0:T(8,128)S(1)}, f32[1024,128]{1,0:T(8,128)S(1)}, u32[]{:S(2)}, u32[]{:S(2)}) collective-permute-start(f32[1024,128]{1,0:T(8,128)S(1)} %bitcast.44), channel_id=1, source_target_pairs={{508,0},{0,4},{4,8},{8,12},{12,16},{16,20},{20,24},{24,28},{28,32}... | collective-permute-start | bytes 1572872 | tf_op jit(solution)/shard_map/ppermute | solution.py:14
  76.6 1.9 %collective-permute-start.4 = (f32[1024,128]{1,0:T(8,128)S(1)}, f32[1024,128]{1,0:T(8,128)S(1)}, u32[]{:S(2)}, u32[]{:S(2)}) collective-permute-start(f32[1024,128]{1,0:T(8,128)S(1)} %bitcast.45), channel_id=1, source_target_pairs={{4,0},{8,4},{12,8},{16,12},{20,16},{24,20},{28,24},{32,28},{36,32}... | collective-permute-start | bytes 1572872 | tf_op jit(solution)/shard_map/ppermute | solution.py:14
  78.5 1.4 %convolution_multiply_fusion = f32[6,128,128]{2,1,0:T(8,128)S(1)} fusion(f32[6,128,1024]{2,1,0:T(8,128)S(1)} %bitcast.41, f32[1024,128,1]{1,0,2:T(8,128)S(1)} %bitcast.46, f32[6]{0:T(128)S(1)} %get-tuple-element.7), kind=kOutput, calls=%fused_computation.14 | convolution fusion | flops 604078080 | bytes 4063256 | tf_op jit(solution)/shard_map/dot_general | solution.py:75
  79.9 2.8 %collective-permute-done.3 = f32[1024,128]{1,0:T(8,128)S(1)} collective-permute-done((f32[1024,128]{1,0:T(8,128)S(1)}, f32[1024,128]{1,0:T(8,128)S(1)}, u32[]{:S(2)}, u32[]{:S(2)}) %collective-permute-start.3) | collective-permute-done | bytes 524320 | tf_op jit(solution)/shard_map/ppermute | solution.py:14
  82.7 6.5 %collective-permute-done.4 = f32[1024,128]{1,0:T(8,128)S(1)} collective-permute-done((f32[1024,128]{1,0:T(8,128)S(1)}, f32[1024,128]{1,0:T(8,128)S(1)}, u32[]{:S(2)}, u32[]{:S(2)}) %collective-permute-start.4) | collective-permute-done | bytes 524320 | tf_op jit(solution)/shard_map/ppermute | solution.py:14
  89.2 2.8 %fusion.8 = f32[6,128,128]{2,1,0:T(8,128)} fusion(f32[6,128,128]{2,1,0:T(8,128)S(1)} %convolution_multiply_fusion, f32[6,128,1024]{2,1,0:T(8,128)S(1)} %bitcast.42, f32[1024,128]{1,0:T(8,128)S(1)} %collective-permute-done.4, f32[6]{0:T(128)S(1)} %get-tuple-element.6, f32[1024,128]{1,0:T(8,128)S(1)} %collective-permute-done.3, f32[6]{0:T(128)S(1)} %get-tuple-element.5), kind=kOutput, calls=%fused_computation.13 | convolution fusion | flops 606437376 | bytes 4980784 | tf_op jit(solution)/shard_map/irk,ikt->irt/dot_general | solution.py:78
  (8 shorter events, 0.1 us)
Async XLA Ops:
  0.0 33.7 %copy-start = (s32[128]{0:T(128)S(1)}, s32[128]{0:T(128)}, u32[]{:S(2)}) copy-start(s32[128]{0:T(128)} %param.13) | copy-start | bytes 1540
  0.0 24.2 %copy-start.1 = (f32[2,64,1,128]{3,2,1,0:T(1,128)S(1)}, f32[2,64,1,128]{3,2,1,0:T(1,128)}, u32[]{:S(2)}) copy-start(f32[2,64,1,128]{3,2,1,0:T(1,128)} %param.8) | copy-start | bytes 196612
  0.0 33.5 %copy-start.2 = (s32[128,16]{0,1:T(8,128)S(1)}, s32[128,16]{0,1:T(8,128)}, u32[]{:S(2)}) copy-start(s32[128,16]{0,1:T(8,128)} %param.11) | copy-start | bytes 24580
  0.0 34.9 %copy-start.3 = (f32[128,16]{0,1:T(8,128)S(1)}, f32[128,16]{0,1:T(8,128)}, u32[]{:S(2)}) copy-start(f32[128,16]{0,1:T(8,128)} %param.12) | copy-start | bytes 24580
  0.0 35.6 %copy-start.4 = (f32[768]{0:T(1024)S(1)}, f32[768]{0:T(1024)}, u32[]{:S(2)}) copy-start(f32[768]{0:T(1024)} %param.10) | copy-start | bytes 9220
  3.1 51.4 %all-to-all-start = ((f32[512,1,512]{2,1,0:T(1,128)}), f32[512,1,512]{2,1,0:T(1,128)S(1)}, u32[]{:S(2)}, u32[]{:S(2)}) async-start(f32[512,1,512]{2,1,0:T(1,128)} %bitcast.10), calls=%async_computation | async-start | bytes 2097152 | tf_op jit(solution)/shard_map/all_to_all | solution.py:56
  24.2 11.5 %collective-permute-start.2 = (f32[2,64,128]{2,1,0:T(8,128)S(1)}, f32[2,64,128]{2,1,0:T(8,128)S(1)}, u32[]{:S(2)}, u32[]{:S(2)}) collective-permute-start(f32[2,64,128]{2,1,0:T(8,128)S(1)} %bitcast.48), channel_id=1, source_target_pairs={{1,0},{2,1},{3,2},{0,3},{5,4},{6,5},{7,6},{4,7},{9,8},{10,9},{11,1... | collective-permute-start | bytes 196616 | tf_op jit(solution)/shard_map/ppermute | solution.py:14
  28.5 7.8 %collective-permute-start.1 = (f32[2,64,128]{2,1,0:T(8,128)S(1)}, f32[2,64,128]{2,1,0:T(8,128)S(1)}, u32[]{:S(2)}, u32[]{:S(2)}) collective-permute-start(f32[2,64,128]{2,1,0:T(8,128)S(1)} %bitcast.49), channel_id=1, source_target_pairs={{2,0},{3,1},{0,2},{1,3},{6,4},{7,5},{4,6},{5,7},{10,8},{11,9},{8,1... | collective-permute-start | bytes 196616 | tf_op jit(solution)/shard_map/ppermute | solution.py:14
  31.0 8.8 %collective-permute-start = (f32[2,64,128]{2,1,0:T(8,128)S(1)}, f32[2,64,128]{2,1,0:T(8,128)S(1)}, u32[]{:S(2)}, u32[]{:S(2)}) collective-permute-start(f32[2,64,128]{2,1,0:T(8,128)S(1)} %bitcast.50), channel_id=1, source_target_pairs={{3,0},{0,1},{1,2},{2,3},{7,4},{4,5},{5,6},{6,7},{11,8},{8,9},{9,10... | collective-permute-start | bytes 196616 | tf_op jit(solution)/shard_map/ppermute | solution.py:14
  56.5 14.0 %all-to-all-start.1 = ((f32[4,256,128]{2,1,0:T(8,128)}), f32[4,256,128]{2,1,0:T(8,128)}, u32[]{:S(2)}, u32[]{:S(2)}) async-start(f32[4,256,128]{2,1,0:T(8,128)} %broadcast_in_dim.16), calls=%async_computation.1 | async-start | bytes 1048576 | tf_op jit(solution)/shard_map/all_to_all | solution.py:20
  71.7 11.0 %collective-permute-start.3 = (f32[1024,128]{1,0:T(8,128)S(1)}, f32[1024,128]{1,0:T(8,128)S(1)}, u32[]{:S(2)}, u32[]{:S(2)}) collective-permute-start(f32[1024,128]{1,0:T(8,128)S(1)} %bitcast.44), channel_id=1, source_target_pairs={{508,0},{0,4},{4,8},{8,12},{12,16},{16,20},{20,24},{24,28},{28,32}... | collective-permute-start | bytes 1572872 | tf_op jit(solution)/shard_map/ppermute | solution.py:14
  76.6 12.6 %collective-permute-start.4 = (f32[1024,128]{1,0:T(8,128)S(1)}, f32[1024,128]{1,0:T(8,128)S(1)}, u32[]{:S(2)}, u32[]{:S(2)}) collective-permute-start(f32[1024,128]{1,0:T(8,128)S(1)} %bitcast.45), channel_id=1, source_target_pairs={{4,0},{8,4},{12,8},{16,12},{20,16},{24,20},{28,24},{32,28},{36,32}... | collective-permute-start | bytes 1572872 | tf_op jit(solution)/shard_map/ppermute | solution.py:14

commit v8 on v7

--- a/solution.py
+++ b/solution.py
@@ -47,49 +47,64 @@
 
 def body(fcst_pert, sensitivity, obs_pert, weighted_innovation, obs_lists, block_taper, counts):
     leads, local_members, _, columns = fcst_pert.shape
-    column_blocks = lax.axis_size("mem")
+    cores = lax.axis_size("core")
+    column_blocks = lax.axis_size("pair") * cores
     regions = lax.axis_size("dom")
     width = columns // column_blocks
     pair = local_members // regions
     grid = fcst_pert.reshape(leads, regions, pair, column_blocks, width)
     grid = jnp.transpose(grid, (3, 1, 0, 2, 4)).reshape(column_blocks * regions, -1)
-    arrived = lax.all_to_all(grid, ("mem", "dom"), 0, 0, tiled=True)
+    arrived = lax.all_to_all(grid, ("pair", "core", "dom"), 0, 0, tiled=True)
     arrived = arrived.reshape(column_blocks, regions, leads, pair, width)
     targets = sensitivity.shape[1]
     levels = shifted_copies(sensitivity[:, :, 0, :], "dom")
     quarter = jnp.einsum("mdljc,dltc->mjlt", arrived, levels, precision=HIGH)
     quarter = quarter.reshape(column_blocks * pair, leads * targets)
-    full = gathered(quarter, "dom").reshape(regions, column_blocks, pair, -1)
-    summed = jnp.transpose(full, (1, 0, 2, 3)).reshape(column_blocks * local_members, -1)
-    column_index = lax.axis_index("mem")
+    both = gathered(quarter, ("core", "dom")).reshape(cores, regions, column_blocks, pair, -1)
+    both = jnp.transpose(both, (0, 2, 1, 3, 4)).reshape(cores, column_blocks * local_members, -1)
+    core_index = lax.axis_index("core")
+    column_index = lax.axis_index("pair") * cores + core_index
     region_index = lax.axis_index("dom")
     owned_rows = obs_pert.shape[0]
     owned_blocks = owned_rows // OBSB
-    behind = from_behind(summed, "mem", 1)
-    ahead = from_behind(summed, "mem", -1)
+    own = lax.dynamic_index_in_dim(both, core_index, 0, keepdims=False)
+    partner = lax.dynamic_index_in_dim(both, 1 - core_index, 0, keepdims=False)
+    route = [
+        (i, (i + cores) % column_blocks if i % cores == 0 else (i - cores) % column_blocks)
+        for i in range(column_blocks)
+    ]
+    far = lax.ppermute(partner, ("pair", "core"), route)
     weight_rows = own_weights(
         obs_lists, block_taper, counts, column_index, region_index, owned_blocks, regions
     )
+    first = core_index == 0
+    far_weight = jnp.where(first, weight_rows[0], weight_rows[2])
+    partner_weight = jnp.where(first, weight_rows[2], weight_rows[0])
     scale = (weighted_innovation / (M - 1))[:, None]
     rows = obs_pert * scale
-    own = jnp.dot(rows, summed, precision=HIGH).reshape(owned_blocks, OBSB, -1)
     rows = rows.reshape(owned_blocks, OBSB, -1)
-    others = weight_rows[0][:, None, None] * behind[None] + weight_rows[2][:, None, None] * ahead[None]
-    result = own * weight_rows[1][:, None, None] + jnp.einsum(
-        "irk,ikt->irt", rows, others, precision=HIGH
-    )
+    near = weight_rows[1][:, None, None] * own[None] + partner_weight[:, None, None] * partner[None]
+    result = jnp.einsum("irk,ikt->irt", rows, near, precision=HIGH)
+    distant = jnp.dot(rows.reshape(owned_rows, -1), far, precision=HIGH)
+    result = result + distant.reshape(owned_blocks, OBSB, -1) * far_weight[:, None, None]
     return result.reshape(owned_rows, -1)
 
 
 def solution(mesh):
+    members, regions = mesh.devices.shape
+    cores = 2
+    split = jax.sharding.Mesh(
+        mesh.devices.reshape(members // cores, cores, regions), ("pair", "core", "dom")
+    )
+    mem = ("pair", "core")
     in_specs = (
-        P(None, "mem", "dom", None),
-        P(None, None, "dom", "mem"),
-        P(("mem", "dom"), None),
-        P(("mem", "dom")),
+        P(None, mem, "dom", None),
+        P(None, None, "dom", mem),
+        P(mem + ("dom",), None),
+        P(mem + ("dom",)),
         P(),
         P(),
         P(),
     )
-    out_specs = P(("mem", "dom"), None)
-    return jax.shard_map(body, mesh=mesh, in_specs=in_specs, out_specs=out_specs, check_vma=False)
+    out_specs = P(mem + ("dom",), None)
+    return jax.shard_map(body, mesh=split, in_specs=in_specs, out_specs=out_specs, check_vma=False)

time: 92.5 us -> 96.5 us (1.043)
  the two profiles are of different devices: /device:TPU:57 before, /device:TPU:2 now
where the time goes in v8:
time: 96.5 us; the launch traced here: 96.1 us
  starting transfers between devices  42.1 us (44%)
  waiting for transfers between devices  37.3 us (39%)
  local copies, waits for them, and re-layouts  8.85 us (9%)
  matrix products  4.35 us (5%)
  other arithmetic  3.32 us (3%)
    all_to_all x1, starting transfers between devices, body(): arrived = lax.all_to_all(grid, ('pair', 'core', 'dom'), 0, 0, tiled=True)  21.2 us
    all_to_all x1, waiting for transfers between devices, body(): arrived = lax.all_to_all(grid, ('pair', 'core', 'dom'), 0, 0, tiled=True)  13.5 us
    ppermute x3, starting transfers between devices, from_behind(): return lax.ppermute(block, axis, route)  12.1 us
    all_to_all x1, waiting for transfers between devices, gathered(): return lax.all_to_all(copies, axis, 0, 0, tiled=True)  11.8 us
    ppermute x1, waiting for transfers between devices, body(): far = lax.ppermute(partner, ('pair', 'core'), route)  9.52 us
    all_to_all x1, starting transfers between devices, gathered(): return lax.all_to_all(copies, axis, 0, 0, tiled=True)  6.1 us
    reshape x1, local copies, waits for them, and re-layouts, body(): grid = fcst_pert.reshape(leads, regions, pair, column_blocks, width)  3.07 us
    ppermute x1, starting transfers between devices, body(): far = lax.ppermute(partner, ('pair', 'core'), route)  2.73 us
  transfers between devices with their start and end apart: 6, of which 4 were waited for; matrix products, arithmetic and copies ran while one was open for 7% of the time, Pallas kernels for 0%

profile of v8, /device:TPU:2, one launch (start us, length us, event | category | flops | bytes accessed | tf_op | source)
XLA Modules:
  0.0 96.1 jit_solution(14301002507924608998)
XLA Ops:
  0.0 0.0 copy-start
  0.0 0.0 copy-start.1
  0.0 0.0 copy-start.2
  0.0 0.0 copy-start.3
  0.0 3.1 %copy.33 = f32[2,4,2,128,128]{4,2,0,1,3:T(2,128)} copy(f32[2,4,2,128,128]{4,3,2,1,0:T(8,128)} %bitcast.47) | data formatting | bytes 2097152 | tf_op jit(solution)/shard_map/reshape | solution.py:55
  3.1 21.2 %all-to-all-start = ((f32[512,1,512]{2,1,0:T(1,128)}), f32[512,1,512]{2,1,0:T(1,128)S(1)}, u32[]{:S(2)}, u32[]{:S(2)}) async-start(f32[512,1,512]{2,1,0:T(1,128)} %bitcast.12), calls=%async_computation | async-start | bytes 2097152 | tf_op jit(solution)/shard_map/all_to_all | solution.py:57
  24.3 0.0 copy-done.1
  24.3 3.4 %collective-permute-start = (f32[2,64,128]{2,1,0:T(8,128)S(1)}, f32[2,64,128]{2,1,0:T(8,128)S(1)}, u32[]{:S(2)}, u32[]{:S(2)}) collective-permute-start(f32[2,64,128]{2,1,0:T(8,128)S(1)} %bitcast.48), channel_id=1, source_target_pairs={{3,0},{0,1},{1,2},{2,3},{7,4},{4,5},{5,6},{6,7},{11,8},{8,9},{9,10... | collective-permute-start | bytes 196616 | tf_op jit(solution)/shard_map/ppermute | solution.py:14
  27.7 6.8 %collective-permute-start.1 = (f32[2,64,128]{2,1,0:T(8,128)S(1)}, f32[2,64,128]{2,1,0:T(8,128)S(1)}, u32[]{:S(2)}, u32[]{:S(2)}) collective-permute-start(f32[2,64,128]{2,1,0:T(8,128)S(1)} %bitcast.49), channel_id=1, source_target_pairs={{2,0},{3,1},{0,2},{1,3},{6,4},{7,5},{4,6},{5,7},{10,8},{11,9},{8,1... | collective-permute-start | bytes 196616 | tf_op jit(solution)/shard_map/ppermute | solution.py:14
  34.5 1.9 %collective-permute-start.2 = (f32[2,64,128]{2,1,0:T(8,128)S(1)}, f32[2,64,128]{2,1,0:T(8,128)S(1)}, u32[]{:S(2)}, u32[]{:S(2)}) collective-permute-start(f32[2,64,128]{2,1,0:T(8,128)S(1)} %bitcast.50), channel_id=1, source_target_pairs={{1,0},{2,1},{3,2},{0,3},{5,4},{6,5},{7,6},{4,7},{9,8},{10,9},{11,1... | collective-permute-start | bytes 196616 | tf_op jit(solution)/shard_map/ppermute | solution.py:14
  36.4 0.0 copy-done.2
  36.4 0.1 copy.31
  36.5 0.0 copy-done.3
  36.6 0.1 copy.32
  36.7 0.6 gather_fusion
  37.2 0.6 gather_fusion.2
  37.8 0.0 copy-done
  37.8 0.6 gather_fusion.1
  38.5 0.0 collective-permute-done
  38.5 0.0 collective-permute-done.1
  38.5 2.5 %collective-permute-done.2 = f32[2,64,128]{2,1,0:T(8,128)S(1)} collective-permute-done((f32[2,64,128]{2,1,0:T(8,128)S(1)}, f32[2,64,128]{2,1,0:T(8,128)S(1)}, u32[]{:S(2)}, u32[]{:S(2)}) %collective-permute-start.2) | collective-permute-done | bytes 65568 | tf_op jit(solution)/shard_map/ppermute | solution.py:14
  41.1 0.0 copy-start.4
  41.1 0.7 scatter_fusion
  41.8 13.5 %all-to-all-done = f32[512,1,512]{2,1,0:T(1,128)S(1)} async-done(((f32[512,1,512]{2,1,0:T(1,128)}), f32[512,1,512]{2,1,0:T(1,128)S(1)}, u32[]{:S(2)}, u32[]{:S(2)}) %all-to-all-start) | async-done | bytes 1048608 | tf_op jit(solution)/shard_map/all_to_all | solution.py:57
  55.2 0.8 convolution_bitcast_fusion
  56.1 0.2 copy.37
  56.3 0.2 broadcast_in_dim.17
  56.4 1.1 %broadcast_in_dim.22 = f32[8,256,128]{2,1,0:T(8,128)} broadcast(f32[256,128]{1,0:T(8,128)S(1)} %broadcast_in_dim.17), dimensions={1,2} | broadcast | bytes 1179648 | tf_op jit(solution)/shard_map/broadcast_in_dim | solution.py:19
  57.5 6.1 %all-to-all-start.1 = ((f32[8,256,128]{2,1,0:T(8,128)}), f32[8,256,128]{2,1,0:T(8,128)}, u32[]{:S(2)}, u32[]{:S(2)}) async-start(f32[8,256,128]{2,1,0:T(8,128)} %broadcast_in_dim.22), calls=%async_computation.1 | async-start | bytes 2097152 | tf_op jit(solution)/shard_map/all_to_all | solution.py:20
  63.6 0.1 iota_compare_fusion
  63.7 0.2 select_reduce_fusion
  63.9 0.0 copy-done.4
  63.9 2.2 %broadcast_multiply_fusion = f32[768,1024]{1,0:T(8,128)S(1)} fusion(f32[768,1024]{1,0:T(8,128)} %param.9, f32[768]{0:T(1024)S(1)} %broadcast_multiply_fusion.1), kind=kLoop, calls=%fused_computation.12 | loop fusion | flops 786432 | bytes 6294528 | tf_op jit(solution)/shard_map/mul | solution.py:84
  66.0 11.8 %all-to-all-done.1 = f32[8,256,128]{2,1,0:T(8,128)} async-done(((f32[8,256,128]{2,1,0:T(8,128)}), f32[8,256,128]{2,1,0:T(8,128)}, u32[]{:S(2)}, u32[]{:S(2)}) %all-to-all-start.1) | async-done | bytes 1048608 | tf_op jit(solution)/shard_map/all_to_all | solution.py:20
  77.8 1.6 %copy.38 = f32[2,128,4,2,128]{4,3,2,1,0:T(2,128)S(1)} copy(f32[2,128,4,2,128]{4,3,1,2,0:T(2,128)} %bitcast.18) | data formatting | bytes 2097152 | tf_op jit(solution)/shard_map/transpose | solution.py:64
  79.4 0.1 dynamic-slice_bitcast_fusion.1
  79.5 2.7 %collective-permute-start.3 = (f32[1024,128]{1,0:T(8,128)S(1)}, f32[1024,128]{1,0:T(8,128)S(1)}, u32[]{:S(2)}, u32[]{:S(2)}) collective-permute-start(f32[1024,128]{1,0:T(8,128)S(1)} %get-tuple-element.6), channel_id=1, source_target_pairs={{0,8},{4,508},{8,16},{12,4},{16,24},{20,12},{24,32},{28,20},{32,40... | collective-permute-start | bytes 1572872 | tf_op jit(solution)/shard_map/ppermute | solution.py:76
  82.2 2.1 %fusion = f32[6,128,128]{2,1,0:T(8,128)S(1)} fusion(f32[6,128,1024]{2,1,0:T(8,128)S(1)} %bitcast.43, f32[1024,128]{1,0:T(8,128)S(1)} %get-tuple-element.6, f32[6]{0:T(128)S(1)} %get-tuple-element.9, f32[1024,128]{1,0:T(8,128)S(1)} %get-tuple-element.5, f32[6]{0:T(128)S(1)} %get-tuple-element.8), kind=kOutput, calls=%fused_computation.4 | convolution fusion | flops 606339072 | bytes 4587568 | tf_op jit(solution)/shard_map/irk,ikt->irt/dot_general | solution.py:87
  84.3 9.5 %collective-permute-done.3 = f32[1024,128]{1,0:T(8,128)S(1)} collective-permute-done((f32[1024,128]{1,0:T(8,128)S(1)}, f32[1024,128]{1,0:T(8,128)S(1)}, u32[]{:S(2)}, u32[]{:S(2)}) %collective-permute-start.3) | collective-permute-done | bytes 524320 | tf_op jit(solution)/shard_map/ppermute | solution.py:76
  93.9 1.4 %fusion.16 = f32[768,128]{1,0:T(8,128)S(1)} fusion(f32[768,1024]{1,0:T(8,128)S(1)} %broadcast_multiply_fusion, f32[1024,128]{1,0:T(8,128)S(1)} %collective-permute-done.3), kind=kOutput, calls=%fused_computation.42 | convolution fusion | flops 603979776 | bytes 4063232 | tf_op jit(solution)/shard_map/dot_general | solution.py:88
  95.3 0.9 multiply_add_fusion
  (8 shorter events, 0.1 us)
Async XLA Ops:
  0.0 37.8 %copy-start = (s32[128]{0:T(128)S(1)}, s32[128]{0:T(128)}, u32[]{:S(2)}) copy-start(s32[128]{0:T(128)} %param.13) | copy-start | bytes 1540
  0.0 24.3 %copy-start.1 = (f32[2,64,1,128]{3,2,1,0:T(1,128)S(1)}, f32[2,64,1,128]{3,2,1,0:T(1,128)}, u32[]{:S(2)}) copy-start(f32[2,64,1,128]{3,2,1,0:T(1,128)} %param.8) | copy-start | bytes 196612
  0.0 36.4 %copy-start.2 = (s32[128,16]{0,1:T(8,128)S(1)}, s32[128,16]{0,1:T(8,128)}, u32[]{:S(2)}) copy-start(s32[128,16]{0,1:T(8,128)} %param.11) | copy-start | bytes 24580
  0.0 36.5 %copy-start.3 = (f32[128,16]{0,1:T(8,128)S(1)}, f32[128,16]{0,1:T(8,128)}, u32[]{:S(2)}) copy-start(f32[128,16]{0,1:T(8,128)} %param.12) | copy-start | bytes 24580
  3.1 52.1 %all-to-all-start = ((f32[512,1,512]{2,1,0:T(1,128)}), f32[512,1,512]{2,1,0:T(1,128)S(1)}, u32[]{:S(2)}, u32[]{:S(2)}) async-start(f32[512,1,512]{2,1,0:T(1,128)} %bitcast.12), calls=%async_computation | async-start | bytes 2097152 | tf_op jit(solution)/shard_map/all_to_all | solution.py:57
  24.3 14.2 %collective-permute-start = (f32[2,64,128]{2,1,0:T(8,128)S(1)}, f32[2,64,128]{2,1,0:T(8,128)S(1)}, u32[]{:S(2)}, u32[]{:S(2)}) collective-permute-start(f32[2,64,128]{2,1,0:T(8,128)S(1)} %bitcast.48), channel_id=1, source_target_pairs={{3,0},{0,1},{1,2},{2,3},{7,4},{4,5},{5,6},{6,7},{11,8},{8,9},{9,10... | collective-permute-start | bytes 196616 | tf_op jit(solution)/shard_map/ppermute | solution.py:14
  27.7 10.8 %collective-permute-start.1 = (f32[2,64,128]{2,1,0:T(8,128)S(1)}, f32[2,64,128]{2,1,0:T(8,128)S(1)}, u32[]{:S(2)}, u32[]{:S(2)}) collective-permute-start(f32[2,64,128]{2,1,0:T(8,128)S(1)} %bitcast.49), channel_id=1, source_target_pairs={{2,0},{3,1},{0,2},{1,3},{6,4},{7,5},{4,6},{5,7},{10,8},{11,9},{8,1... | collective-permute-start | bytes 196616 | tf_op jit(solution)/shard_map/ppermute | solution.py:14
  34.5 6.5 %collective-permute-start.2 = (f32[2,64,128]{2,1,0:T(8,128)S(1)}, f32[2,64,128]{2,1,0:T(8,128)S(1)}, u32[]{:S(2)}, u32[]{:S(2)}) collective-permute-start(f32[2,64,128]{2,1,0:T(8,128)S(1)} %bitcast.50), channel_id=1, source_target_pairs={{1,0},{2,1},{3,2},{0,3},{5,4},{6,5},{7,6},{4,7},{9,8},{10,9},{11,1... | collective-permute-start | bytes 196616 | tf_op jit(solution)/shard_map/ppermute | solution.py:14
  41.1 22.8 %copy-start.4 = (f32[768]{0:T(1024)S(1)}, f32[768]{0:T(1024)}, u32[]{:S(2)}) copy-start(f32[768]{0:T(1024)} %param.10) | copy-start | bytes 9220
  57.5 20.3 %all-to-all-start.1 = ((f32[8,256,128]{2,1,0:T(8,128)}), f32[8,256,128]{2,1,0:T(8,128)}, u32[]{:S(2)}, u32[]{:S(2)}) async-start(f32[8,256,128]{2,1,0:T(8,128)} %broadcast_in_dim.22), calls=%async_computation.1 | async-start | bytes 2097152 | tf_op jit(solution)/shard_map/all_to_all | solution.py:20
  79.5 14.4 %collective-permute-start.3 = (f32[1024,128]{1,0:T(8,128)S(1)}, f32[1024,128]{1,0:T(8,128)S(1)}, u32[]{:S(2)}, u32[]{:S(2)}) collective-permute-start(f32[1024,128]{1,0:T(8,128)S(1)} %get-tuple-element.6), channel_id=1, source_target_pairs={{0,8},{4,508},{8,16},{12,4},{16,24},{20,12},{24,32},{28,20},{32,40... | collective-permute-start | bytes 1572872 | tf_op jit(solution)/shard_map/ppermute | solution.py:76

commit v9 on v7

--- a/solution.py
+++ b/solution.py
@@ -72,12 +72,10 @@
     )
     scale = (weighted_innovation / (M - 1))[:, None]
     rows = obs_pert * scale
-    own = jnp.dot(rows, summed, precision=HIGH).reshape(owned_blocks, OBSB, -1)
-    rows = rows.reshape(owned_blocks, OBSB, -1)
-    others = weight_rows[0][:, None, None] * behind[None] + weight_rows[2][:, None, None] * ahead[None]
-    result = own * weight_rows[1][:, None, None] + jnp.einsum(
-        "irk,ikt->irt", rows, others, precision=HIGH
-    )
+    result = 0
+    for source, weights in zip((behind, summed, ahead), weight_rows):
+        product = jnp.dot(rows, source, precision=HIGH).reshape(owned_blocks, OBSB, -1)
+        result = result + product * weights[:, None, None]
     return result.reshape(owned_rows, -1)
 
 

time: 92.5 us -> 91.9 us (level)
  waiting for transfers between devices: 34.9 us -> 32.3 us
  starting transfers between devices: 41.3 us -> 42.5 us
    ppermute x5, waiting for transfers between devices: 13.5 us -> 8.57 us  [from_behind(): return lax.ppermute(block, axis, route)]
    all_to_all x1, waiting for transfers between devices: 13.9 us -> 16.2 us  [body(): arrived = lax.all_to_all(grid, ('mem', 'dom'), 0, 0, tiled=True)]
    ppermute x5, starting transfers between devices: 16.1 us -> 17.3 us  [from_behind(): return lax.ppermute(block, axis, route)]
    dot_general x2 -> x3, matrix products: 4.23 us -> 4.17 us  [body(): jnp.dot(rows, source, precision=HIGH).reshape(owned_blocks, OBSB, -1)]
  transfers between devices with their start and end apart: 7 -> 7, of which waited for: 6 -> 5; matrix products, arithmetic and copies ran while one was open for 7% -> 9% of each run, Pallas kernels for 0% -> 0%
where the time goes in v9:
time: 91.9 us; the launch traced here: 91.5 us
  starting transfers between devices  42.5 us (46%)
  waiting for transfers between devices  32.3 us (35%)
  local copies, waits for them, and re-layouts  8.13 us (9%)
  matrix products  5.02 us (5%)
  other arithmetic  3.33 us (4%)
    all_to_all x1, starting transfers between devices, body(): arrived = lax.all_to_all(grid, ('mem', 'dom'), 0, 0, tiled=True)  21.1 us
    ppermute x5, starting transfers between devices, from_behind(): return lax.ppermute(block, axis, route)  17.3 us
    all_to_all x1, waiting for transfers between devices, body(): arrived = lax.all_to_all(grid, ('mem', 'dom'), 0, 0, tiled=True)  16.2 us
    ppermute x5, waiting for transfers between devices, from_behind(): return lax.ppermute(block, axis, route)  8.57 us
    all_to_all x1, waiting for transfers between devices, gathered(): return lax.all_to_all(copies, axis, 0, 0, tiled=True)  7.52 us
    dot_general x3, matrix products, body(): jnp.dot(rows, source, precision=HIGH).reshape(owned_blocks, OBSB, -1)  4.17 us
    all_to_all x1, starting transfers between devices, gathered(): return lax.all_to_all(copies, axis, 0, 0, tiled=True)  4.13 us
    reshape x1, local copies, waits for them, and re-layouts, body(): grid = fcst_pert.reshape(leads, regions, pair, column_blocks, width)  3.06 us
  transfers between devices with their start and end apart: 7, of which 5 were waited for; matrix products, arithmetic and copies ran while one was open for 9% of the time, Pallas kernels for 0%

profile of v9, /device:TPU:57, one launch (start us, length us, event | category | flops | bytes accessed | tf_op | source)
XLA Modules:
  0.0 91.5 jit_solution(3310734836382819400)
XLA Ops:
  0.0 0.0 copy-start
  0.0 0.0 copy-start.1
  0.0 0.0 copy-start.2
  0.0 0.0 copy-start.3
  0.0 0.0 copy-start.4
  0.0 3.1 %copy.25 = f32[2,4,2,128,128]{4,2,0,1,3:T(2,128)} copy(f32[2,4,2,128,128]{4,3,2,1,0:T(8,128)} %bitcast.52) | data formatting | bytes 2097152 | tf_op jit(solution)/shard_map/reshape | solution.py:54
  3.1 21.1 %all-to-all-start = ((f32[512,1,512]{2,1,0:T(1,128)}), f32[512,1,512]{2,1,0:T(1,128)S(1)}, u32[]{:S(2)}, u32[]{:S(2)}) async-start(f32[512,1,512]{2,1,0:T(1,128)} %bitcast.9), calls=%async_computation | async-start | bytes 2097152 | tf_op jit(solution)/shard_map/all_to_all | solution.py:56
  24.2 0.0 copy-done.1
  24.2 3.1 %collective-permute-start = (f32[2,64,128]{2,1,0:T(8,128)S(1)}, f32[2,64,128]{2,1,0:T(8,128)S(1)}, u32[]{:S(2)}, u32[]{:S(2)}) collective-permute-start(f32[2,64,128]{2,1,0:T(8,128)S(1)} %bitcast.53), channel_id=1, source_target_pairs={{3,0},{0,1},{1,2},{2,3},{7,4},{4,5},{5,6},{6,7},{11,8},{8,9},{9,10... | collective-permute-start | bytes 196616 | tf_op jit(solution)/shard_map/ppermute | solution.py:14
  27.3 4.3 %collective-permute-start.1 = (f32[2,64,128]{2,1,0:T(8,128)S(1)}, f32[2,64,128]{2,1,0:T(8,128)S(1)}, u32[]{:S(2)}, u32[]{:S(2)}) collective-permute-start(f32[2,64,128]{2,1,0:T(8,128)S(1)} %bitcast.54), channel_id=1, source_target_pairs={{2,0},{3,1},{0,2},{1,3},{6,4},{7,5},{4,6},{5,7},{10,8},{11,9},{8,1... | collective-permute-start | bytes 196616 | tf_op jit(solution)/shard_map/ppermute | solution.py:14
  31.6 3.1 %collective-permute-start.2 = (f32[2,64,128]{2,1,0:T(8,128)S(1)}, f32[2,64,128]{2,1,0:T(8,128)S(1)}, u32[]{:S(2)}, u32[]{:S(2)}) collective-permute-start(f32[2,64,128]{2,1,0:T(8,128)S(1)} %bitcast.55), channel_id=1, source_target_pairs={{1,0},{2,1},{3,2},{0,3},{5,4},{6,5},{7,6},{4,7},{9,8},{10,9},{11,1... | collective-permute-start | bytes 196616 | tf_op jit(solution)/shard_map/ppermute | solution.py:14
  34.7 0.0 copy-done.2
  34.7 0.1 copy.31
  34.8 0.0 copy-done.3
  34.8 0.1 copy.32
  35.0 0.6 gather_fusion
  35.5 0.6 gather_fusion.2
  36.1 0.0 copy-done
  36.1 0.6 gather_fusion.1
  36.7 0.1 iota_compare_fusion
  36.8 0.0 copy-done.4
  36.8 0.0 collective-permute-done
  36.8 0.0 collective-permute-done.1
  36.8 0.7 collective-permute-done.2
  37.6 0.7 scatter_fusion
  38.2 16.2 %all-to-all-done = f32[512,1,512]{2,1,0:T(1,128)S(1)} async-done(((f32[512,1,512]{2,1,0:T(1,128)}), f32[512,1,512]{2,1,0:T(1,128)S(1)}, u32[]{:S(2)}, u32[]{:S(2)}) %all-to-all-start) | async-done | bytes 1048608 | tf_op jit(solution)/shard_map/all_to_all | solution.py:56
  54.5 0.8 convolution_bitcast_fusion
  55.3 0.2 copy.29
  55.5 0.2 broadcast_in_dim.15
  55.7 0.8 broadcast_in_dim.16
  56.5 4.1 %all-to-all-start.1 = ((f32[4,256,128]{2,1,0:T(8,128)}), f32[4,256,128]{2,1,0:T(8,128)}, u32[]{:S(2)}, u32[]{:S(2)}) async-start(f32[4,256,128]{2,1,0:T(8,128)} %broadcast_in_dim.16), calls=%async_computation.1 | async-start | bytes 1048576 | tf_op jit(solution)/shard_map/all_to_all | solution.py:20
  60.7 0.2 select_reduce_fusion
  60.8 2.2 %broadcast_multiply_fusion = f32[768,1024]{1,0:T(8,128)S(1)} fusion(f32[768,1024]{1,0:T(8,128)} %param.9, f32[768]{0:T(1024)S(1)} %broadcast_multiply_fusion.1), kind=kLoop, calls=%fused_computation.4 | loop fusion | flops 786432 | bytes 6294528 | tf_op jit(solution)/shard_map/mul | solution.py:74
  63.0 7.5 %all-to-all-done.1 = f32[4,256,128]{2,1,0:T(8,128)} async-done(((f32[4,256,128]{2,1,0:T(8,128)}), f32[4,256,128]{2,1,0:T(8,128)}, u32[]{:S(2)}, u32[]{:S(2)}) %all-to-all-start.1) | async-done | bytes 524320 | tf_op jit(solution)/shard_map/all_to_all | solution.py:20
  70.5 1.2 %copy.30 = f32[128,4,2,128]{3,2,1,0:T(2,128)S(1)} copy(f32[128,4,2,128]{3,2,0,1:T(2,128)} %bitcast.15) | data formatting | bytes 1048576 | tf_op jit(solution)/shard_map/transpose | solution.py:63
  71.7 4.9 %collective-permute-start.3 = (f32[1024,128]{1,0:T(8,128)S(1)}, f32[1024,128]{1,0:T(8,128)S(1)}, u32[]{:S(2)}, u32[]{:S(2)}) collective-permute-start(f32[1024,128]{1,0:T(8,128)S(1)} %bitcast.47), channel_id=1, source_target_pairs={{508,0},{0,4},{4,8},{8,12},{12,16},{16,20},{20,24},{24,28},{28,32}... | collective-permute-start | bytes 1572872 | tf_op jit(solution)/shard_map/ppermute | solution.py:14
  76.6 1.9 %collective-permute-start.4 = (f32[1024,128]{1,0:T(8,128)S(1)}, f32[1024,128]{1,0:T(8,128)S(1)}, u32[]{:S(2)}, u32[]{:S(2)}) collective-permute-start(f32[1024,128]{1,0:T(8,128)S(1)} %bitcast.48), channel_id=1, source_target_pairs={{4,0},{8,4},{12,8},{16,12},{20,16},{24,20},{28,24},{32,28},{36,32}... | collective-permute-start | bytes 1572872 | tf_op jit(solution)/shard_map/ppermute | solution.py:14
  78.5 1.4 %convolution_multiply_fusion = f32[6,128,128]{2,1,0:T(8,128)S(1)} fusion(f32[6,128,1024]{2,1,0:T(8,128)S(1)} %bitcast.45, f32[1024,128,1]{1,0,2:T(8,128)S(1)} %bitcast.49, f32[6]{0:T(128)S(1)} %get-tuple-element.7), kind=kOutput, calls=%fused_computation.5 | convolution fusion | flops 604078080 | bytes 4063256 | tf_op jit(solution)/shard_map/dot_general | solution.py:77
  79.9 2.8 %collective-permute-done.3 = f32[1024,128]{1,0:T(8,128)S(1)} collective-permute-done((f32[1024,128]{1,0:T(8,128)S(1)}, f32[1024,128]{1,0:T(8,128)S(1)}, u32[]{:S(2)}, u32[]{:S(2)}) %collective-permute-start.3) | collective-permute-done | bytes 524320 | tf_op jit(solution)/shard_map/ppermute | solution.py:14
  82.7 1.4 %fusion.6 = f32[768,128]{1,0:T(8,128)S(1)} fusion(f32[768,1024]{1,0:T(8,128)S(1)} %broadcast_multiply_fusion, f32[1024,128]{1,0:T(8,128)S(1)} %collective-permute-done.3), kind=kOutput, calls=%fused_computation.31 | convolution fusion | flops 603979776 | bytes 4063232 | tf_op jit(solution)/shard_map/dot_general | solution.py:77
  84.1 5.1 %collective-permute-done.4 = f32[1024,128]{1,0:T(8,128)S(1)} collective-permute-done((f32[1024,128]{1,0:T(8,128)S(1)}, f32[1024,128]{1,0:T(8,128)S(1)}, u32[]{:S(2)}, u32[]{:S(2)}) %collective-permute-start.4) | collective-permute-done | bytes 524320 | tf_op jit(solution)/shard_map/ppermute | solution.py:14
  89.2 1.4 %fusion.7 = f32[768,128]{1,0:T(8,128)S(1)} fusion(f32[768,1024]{1,0:T(8,128)S(1)} %broadcast_multiply_fusion, f32[1024,128]{1,0:T(8,128)S(1)} %collective-permute-done.4), kind=kOutput, calls=%fused_computation.32 | convolution fusion | flops 603979776 | bytes 4063232 | tf_op jit(solution)/shard_map/dot_general | solution.py:77
  90.6 0.9 multiply_add_fusion
  (8 shorter events, 0.1 us)
Async XLA Ops:
  0.0 36.1 %copy-start = (s32[128]{0:T(128)S(1)}, s32[128]{0:T(128)}, u32[]{:S(2)}) copy-start(s32[128]{0:T(128)} %param.13) | copy-start | bytes 1540
  0.0 24.2 %copy-start.1 = (f32[2,64,1,128]{3,2,1,0:T(1,128)S(1)}, f32[2,64,1,128]{3,2,1,0:T(1,128)}, u32[]{:S(2)}) copy-start(f32[2,64,1,128]{3,2,1,0:T(1,128)} %param.8) | copy-start | bytes 196612
  0.0 34.7 %copy-start.2 = (s32[128,16]{0,1:T(8,128)S(1)}, s32[128,16]{0,1:T(8,128)}, u32[]{:S(2)}) copy-start(s32[128,16]{0,1:T(8,128)} %param.11) | copy-start | bytes 24580
  0.0 34.8 %copy-start.3 = (f32[128,16]{0,1:T(8,128)S(1)}, f32[128,16]{0,1:T(8,128)}, u32[]{:S(2)}) copy-start(f32[128,16]{0,1:T(8,128)} %param.12) | copy-start | bytes 24580
  0.0 36.8 %copy-start.4 = (f32[768]{0:T(1024)S(1)}, f32[768]{0:T(1024)}, u32[]{:S(2)}) copy-start(f32[768]{0:T(1024)} %param.10) | copy-start | bytes 9220
  3.1 51.4 %all-to-all-start = ((f32[512,1,512]{2,1,0:T(1,128)}), f32[512,1,512]{2,1,0:T(1,128)S(1)}, u32[]{:S(2)}, u32[]{:S(2)}) async-start(f32[512,1,512]{2,1,0:T(1,128)} %bitcast.9), calls=%async_computation | async-start | bytes 2097152 | tf_op jit(solution)/shard_map/all_to_all | solution.py:56
  24.2 12.7 %collective-permute-start = (f32[2,64,128]{2,1,0:T(8,128)S(1)}, f32[2,64,128]{2,1,0:T(8,128)S(1)}, u32[]{:S(2)}, u32[]{:S(2)}) collective-permute-start(f32[2,64,128]{2,1,0:T(8,128)S(1)} %bitcast.53), channel_id=1, source_target_pairs={{3,0},{0,1},{1,2},{2,3},{7,4},{4,5},{5,6},{6,7},{11,8},{8,9},{9,10... | collective-permute-start | bytes 196616 | tf_op jit(solution)/shard_map/ppermute | solution.py:14
  27.3 9.6 %collective-permute-start.1 = (f32[2,64,128]{2,1,0:T(8,128)S(1)}, f32[2,64,128]{2,1,0:T(8,128)S(1)}, u32[]{:S(2)}, u32[]{:S(2)}) collective-permute-start(f32[2,64,128]{2,1,0:T(8,128)S(1)} %bitcast.54), channel_id=1, source_target_pairs={{2,0},{3,1},{0,2},{1,3},{6,4},{7,5},{4,6},{5,7},{10,8},{11,9},{8,1... | collective-permute-start | bytes 196616 | tf_op jit(solution)/shard_map/ppermute | solution.py:14
  31.6 5.9 %collective-permute-start.2 = (f32[2,64,128]{2,1,0:T(8,128)S(1)}, f32[2,64,128]{2,1,0:T(8,128)S(1)}, u32[]{:S(2)}, u32[]{:S(2)}) collective-permute-start(f32[2,64,128]{2,1,0:T(8,128)S(1)} %bitcast.55), channel_id=1, source_target_pairs={{1,0},{2,1},{3,2},{0,3},{5,4},{6,5},{7,6},{4,7},{9,8},{10,9},{11,1... | collective-permute-start | bytes 196616 | tf_op jit(solution)/shard_map/ppermute | solution.py:14
  56.5 14.0 %all-to-all-start.1 = ((f32[4,256,128]{2,1,0:T(8,128)}), f32[4,256,128]{2,1,0:T(8,128)}, u32[]{:S(2)}, u32[]{:S(2)}) async-start(f32[4,256,128]{2,1,0:T(8,128)} %broadcast_in_dim.16), calls=%async_computation.1 | async-start | bytes 1048576 | tf_op jit(solution)/shard_map/all_to_all | solution.py:20
  71.7 11.0 %collective-permute-start.3 = (f32[1024,128]{1,0:T(8,128)S(1)}, f32[1024,128]{1,0:T(8,128)S(1)}, u32[]{:S(2)}, u32[]{:S(2)}) collective-permute-start(f32[1024,128]{1,0:T(8,128)S(1)} %bitcast.47), channel_id=1, source_target_pairs={{508,0},{0,4},{4,8},{8,12},{12,16},{16,20},{20,24},{24,28},{28,32}... | collective-permute-start | bytes 1572872 | tf_op jit(solution)/shard_map/ppermute | solution.py:14
  76.6 12.6 %collective-permute-start.4 = (f32[1024,128]{1,0:T(8,128)S(1)}, f32[1024,128]{1,0:T(8,128)S(1)}, u32[]{:S(2)}, u32[]{:S(2)}) collective-permute-start(f32[1024,128]{1,0:T(8,128)S(1)} %bitcast.48), channel_id=1, source_target_pairs={{4,0},{8,4},{12,8},{16,12},{20,16},{24,20},{28,24},{32,28},{36,32}... | collective-permute-start | bytes 1572872 | tf_op jit(solution)/shard_map/ppermute | solution.py:14

commit v10 on v9

--- a/solution.py
+++ b/solution.py
@@ -59,8 +59,7 @@
     levels = shifted_copies(sensitivity[:, :, 0, :], "dom")
     quarter = jnp.einsum("mdljc,dltc->mjlt", arrived, levels, precision=HIGH)
     quarter = quarter.reshape(column_blocks * pair, leads * targets)
-    full = gathered(quarter, "dom").reshape(regions, column_blocks, pair, -1)
-    summed = jnp.transpose(full, (1, 0, 2, 3)).reshape(column_blocks * local_members, -1)
+    summed = gathered(quarter, "dom").reshape(column_blocks * local_members, -1)
     column_index = lax.axis_index("mem")
     region_index = lax.axis_index("dom")
     owned_rows = obs_pert.shape[0]
@@ -71,7 +70,8 @@
         obs_lists, block_taper, counts, column_index, region_index, owned_blocks, regions
     )
     scale = (weighted_innovation / (M - 1))[:, None]
-    rows = obs_pert * scale
+    rows = obs_pert.reshape(owned_rows, column_blocks, regions, pair)
+    rows = jnp.transpose(rows, (0, 2, 1, 3)).reshape(owned_rows, -1) * scale
     result = 0
     for source, weights in zip((behind, summed, ahead), weight_rows):
         product = jnp.dot(rows, source, precision=HIGH).reshape(owned_blocks, OBSB, -1)

time: 91.9 us -> 105 us (1.14)
  the two profiles are of different devices: /device:TPU:57 before, /device:TPU:2 now
where the time goes in v10:
time: 105 us; the launch traced here: 104 us
  starting transfers between devices  49.8 us (47%)
  local copies, waits for them, and re-layouts  38.8 us (37%)
  matrix products  10.5 us (10%)
  other arithmetic  4.49 us (4%)
    all_to_all x1, starting transfers between devices, body(): arrived = lax.all_to_all(grid, ('mem', 'dom'), 0, 0, tiled=True)  23.3 us
    ppermute x5, starting transfers between devices, from_behind(): return lax.ppermute(block, axis, route)  20.6 us
    mul x3, local copies, waits for them, and re-layouts, body(): rows = jnp.transpose(rows, (0, 2, 1, 3)).reshape(owned_rows, -1) * scale  11.8 us
    dot_general x3, matrix products, body(): jnp.dot(rows, source, precision=HIGH).reshape(owned_blocks, OBSB, -1)  8.47 us
    reshape x2, local copies, waits for them, and re-layouts, body(): rows = obs_pert.reshape(owned_rows, column_blocks, regions, pair)  7.17 us
    all_to_all x1, starting transfers between devices, gathered(): return lax.all_to_all(copies, axis, 0, 0, tiled=True)  5.95 us
    reshape x1, local copies, waits for them, and re-layouts, body(): rows = jnp.transpose(rows, (0, 2, 1, 3)).reshape(owned_rows, -1) * scale  5.48 us
    mul x3, other arithmetic, body(): rows = jnp.transpose(rows, (0, 2, 1, 3)).reshape(owned_rows, -1) * scale  4.2 us
  transfers between devices with their start and end apart: 7, of which 1 were waited for; matrix products, arithmetic and copies ran while one was open for 42% of the time, Pallas kernels for 0%

profile of v10, /device:TPU:2, one launch (start us, length us, event | category | flops | bytes accessed | tf_op | source)
XLA Modules:
  0.0 104.4 jit_solution(4710238377058378611)
XLA Ops:
  0.0 0.0 copy-start
  0.0 0.0 copy-start.2
  0.0 3.1 %copy.53 = f32[2,4,2,128,128]{4,2,0,1,3:T(2,128)} copy(f32[2,4,2,128,128]{4,3,2,1,0:T(8,128)} %bitcast.53) | data formatting | bytes 2097152 | tf_op jit(solution)/shard_map/reshape | solution.py:54
  3.1 23.3 %all-to-all-start = ((f32[512,1,512]{2,1,0:T(1,128)}), f32[512,1,512]{2,1,0:T(1,128)}, u32[]{:S(2)}, u32[]{:S(2)}) async-start(f32[512,1,512]{2,1,0:T(1,128)} %bitcast.11), calls=%async_computation | async-start | bytes 2097152 | tf_op jit(solution)/shard_map/all_to_all | solution.py:56
  26.4 0.0 copy-done.2
  26.4 6.3 %collective-permute-start.2 = (f32[2,64,128]{2,1,0:T(8,128)S(1)}, f32[2,64,128]{2,1,0:T(8,128)S(1)}, u32[]{:S(2)}, u32[]{:S(2)}) collective-permute-start(f32[2,64,128]{2,1,0:T(8,128)S(1)} %bitcast.54), channel_id=1, source_target_pairs={{1,0},{2,1},{3,2},{0,3},{5,4},{6,5},{7,6},{4,7},{9,8},{10,9},{11,1... | collective-permute-start | bytes 196616 | tf_op jit(solution)/shard_map/ppermute | solution.py:14
  32.7 1.9 %collective-permute-start.1 = (f32[2,64,128]{2,1,0:T(8,128)S(1)}, f32[2,64,128]{2,1,0:T(8,128)S(1)}, u32[]{:S(2)}, u32[]{:S(2)}) collective-permute-start(f32[2,64,128]{2,1,0:T(8,128)S(1)} %bitcast.55), channel_id=1, source_target_pairs={{2,0},{3,1},{0,2},{1,3},{6,4},{7,5},{4,6},{5,7},{10,8},{11,9},{8,1... | collective-permute-start | bytes 196616 | tf_op jit(solution)/shard_map/ppermute | solution.py:14
  34.6 3.4 %collective-permute-start = (f32[2,64,128]{2,1,0:T(8,128)S(1)}, f32[2,64,128]{2,1,0:T(8,128)S(1)}, u32[]{:S(2)}, u32[]{:S(2)}) collective-permute-start(f32[2,64,128]{2,1,0:T(8,128)S(1)} %bitcast.56), channel_id=1, source_target_pairs={{3,0},{0,1},{1,2},{2,3},{7,4},{4,5},{5,6},{6,7},{11,8},{8,9},{9,10... | collective-permute-start | bytes 196616 | tf_op jit(solution)/shard_map/ppermute | solution.py:14
  38.0 2.4 %copy.50 = f32[768,1024]{0,1:T(8,128)S(1)} copy(f32[768,1024]{1,0:T(8,128)} %param.9) | data formatting | bytes 6291456 | tf_op args[2]
  40.4 3.0 %reshape.177 = f32[768,128,4,2]{0,3,2,1:T(2,128)} reshape(f32[768,1024]{0,1:T(8,128)S(1)} %copy.50) | data formatting | bytes 6291456 | tf_op jit(solution)/shard_map/reshape | solution.py:73
  43.5 4.1 %copy.51 = f32[768,128,4,2]{1,0,3,2:T(8,128)S(1)} copy(f32[768,128,4,2]{0,3,2,1:T(2,128)} %reshape.177) | data formatting | bytes 6291456 | tf_op jit(solution)/shard_map/reshape | solution.py:73
  47.6 3.6 %copy.52 = f32[768,4,128,2]{0,3,2,1:T(2,128)} copy(f32[768,4,128,2]{2,0,3,1:T(8,128)S(1)} %bitcast.52) | data formatting | bytes 6291456 | tf_op jit(solution)/shard_map/transpose | solution.py:74
  51.1 0.0 copy-start.5
  51.1 5.5 %reshape.178 = f32[6,128,1024]{1,0,2:T(8,128)} reshape(f32[768,4,128,2]{0,3,2,1:T(2,128)} %copy.52) | data formatting | bytes 6291456 | tf_op jit(solution)/shard_map/reshape | solution.py:74
  56.7 0.0 copy-done.5
  56.7 0.0 copy-start.1
  56.7 2.0 %broadcast_multiply_fusion.1 = f32[768,4,128,2]{2,0,3,1:T(8,128)} fusion(f32[768]{0:T(1024)S(1)} %get-tuple-element.6, f32[768,128,4,2]{1,0,3,2:T(8,128)S(1)} %copy.51), kind=kLoop, calls=%fused_computation.7 | loop fusion | flops 786432 | bytes 6294528 | tf_op jit(solution)/shard_map/mul | solution.py:74
  58.7 1.3 %copy-done.1 = f32[6,128,1024]{1,0,2:T(8,128)S(1)} copy-done((f32[6,128,1024]{1,0,2:T(8,128)S(1)}, f32[6,128,1024]{1,0,2:T(8,128)}, u32[]{:S(2)}) %copy-start.1) | copy-done | bytes 3145752
  60.0 2.2 %broadcast_multiply_fusion = f32[6,128,1024]{1,0,2:T(8,128)} fusion(f32[6,128,1024]{1,0,2:T(8,128)S(1)} %copy-done.1, f32[6,128]{1,0:T(8,128)S(1)} %get-tuple-element.5), kind=kLoop, calls=%fused_computation.6 | loop fusion | flops 786432 | bytes 6294528 | tf_op jit(solution)/shard_map/mul | solution.py:74
  62.2 0.0 collective-permute-done.2
  62.3 0.0 collective-permute-done.1
  62.3 0.0 collective-permute-done
  62.3 0.7 scatter_fusion
  63.0 0.0 all-to-all-done
  63.0 2.1 %convolution_bitcast_fusion = f32[128,2,2,64]{0,3,1,2:T(8,128)S(1)} fusion(f32[128,4,2,2,128]{4,3,2,1,0:T(2,128)} %bitcast.12, f32[4,2,64,128]{3,2,1,0:T(8,128)S(1)} %scatter_fusion), kind=kOutput, calls=%fused_computation.13 | convolution fusion | flops 100663296 | bytes 1441792 | tf_op jit(solution)/shard_map/mdljc,dltc->mjlt/dot_general | solution.py:60
  65.1 0.2 copy.57
  65.3 0.2 broadcast_in_dim.15
  65.5 0.9 broadcast_in_dim.16
  66.3 6.0 %all-to-all-start.1 = ((f32[4,256,128]{2,1,0:T(8,128)}), f32[4,256,128]{2,1,0:T(8,128)}, u32[]{:S(2)}, u32[]{:S(2)}) async-start(f32[4,256,128]{2,1,0:T(8,128)} %broadcast_in_dim.16), calls=%async_computation.1 | async-start | bytes 1048576 | tf_op jit(solution)/shard_map/all_to_all | solution.py:20
  72.3 4.3 %copy.61 = f32[768,4,128,2]{0,3,2,1:T(2,128)S(1)} copy(f32[768,4,128,2]{2,0,3,1:T(8,128)} %broadcast_multiply_fusion.1) | data formatting | bytes 6291456 | tf_op jit(solution)/shard_map/mul | solution.py:74
  76.6 0.0 copy-start.3
  76.6 0.0 copy-start.4
  76.6 3.9 %mul.66 = f32[6,128,1024]{1,0,2:T(8,128)} reshape(f32[768,4,128,2]{0,3,2,1:T(2,128)S(1)} %copy.61) | data formatting | bytes 6291456 | tf_op jit(solution)/shard_map/mul | solution.py:74
  80.5 0.0 copy-done.3
  80.5 0.1 copy.60
  80.6 0.0 copy-done.4
  80.6 0.1 copy.59
  80.7 0.6 gather_fusion.2
  81.2 0.6 gather_fusion
  81.8 0.0 copy-done
  81.8 0.6 gather_fusion.1
  82.4 3.7 %copy.58 = f32[6,128,1024]{2,1,0:T(8,128)S(1)} copy(f32[6,128,1024]{1,0,2:T(8,128)} %broadcast_multiply_fusion) | data formatting | bytes 6291456 | tf_op jit(solution)/shard_map/mul | solution.py:74
  86.1 0.1 iota_compare_fusion
  86.2 0.2 select_reduce_fusion
  86.4 0.0 all-to-all-done.1
  86.4 1.9 %collective-permute-start.3 = (f32[1024,128]{1,0:T(8,128)}, f32[1024,128]{1,0:T(8,128)S(1)}, u32[]{:S(2)}, u32[]{:S(2)}) collective-permute-start(f32[1024,128]{1,0:T(8,128)} %bitcast.16), channel_id=1, source_target_pairs={{508,0},{0,4},{4,8},{8,12},{12,16},{16,20},{20,24},{24,28},{28,32}... | collective-permute-start | bytes 1572872 | tf_op jit(solution)/shard_map/ppermute | solution.py:14
  88.3 7.1 %collective-permute-start.4 = (f32[1024,128]{1,0:T(8,128)}, f32[1024,128]{1,0:T(8,128)S(1)}, u32[]{:S(2)}, u32[]{:S(2)}) collective-permute-start(f32[1024,128]{1,0:T(8,128)} %bitcast.16), channel_id=1, source_target_pairs={{4,0},{8,4},{12,8},{16,12},{20,16},{24,20},{28,24},{32,28},{36,32}... | collective-permute-start | bytes 1572872 | tf_op jit(solution)/shard_map/ppermute | solution.py:14
  95.4 4.9 %fusion.2 = f32[6,128,128]{2,1,0:T(8,128)S(1)} fusion(f32[1024,128,1]{1,0,2:T(8,128)} %bitcast.20, f32[6,128,1024]{1,0,2:T(8,128)} %mul.66, f32[6]{0:T(128)S(1)} %get-tuple-element.8), kind=kOutput, calls=%fused_computation.8 | convolution fusion | flops 604078080 | bytes 4063256 | tf_op jit(solution)/shard_map/dot_general | solution.py:77
  100.4 0.0 collective-permute-done.3
  100.4 1.4 %fusion.6 = f32[6,128,128]{2,1,0:T(8,128)S(1)} fusion(f32[6,128,128]{2,1,0:T(8,128)S(1)} %fusion.2, f32[6,128,1024]{2,1,0:T(8,128)S(1)} %copy.58, f32[1024,128]{1,0:T(8,128)S(1)} %collective-permute-done.3, f32[6]{0:T(128)S(1)} %get-tuple-element.9), kind=kOutput, calls=%fused_computation.12 | convolution fusion | flops 604176384 | bytes 4456472 | tf_op jit(solution)/shard_map/dot_general | solution.py:77
  101.8 0.5 collective-permute-done.4
  102.2 2.1 %fusion.5 = f32[6,128,128]{2,1,0:T(8,128)} fusion(f32[6,128,128]{2,1,0:T(8,128)S(1)} %fusion.6, f32[6,128,1024]{2,1,0:T(8,128)S(1)} %copy.58, f32[1024,128]{1,0:T(8,128)S(1)} %collective-permute-done.4, f32[6]{0:T(128)S(1)} %get-tuple-element.7), kind=kOutput, calls=%fused_computation.10 | convolution fusion | flops 604176384 | bytes 4456472 | tf_op jit(solution)/shard_map/dot_general | solution.py:77
  (8 shorter events, 0.1 us)
Async XLA Ops:
  0.0 81.8 %copy-start = (s32[128]{0:T(128)S(1)}, s32[128]{0:T(128)}, u32[]{:S(2)}) copy-start(s32[128]{0:T(128)} %param.13) | copy-start | bytes 1540
  0.0 26.4 %copy-start.2 = (f32[2,64,1,128]{3,2,1,0:T(1,128)S(1)}, f32[2,64,1,128]{3,2,1,0:T(1,128)}, u32[]{:S(2)}) copy-start(f32[2,64,1,128]{3,2,1,0:T(1,128)} %param.8) | copy-start | bytes 196612
  3.1 59.9 %all-to-all-start = ((f32[512,1,512]{2,1,0:T(1,128)}), f32[512,1,512]{2,1,0:T(1,128)}, u32[]{:S(2)}, u32[]{:S(2)}) async-start(f32[512,1,512]{2,1,0:T(1,128)} %bitcast.11), calls=%async_computation | async-start | bytes 2097152 | tf_op jit(solution)/shard_map/all_to_all | solution.py:56
  26.4 35.8 %collective-permute-start.2 = (f32[2,64,128]{2,1,0:T(8,128)S(1)}, f32[2,64,128]{2,1,0:T(8,128)S(1)}, u32[]{:S(2)}, u32[]{:S(2)}) collective-permute-start(f32[2,64,128]{2,1,0:T(8,128)S(1)} %bitcast.54), channel_id=1, source_target_pairs={{1,0},{2,1},{3,2},{0,3},{5,4},{6,5},{7,6},{4,7},{9,8},{10,9},{11,1... | collective-permute-start | bytes 196616 | tf_op jit(solution)/shard_map/ppermute | solution.py:14
  32.7 29.5 %collective-permute-start.1 = (f32[2,64,128]{2,1,0:T(8,128)S(1)}, f32[2,64,128]{2,1,0:T(8,128)S(1)}, u32[]{:S(2)}, u32[]{:S(2)}) collective-permute-start(f32[2,64,128]{2,1,0:T(8,128)S(1)} %bitcast.55), channel_id=1, source_target_pairs={{2,0},{3,1},{0,2},{1,3},{6,4},{7,5},{4,6},{5,7},{10,8},{11,9},{8,1... | collective-permute-start | bytes 196616 | tf_op jit(solution)/shard_map/ppermute | solution.py:14
  34.6 27.6 %collective-permute-start = (f32[2,64,128]{2,1,0:T(8,128)S(1)}, f32[2,64,128]{2,1,0:T(8,128)S(1)}, u32[]{:S(2)}, u32[]{:S(2)}) collective-permute-start(f32[2,64,128]{2,1,0:T(8,128)S(1)} %bitcast.56), channel_id=1, source_target_pairs={{3,0},{0,1},{1,2},{2,3},{7,4},{4,5},{5,6},{6,7},{11,8},{8,9},{9,10... | collective-permute-start | bytes 196616 | tf_op jit(solution)/shard_map/ppermute | solution.py:14
  51.1 5.5 %copy-start.5 = (f32[768]{0:T(1024)S(1)}, f32[768]{0:T(1024)}, u32[]{:S(2)}) copy-start(f32[768]{0:T(1024)} %param.10) | copy-start | bytes 9220
  56.7 3.3 %copy-start.1 = (f32[6,128,1024]{1,0,2:T(8,128)S(1)}, f32[6,128,1024]{1,0,2:T(8,128)}, u32[]{:S(2)}) copy-start(f32[6,128,1024]{1,0,2:T(8,128)} %reshape.178) | copy-start | bytes 9437188
  66.3 20.0 %all-to-all-start.1 = ((f32[4,256,128]{2,1,0:T(8,128)}), f32[4,256,128]{2,1,0:T(8,128)}, u32[]{:S(2)}, u32[]{:S(2)}) async-start(f32[4,256,128]{2,1,0:T(8,128)} %broadcast_in_dim.16), calls=%async_computation.1 | async-start | bytes 1048576 | tf_op jit(solution)/shard_map/all_to_all | solution.py:20
  76.6 3.9 %copy-start.3 = (f32[128,16]{0,1:T(8,128)S(1)}, f32[128,16]{0,1:T(8,128)}, u32[]{:S(2)}) copy-start(f32[128,16]{0,1:T(8,128)} %param.12) | copy-start | bytes 24580
  76.6 4.0 %copy-start.4 = (s32[128,16]{0,1:T(8,128)S(1)}, s32[128,16]{0,1:T(8,128)}, u32[]{:S(2)}) copy-start(s32[128,16]{0,1:T(8,128)} %param.11) | copy-start | bytes 24580
  86.4 14.0 %collective-permute-start.3 = (f32[1024,128]{1,0:T(8,128)}, f32[1024,128]{1,0:T(8,128)S(1)}, u32[]{:S(2)}, u32[]{:S(2)}) collective-permute-start(f32[1024,128]{1,0:T(8,128)} %bitcast.16), channel_id=1, source_target_pairs={{508,0},{0,4},{4,8},{8,12},{12,16},{16,20},{20,24},{24,28},{28,32}... | collective-permute-start | bytes 1572872 | tf_op jit(solution)/shard_map/ppermute | solution.py:14
  88.3 14.0 %collective-permute-start.4 = (f32[1024,128]{1,0:T(8,128)}, f32[1024,128]{1,0:T(8,128)S(1)}, u32[]{:S(2)}, u32[]{:S(2)}) collective-permute-start(f32[1024,128]{1,0:T(8,128)} %bitcast.16), channel_id=1, source_target_pairs={{4,0},{8,4},{12,8},{16,12},{20,16},{24,20},{28,24},{32,28},{36,32}... | collective-permute-start | bytes 1572872 | tf_op jit(solution)/shard_map/ppermute | solution.py:14

commit v11 on v9

--- a/solution.py
+++ b/solution.py
@@ -66,16 +66,21 @@
     owned_rows = obs_pert.shape[0]
     owned_blocks = owned_rows // OBSB
     behind = from_behind(summed, "mem", 1)
-    ahead = from_behind(summed, "mem", -1)
     weight_rows = own_weights(
         obs_lists, block_taper, counts, column_index, region_index, owned_blocks, regions
     )
     scale = (weighted_innovation / (M - 1))[:, None]
     rows = obs_pert * scale
-    result = 0
-    for source, weights in zip((behind, summed, ahead), weight_rows):
+
+    def weighted(source, weights):
         product = jnp.dot(rows, source, precision=HIGH).reshape(owned_blocks, OBSB, -1)
-        result = result + product * weights[:, None, None]
+        return product * weights[:, None, None]
+
+    result = weighted(summed, weight_rows[1])
+    summed, result = lax.optimization_barrier((summed, result))
+    ahead = from_behind(summed, "mem", -1)
+    result = result + weighted(behind, weight_rows[0])
+    result = result + weighted(ahead, weight_rows[2])
     return result.reshape(owned_rows, -1)
 
 

time: 91.9 us -> 93.3 us (1.015)
  waiting for transfers between devices: 32.3 us -> 34.9 us
  starting transfers between devices: 42.5 us -> 41.3 us
    ppermute x5, waiting for transfers between devices: 8.57 us -> 13.3 us  [from_behind(): return lax.ppermute(block, axis, route)]
    all_to_all x1, waiting for transfers between devices: 16.2 us -> 13.9 us  [body(): arrived = lax.all_to_all(grid, ('mem', 'dom'), 0, 0, tiled=True)]
    ppermute x5, starting transfers between devices: 17.3 us -> 16.1 us  [from_behind(): return lax.ppermute(block, axis, route)]
  transfers between devices with their start and end apart: 7 -> 7, of which waited for: 5 -> 6; matrix products, arithmetic and copies ran while one was open for 9% -> 8% of each run, Pallas kernels for 0% -> 0%
where the time goes in v11:
time: 93.3 us; the launch traced here: 92.9 us
  starting transfers between devices  41.3 us (44%)
  waiting for transfers between devices  34.9 us (37%)
  local copies, waits for them, and re-layouts  8.15 us (9%)
  matrix products  5.01 us (5%)
  other arithmetic  3.33 us (4%)
    all_to_all x1, starting transfers between devices, body(): arrived = lax.all_to_all(grid, ('mem', 'dom'), 0, 0, tiled=True)  21.1 us
    ppermute x5, starting transfers between devices, from_behind(): return lax.ppermute(block, axis, route)  16.1 us
    all_to_all x1, waiting for transfers between devices, body(): arrived = lax.all_to_all(grid, ('mem', 'dom'), 0, 0, tiled=True)  13.9 us
    ppermute x5, waiting for transfers between devices, from_behind(): return lax.ppermute(block, axis, route)  13.3 us
    all_to_all x1, waiting for transfers between devices, gathered(): return lax.all_to_all(copies, axis, 0, 0, tiled=True)  7.66 us
    dot_general x3, matrix products, weighted(): jnp.dot(rows, source, precision=HIGH).reshape(owned_blocks, OBSB, -1)  4.16 us
    all_to_all x1, starting transfers between devices, gathered(): return lax.all_to_all(copies, axis, 0, 0, tiled=True)  4.13 us
    reshape x1, local copies, waits for them, and re-layouts, body(): grid = fcst_pert.reshape(leads, regions, pair, column_blocks, width)  3.07 us
  transfers between devices with their start and end apart: 7, of which 6 were waited for; matrix products, arithmetic and copies ran while one was open for 8% of the time, Pallas kernels for 0%

profile of v11, /device:TPU:57, one launch (start us, length us, event | category | flops | bytes accessed | tf_op | source)
XLA Modules:
  0.0 92.9 jit_solution(14209956188221718510)
XLA Ops:
  0.0 0.0 copy-start
  0.0 0.0 copy-start.1
  0.0 0.0 copy-start.2
  0.0 0.0 copy-start.3
  0.0 0.0 copy-start.4
  0.0 3.1 %copy.25 = f32[2,4,2,128,128]{4,2,0,1,3:T(2,128)} copy(f32[2,4,2,128,128]{4,3,2,1,0:T(8,128)} %bitcast.53) | data formatting | bytes 2097152 | tf_op jit(solution)/shard_map/reshape | solution.py:54
  3.1 21.1 %all-to-all-start = ((f32[512,1,512]{2,1,0:T(1,128)}), f32[512,1,512]{2,1,0:T(1,128)S(1)}, u32[]{:S(2)}, u32[]{:S(2)}) async-start(f32[512,1,512]{2,1,0:T(1,128)} %bitcast.9), calls=%async_computation | async-start | bytes 2097152 | tf_op jit(solution)/shard_map/all_to_all | solution.py:56
  24.2 0.0 copy-done.1
  24.2 4.4 %collective-permute-start.2 = (f32[2,64,128]{2,1,0:T(8,128)S(1)}, f32[2,64,128]{2,1,0:T(8,128)S(1)}, u32[]{:S(2)}, u32[]{:S(2)}) collective-permute-start(f32[2,64,128]{2,1,0:T(8,128)S(1)} %bitcast.54), channel_id=1, source_target_pairs={{1,0},{2,1},{3,2},{0,3},{5,4},{6,5},{7,6},{4,7},{9,8},{10,9},{11,1... | collective-permute-start | bytes 196616 | tf_op jit(solution)/shard_map/ppermute | solution.py:14
  28.5 2.5 %collective-permute-start.1 = (f32[2,64,128]{2,1,0:T(8,128)S(1)}, f32[2,64,128]{2,1,0:T(8,128)S(1)}, u32[]{:S(2)}, u32[]{:S(2)}) collective-permute-start(f32[2,64,128]{2,1,0:T(8,128)S(1)} %bitcast.55), channel_id=1, source_target_pairs={{2,0},{3,1},{0,2},{1,3},{6,4},{7,5},{4,6},{5,7},{10,8},{11,9},{8,1... | collective-permute-start | bytes 196616 | tf_op jit(solution)/shard_map/ppermute | solution.py:14
  31.0 2.5 %collective-permute-start = (f32[2,64,128]{2,1,0:T(8,128)S(1)}, f32[2,64,128]{2,1,0:T(8,128)S(1)}, u32[]{:S(2)}, u32[]{:S(2)}) collective-permute-start(f32[2,64,128]{2,1,0:T(8,128)S(1)} %bitcast.56), channel_id=1, source_target_pairs={{3,0},{0,1},{1,2},{2,3},{7,4},{4,5},{5,6},{6,7},{11,8},{8,9},{9,10... | collective-permute-start | bytes 196616 | tf_op jit(solution)/shard_map/ppermute | solution.py:14
  33.5 0.0 copy-done.2
  33.5 0.1 copy.31
  33.7 0.0 copy-done
  33.7 0.6 gather_fusion.1
  34.3 0.6 gather_fusion
  34.9 0.0 copy-done.3
  34.9 0.1 copy.32
  35.0 0.6 gather_fusion.2
  35.6 0.1 iota_compare_fusion
  35.6 0.2 select_reduce_fusion
  35.8 0.0 copy-done.4
  35.8 0.0 collective-permute-done.2
  35.8 0.6 collective-permute-done.1
  36.4 3.5 %collective-permute-done = f32[2,64,128]{2,1,0:T(8,128)S(1)} collective-permute-done((f32[2,64,128]{2,1,0:T(8,128)S(1)}, f32[2,64,128]{2,1,0:T(8,128)S(1)}, u32[]{:S(2)}, u32[]{:S(2)}) %collective-permute-start) | collective-permute-done | bytes 65568 | tf_op jit(solution)/shard_map/ppermute | solution.py:14
  39.9 0.7 scatter_fusion
  40.6 13.9 %all-to-all-done = f32[512,1,512]{2,1,0:T(1,128)S(1)} async-done(((f32[512,1,512]{2,1,0:T(1,128)}), f32[512,1,512]{2,1,0:T(1,128)S(1)}, u32[]{:S(2)}, u32[]{:S(2)}) %all-to-all-start) | async-done | bytes 1048608 | tf_op jit(solution)/shard_map/all_to_all | solution.py:56
  54.5 0.8 convolution_bitcast_fusion
  55.3 0.2 copy.29
  55.5 0.2 broadcast_in_dim.15
  55.7 0.8 broadcast_in_dim.16
  56.5 4.1 %all-to-all-start.1 = ((f32[4,256,128]{2,1,0:T(8,128)}), f32[4,256,128]{2,1,0:T(8,128)}, u32[]{:S(2)}, u32[]{:S(2)}) async-start(f32[4,256,128]{2,1,0:T(8,128)} %broadcast_in_dim.16), calls=%async_computation.1 | async-start | bytes 1048576 | tf_op jit(solution)/shard_map/all_to_all | solution.py:20
  60.7 2.2 %broadcast_multiply_fusion = f32[768,1024]{1,0:T(8,128)S(1)} fusion(f32[768,1024]{1,0:T(8,128)} %param.9, f32[768]{0:T(1024)S(1)} %broadcast_multiply_fusion.1), kind=kLoop, calls=%fused_computation.4 | loop fusion | flops 786432 | bytes 6294528 | tf_op jit(solution)/shard_map/mul | solution.py:73
  62.9 7.7 %all-to-all-done.1 = f32[4,256,128]{2,1,0:T(8,128)} async-done(((f32[4,256,128]{2,1,0:T(8,128)}), f32[4,256,128]{2,1,0:T(8,128)}, u32[]{:S(2)}, u32[]{:S(2)}) %all-to-all-start.1) | async-done | bytes 524320 | tf_op jit(solution)/shard_map/all_to_all | solution.py:20
  70.5 1.2 %copy.30 = f32[128,4,2,128]{3,2,1,0:T(2,128)S(1)} copy(f32[128,4,2,128]{3,2,0,1:T(2,128)} %bitcast.15) | data formatting | bytes 1048576 | tf_op jit(solution)/shard_map/transpose | solution.py:63
  71.7 4.9 %collective-permute-start.3 = (f32[1024,128]{1,0:T(8,128)S(1)}, f32[1024,128]{1,0:T(8,128)S(1)}, u32[]{:S(2)}, u32[]{:S(2)}) collective-permute-start(f32[1024,128]{1,0:T(8,128)S(1)} %bitcast.48), channel_id=1, source_target_pairs={{508,0},{0,4},{4,8},{8,12},{12,16},{16,20},{20,24},{24,28},{28,32}... | collective-permute-start | bytes 1572872 | tf_op jit(solution)/shard_map/ppermute | solution.py:14
  76.6 1.4 %convolution_multiply_fusion = f32[6,128,128]{2,1,0:T(8,128)S(1)} fusion(f32[6,128,1024]{2,1,0:T(8,128)S(1)} %bitcast.46, f32[1024,128,1]{1,0,2:T(8,128)S(1)} %bitcast.49, f32[6]{0:T(128)S(1)} %get-tuple-element.11), kind=kOutput, calls=%fused_computation.5 | convolution fusion | flops 604078080 | bytes 4063256 | tf_op jit(solution)/shard_map/dot_general | solution.py:76
  78.0 1.9 %collective-permute-start.4 = (f32[1024,128]{1,0:T(8,128)S(1)}, f32[1024,128]{1,0:T(8,128)S(1)}, u32[]{:S(2)}, u32[]{:S(2)}) collective-permute-start(f32[1024,128]{1,0:T(8,128)S(1)} %bitcast.50), channel_id=1, source_target_pairs={{4,0},{8,4},{12,8},{16,12},{20,16},{24,20},{28,24},{32,28},{36,32}... | collective-permute-start | bytes 1572872 | tf_op jit(solution)/shard_map/ppermute | solution.py:14
  79.9 2.8 %collective-permute-done.3 = f32[1024,128]{1,0:T(8,128)S(1)} collective-permute-done((f32[1024,128]{1,0:T(8,128)S(1)}, f32[1024,128]{1,0:T(8,128)S(1)}, u32[]{:S(2)}, u32[]{:S(2)}) %collective-permute-start.3) | collective-permute-done | bytes 524320 | tf_op jit(solution)/shard_map/ppermute | solution.py:14
  82.7 1.4 %fusion.6 = f32[768,128]{1,0:T(8,128)S(1)} fusion(f32[768,1024]{1,0:T(8,128)S(1)} %broadcast_multiply_fusion, f32[1024,128]{1,0:T(8,128)S(1)} %collective-permute-done.3), kind=kOutput, calls=%fused_computation.31 | convolution fusion | flops 603979776 | bytes 4063232 | tf_op jit(solution)/shard_map/dot_general | solution.py:76
  84.1 6.5 %collective-permute-done.4 = f32[1024,128]{1,0:T(8,128)S(1)} collective-permute-done((f32[1024,128]{1,0:T(8,128)S(1)}, f32[1024,128]{1,0:T(8,128)S(1)}, u32[]{:S(2)}, u32[]{:S(2)}) %collective-permute-start.4) | collective-permute-done | bytes 524320 | tf_op jit(solution)/shard_map/ppermute | solution.py:14
  90.6 1.4 %fusion.7 = f32[768,128]{1,0:T(8,128)S(1)} fusion(f32[768,1024]{1,0:T(8,128)S(1)} %broadcast_multiply_fusion, f32[1024,128]{1,0:T(8,128)S(1)} %collective-permute-done.4), kind=kOutput, calls=%fused_computation.32 | convolution fusion | flops 603979776 | bytes 4063232 | tf_op jit(solution)/shard_map/dot_general | solution.py:76
  92.0 0.9 multiply_add_fusion
  (8 shorter events, 0.1 us)
Async XLA Ops:
  0.0 33.7 %copy-start = (s32[128]{0:T(128)S(1)}, s32[128]{0:T(128)}, u32[]{:S(2)}) copy-start(s32[128]{0:T(128)} %param.13) | copy-start | bytes 1540
  0.0 24.2 %copy-start.1 = (f32[2,64,1,128]{3,2,1,0:T(1,128)S(1)}, f32[2,64,1,128]{3,2,1,0:T(1,128)}, u32[]{:S(2)}) copy-start(f32[2,64,1,128]{3,2,1,0:T(1,128)} %param.8) | copy-start | bytes 196612
  0.0 33.5 %copy-start.2 = (s32[128,16]{0,1:T(8,128)S(1)}, s32[128,16]{0,1:T(8,128)}, u32[]{:S(2)}) copy-start(s32[128,16]{0,1:T(8,128)} %param.11) | copy-start | bytes 24580
  0.0 34.9 %copy-start.3 = (f32[128,16]{0,1:T(8,128)S(1)}, f32[128,16]{0,1:T(8,128)}, u32[]{:S(2)}) copy-start(f32[128,16]{0,1:T(8,128)} %param.12) | copy-start | bytes 24580
  0.0 35.8 %copy-start.4 = (f32[768]{0:T(1024)S(1)}, f32[768]{0:T(1024)}, u32[]{:S(2)}) copy-start(f32[768]{0:T(1024)} %param.10) | copy-start | bytes 9220
  3.1 51.4 %all-to-all-start = ((f32[512,1,512]{2,1,0:T(1,128)}), f32[512,1,512]{2,1,0:T(1,128)S(1)}, u32[]{:S(2)}, u32[]{:S(2)}) async-start(f32[512,1,512]{2,1,0:T(1,128)} %bitcast.9), calls=%async_computation | async-start | bytes 2097152 | tf_op jit(solution)/shard_map/all_to_all | solution.py:56
  24.2 11.6 %collective-permute-start.2 = (f32[2,64,128]{2,1,0:T(8,128)S(1)}, f32[2,64,128]{2,1,0:T(8,128)S(1)}, u32[]{:S(2)}, u32[]{:S(2)}) collective-permute-start(f32[2,64,128]{2,1,0:T(8,128)S(1)} %bitcast.54), channel_id=1, source_target_pairs={{1,0},{2,1},{3,2},{0,3},{5,4},{6,5},{7,6},{4,7},{9,8},{10,9},{11,1... | collective-permute-start | bytes 196616 | tf_op jit(solution)/shard_map/ppermute | solution.py:14
  28.5 7.8 %collective-permute-start.1 = (f32[2,64,128]{2,1,0:T(8,128)S(1)}, f32[2,64,128]{2,1,0:T(8,128)S(1)}, u32[]{:S(2)}, u32[]{:S(2)}) collective-permute-start(f32[2,64,128]{2,1,0:T(8,128)S(1)} %bitcast.55), channel_id=1, source_target_pairs={{2,0},{3,1},{0,2},{1,3},{6,4},{7,5},{4,6},{5,7},{10,8},{11,9},{8,1... | collective-permute-start | bytes 196616 | tf_op jit(solution)/shard_map/ppermute | solution.py:14
  31.0 8.8 %collective-permute-start = (f32[2,64,128]{2,1,0:T(8,128)S(1)}, f32[2,64,128]{2,1,0:T(8,128)S(1)}, u32[]{:S(2)}, u32[]{:S(2)}) collective-permute-start(f32[2,64,128]{2,1,0:T(8,128)S(1)} %bitcast.56), channel_id=1, source_target_pairs={{3,0},{0,1},{1,2},{2,3},{7,4},{4,5},{5,6},{6,7},{11,8},{8,9},{9,10... | collective-permute-start | bytes 196616 | tf_op jit(solution)/shard_map/ppermute | solution.py:14
  56.5 14.0 %all-to-all-start.1 = ((f32[4,256,128]{2,1,0:T(8,128)}), f32[4,256,128]{2,1,0:T(8,128)}, u32[]{:S(2)}, u32[]{:S(2)}) async-start(f32[4,256,128]{2,1,0:T(8,128)} %broadcast_in_dim.16), calls=%async_computation.1 | async-start | bytes 1048576 | tf_op jit(solution)/shard_map/all_to_all | solution.py:20
  71.7 11.0 %collective-permute-start.3 = (f32[1024,128]{1,0:T(8,128)S(1)}, f32[1024,128]{1,0:T(8,128)S(1)}, u32[]{:S(2)}, u32[]{:S(2)}) collective-permute-start(f32[1024,128]{1,0:T(8,128)S(1)} %bitcast.48), channel_id=1, source_target_pairs={{508,0},{0,4},{4,8},{8,12},{12,16},{16,20},{20,24},{24,28},{28,32}... | collective-permute-start | bytes 1572872 | tf_op jit(solution)/shard_map/ppermute | solution.py:14
  78.0 12.6 %collective-permute-start.4 = (f32[1024,128]{1,0:T(8,128)S(1)}, f32[1024,128]{1,0:T(8,128)S(1)}, u32[]{:S(2)}, u32[]{:S(2)}) collective-permute-start(f32[1024,128]{1,0:T(8,128)S(1)} %bitcast.50), channel_id=1, source_target_pairs={{4,0},{8,4},{12,8},{16,12},{20,16},{24,20},{28,24},{32,28},{36,32}... | collective-permute-start | bytes 1572872 | tf_op jit(solution)/shard_map/ppermute | solution.py:14

commit v12 on v9

--- a/solution.py
+++ b/solution.py
@@ -52,12 +52,12 @@
     width = columns // column_blocks
     pair = local_members // regions
     grid = fcst_pert.reshape(leads, regions, pair, column_blocks, width)
-    grid = jnp.transpose(grid, (3, 1, 0, 2, 4)).reshape(column_blocks * regions, -1)
-    arrived = lax.all_to_all(grid, ("mem", "dom"), 0, 0, tiled=True)
-    arrived = arrived.reshape(column_blocks, regions, leads, pair, width)
+    grid = jnp.transpose(grid, (1, 3, 0, 2, 4)).reshape(regions * column_blocks, -1)
+    arrived = lax.all_to_all(grid, ("dom", "mem"), 0, 0, tiled=True)
+    arrived = arrived.reshape(regions, column_blocks, leads, pair, width)
     targets = sensitivity.shape[1]
     levels = shifted_copies(sensitivity[:, :, 0, :], "dom")
-    quarter = jnp.einsum("mdljc,dltc->mjlt", arrived, levels, precision=HIGH)
+    quarter = jnp.einsum("dmljc,dltc->mjlt", arrived, levels, precision=HIGH)
     quarter = quarter.reshape(column_blocks * pair, leads * targets)
     full = gathered(quarter, "dom").reshape(regions, column_blocks, pair, -1)
     summed = jnp.transpose(full, (1, 0, 2, 3)).reshape(column_blocks * local_members, -1)

time: 91.9 us -> 92.6 us (level)
  no operation moved by 1% of the time
where the time goes in v12:
time: 92.6 us; the launch traced here: 92.2 us
  starting transfers between devices  43.2 us (47%)
  waiting for transfers between devices  32.5 us (35%)
  local copies, waits for them, and re-layouts  8.13 us (9%)
  matrix products  4.77 us (5%)
  other arithmetic  3.33 us (4%)
    all_to_all x1, starting transfers between devices, body(): arrived = lax.all_to_all(grid, ('dom', 'mem'), 0, 0, tiled=True)  21.1 us
    ppermute x5, starting transfers between devices, from_behind(): return lax.ppermute(block, axis, route)  18 us
    all_to_all x1, waiting for transfers between devices, body(): arrived = lax.all_to_all(grid, ('dom', 'mem'), 0, 0, tiled=True)  16.3 us
    ppermute x5, waiting for transfers between devices, from_behind(): return lax.ppermute(block, axis, route)  8.97 us
    all_to_all x1, waiting for transfers between devices, gathered(): return lax.all_to_all(copies, axis, 0, 0, tiled=True)  7.31 us
    dot_general x3, matrix products, body(): jnp.dot(rows, source, precision=HIGH).reshape(owned_blocks, OBSB, -1)  4.16 us
    all_to_all x1, starting transfers between devices, gathered(): return lax.all_to_all(copies, axis, 0, 0, tiled=True)  4.13 us
    reshape x1, local copies, waits for them, and re-layouts, body(): grid = fcst_pert.reshape(leads, regions, pair, column_blocks, width)  3.06 us
  transfers between devices with their start and end apart: 7, of which 5 were waited for; matrix products, arithmetic and copies ran while one was open for 9% of the time, Pallas kernels for 0%

profile of v12, /device:TPU:57, one launch (start us, length us, event | category | flops | bytes accessed | tf_op | source)
XLA Modules:
  0.0 92.2 jit_solution(10697971034241764740)
XLA Ops:
  0.0 0.0 copy-start
  0.0 0.0 copy-start.1
  0.0 0.0 copy-start.2
  0.0 0.0 copy-start.3
  0.0 0.0 copy-start.4
  0.0 3.1 %copy.25 = f32[2,4,2,128,128]{4,2,0,3,1:T(2,128)} copy(f32[2,4,2,128,128]{4,3,2,1,0:T(8,128)} %bitcast.52) | data formatting | bytes 2097152 | tf_op jit(solution)/shard_map/reshape | solution.py:54
  3.1 21.1 %all-to-all-start = ((f32[512,1,512]{2,1,0:T(1,128)}), f32[512,1,512]{2,1,0:T(1,128)S(1)}, u32[]{:S(2)}, u32[]{:S(2)}) async-start(f32[512,1,512]{2,1,0:T(1,128)} %bitcast.9), calls=%async_computation | async-start | bytes 2097152 | tf_op jit(solution)/shard_map/all_to_all | solution.py:56
  24.2 0.0 copy-done.1
  24.2 3.1 %collective-permute-start = (f32[2,64,128]{2,1,0:T(8,128)S(1)}, f32[2,64,128]{2,1,0:T(8,128)S(1)}, u32[]{:S(2)}, u32[]{:S(2)}) collective-permute-start(f32[2,64,128]{2,1,0:T(8,128)S(1)} %bitcast.53), channel_id=1, source_target_pairs={{3,0},{0,1},{1,2},{2,3},{7,4},{4,5},{5,6},{6,7},{11,8},{8,9},{9,10... | collective-permute-start | bytes 196616 | tf_op jit(solution)/shard_map/ppermute | solution.py:14
  27.3 4.3 %collective-permute-start.1 = (f32[2,64,128]{2,1,0:T(8,128)S(1)}, f32[2,64,128]{2,1,0:T(8,128)S(1)}, u32[]{:S(2)}, u32[]{:S(2)}) collective-permute-start(f32[2,64,128]{2,1,0:T(8,128)S(1)} %bitcast.54), channel_id=1, source_target_pairs={{2,0},{3,1},{0,2},{1,3},{6,4},{7,5},{4,6},{5,7},{10,8},{11,9},{8,1... | collective-permute-start | bytes 196616 | tf_op jit(solution)/shard_map/ppermute | solution.py:14
  31.6 3.1 %collective-permute-start.2 = (f32[2,64,128]{2,1,0:T(8,128)S(1)}, f32[2,64,128]{2,1,0:T(8,128)S(1)}, u32[]{:S(2)}, u32[]{:S(2)}) collective-permute-start(f32[2,64,128]{2,1,0:T(8,128)S(1)} %bitcast.55), channel_id=1, source_target_pairs={{1,0},{2,1},{3,2},{0,3},{5,4},{6,5},{7,6},{4,7},{9,8},{10,9},{11,1... | collective-permute-start | bytes 196616 | tf_op jit(solution)/shard_map/ppermute | solution.py:14
  34.7 0.0 copy-done.2
  34.7 0.1 copy.31
  34.8 0.0 copy-done.3
  34.8 0.1 copy.32
  35.0 0.6 gather_fusion
  35.5 0.6 gather_fusion.2
  36.1 0.0 copy-done
  36.1 0.6 gather_fusion.1
  36.7 0.1 iota_compare_fusion
  36.8 0.0 copy-done.4
  36.8 0.0 collective-permute-done
  36.8 0.0 collective-permute-done.1
  36.8 1.1 %collective-permute-done.2 = f32[2,64,128]{2,1,0:T(8,128)S(1)} collective-permute-done((f32[2,64,128]{2,1,0:T(8,128)S(1)}, f32[2,64,128]{2,1,0:T(8,128)S(1)}, u32[]{:S(2)}, u32[]{:S(2)}) %collective-permute-start.2) | collective-permute-done | bytes 65568 | tf_op jit(solution)/shard_map/ppermute | solution.py:14
  38.0 0.7 scatter_fusion
  38.6 16.3 %all-to-all-done = f32[512,1,512]{2,1,0:T(1,128)S(1)} async-done(((f32[512,1,512]{2,1,0:T(1,128)}), f32[512,1,512]{2,1,0:T(1,128)S(1)}, u32[]{:S(2)}, u32[]{:S(2)}) %all-to-all-start) | async-done | bytes 1048608 | tf_op jit(solution)/shard_map/all_to_all | solution.py:56
  54.9 0.6 convolution_bitcast_fusion
  55.5 0.2 copy.29
  55.7 0.2 broadcast_in_dim.15
  55.9 0.8 broadcast_in_dim.16
  56.7 4.1 %all-to-all-start.1 = ((f32[4,256,128]{2,1,0:T(8,128)}), f32[4,256,128]{2,1,0:T(8,128)}, u32[]{:S(2)}, u32[]{:S(2)}) async-start(f32[4,256,128]{2,1,0:T(8,128)} %broadcast_in_dim.16), calls=%async_computation.1 | async-start | bytes 1048576 | tf_op jit(solution)/shard_map/all_to_all | solution.py:20
  60.8 0.2 select_reduce_fusion
  61.0 2.2 %broadcast_multiply_fusion = f32[768,1024]{1,0:T(8,128)S(1)} fusion(f32[768,1024]{1,0:T(8,128)} %param.9, f32[768]{0:T(1024)S(1)} %broadcast_multiply_fusion.1), kind=kLoop, calls=%fused_computation.4 | loop fusion | flops 786432 | bytes 6294528 | tf_op jit(solution)/shard_map/mul | solution.py:74
  63.2 7.3 %all-to-all-done.1 = f32[4,256,128]{2,1,0:T(8,128)} async-done(((f32[4,256,128]{2,1,0:T(8,128)}), f32[4,256,128]{2,1,0:T(8,128)}, u32[]{:S(2)}, u32[]{:S(2)}) %all-to-all-start.1) | async-done | bytes 524320 | tf_op jit(solution)/shard_map/all_to_all | solution.py:20
  70.5 1.2 %copy.30 = f32[128,4,2,128]{3,2,1,0:T(2,128)S(1)} copy(f32[128,4,2,128]{3,2,0,1:T(2,128)} %bitcast.15) | data formatting | bytes 1048576 | tf_op jit(solution)/shard_map/transpose | solution.py:63
  71.7 5.6 %collective-permute-start.3 = (f32[1024,128]{1,0:T(8,128)S(1)}, f32[1024,128]{1,0:T(8,128)S(1)}, u32[]{:S(2)}, u32[]{:S(2)}) collective-permute-start(f32[1024,128]{1,0:T(8,128)S(1)} %bitcast.47), channel_id=1, source_target_pairs={{508,0},{0,4},{4,8},{8,12},{12,16},{16,20},{20,24},{24,28},{28,32}... | collective-permute-start | bytes 1572872 | tf_op jit(solution)/shard_map/ppermute | solution.py:14
  77.3 1.9 %collective-permute-start.4 = (f32[1024,128]{1,0:T(8,128)S(1)}, f32[1024,128]{1,0:T(8,128)S(1)}, u32[]{:S(2)}, u32[]{:S(2)}) collective-permute-start(f32[1024,128]{1,0:T(8,128)S(1)} %bitcast.48), channel_id=1, source_target_pairs={{4,0},{8,4},{12,8},{16,12},{20,16},{24,20},{28,24},{32,28},{36,32}... | collective-permute-start | bytes 1572872 | tf_op jit(solution)/shard_map/ppermute | solution.py:14
  79.2 1.4 %convolution_multiply_fusion = f32[6,128,128]{2,1,0:T(8,128)S(1)} fusion(f32[6,128,1024]{2,1,0:T(8,128)S(1)} %bitcast.45, f32[1024,128,1]{1,0,2:T(8,128)S(1)} %bitcast.49, f32[6]{0:T(128)S(1)} %get-tuple-element.7), kind=kOutput, calls=%fused_computation.5 | convolution fusion | flops 604078080 | bytes 4063256 | tf_op jit(solution)/shard_map/dot_general | solution.py:77
  80.6 2.8 %collective-permute-done.3 = f32[1024,128]{1,0:T(8,128)S(1)} collective-permute-done((f32[1024,128]{1,0:T(8,128)S(1)}, f32[1024,128]{1,0:T(8,128)S(1)}, u32[]{:S(2)}, u32[]{:S(2)}) %collective-permute-start.3) | collective-permute-done | bytes 524320 | tf_op jit(solution)/shard_map/ppermute | solution.py:14
  83.4 1.4 %fusion.6 = f32[768,128]{1,0:T(8,128)S(1)} fusion(f32[768,1024]{1,0:T(8,128)S(1)} %broadcast_multiply_fusion, f32[1024,128]{1,0:T(8,128)S(1)} %collective-permute-done.3), kind=kOutput, calls=%fused_computation.31 | convolution fusion | flops 603979776 | bytes 4063232 | tf_op jit(solution)/shard_map/dot_general | solution.py:77
  84.8 5.1 %collective-permute-done.4 = f32[1024,128]{1,0:T(8,128)S(1)} collective-permute-done((f32[1024,128]{1,0:T(8,128)S(1)}, f32[1024,128]{1,0:T(8,128)S(1)}, u32[]{:S(2)}, u32[]{:S(2)}) %collective-permute-start.4) | collective-permute-done | bytes 524320 | tf_op jit(solution)/shard_map/ppermute | solution.py:14
  89.9 1.4 %fusion.7 = f32[768,128]{1,0:T(8,128)S(1)} fusion(f32[768,1024]{1,0:T(8,128)S(1)} %broadcast_multiply_fusion, f32[1024,128]{1,0:T(8,128)S(1)} %collective-permute-done.4), kind=kOutput, calls=%fused_computation.32 | convolution fusion | flops 603979776 | bytes 4063232 | tf_op jit(solution)/shard_map/dot_general | solution.py:77
  91.3 0.9 multiply_add_fusion
  (8 shorter events, 0.1 us)
Async XLA Ops:
  0.0 36.1 %copy-start = (s32[128]{0:T(128)S(1)}, s32[128]{0:T(128)}, u32[]{:S(2)}) copy-start(s32[128]{0:T(128)} %param.13) | copy-start | bytes 1540
  0.0 24.2 %copy-start.1 = (f32[2,64,1,128]{3,2,1,0:T(1,128)S(1)}, f32[2,64,1,128]{3,2,1,0:T(1,128)}, u32[]{:S(2)}) copy-start(f32[2,64,1,128]{3,2,1,0:T(1,128)} %param.8) | copy-start | bytes 196612
  0.0 34.7 %copy-start.2 = (s32[128,16]{0,1:T(8,128)S(1)}, s32[128,16]{0,1:T(8,128)}, u32[]{:S(2)}) copy-start(s32[128,16]{0,1:T(8,128)} %param.11) | copy-start | bytes 24580
  0.0 34.8 %copy-start.3 = (f32[128,16]{0,1:T(8,128)S(1)}, f32[128,16]{0,1:T(8,128)}, u32[]{:S(2)}) copy-start(f32[128,16]{0,1:T(8,128)} %param.12) | copy-start | bytes 24580
  0.0 36.8 %copy-start.4 = (f32[768]{0:T(1024)S(1)}, f32[768]{0:T(1024)}, u32[]{:S(2)}) copy-start(f32[768]{0:T(1024)} %param.10) | copy-start | bytes 9220
  3.1 51.8 %all-to-all-start = ((f32[512,1,512]{2,1,0:T(1,128)}), f32[512,1,512]{2,1,0:T(1,128)S(1)}, u32[]{:S(2)}, u32[]{:S(2)}) async-start(f32[512,1,512]{2,1,0:T(1,128)} %bitcast.9), calls=%async_computation | async-start | bytes 2097152 | tf_op jit(solution)/shard_map/all_to_all | solution.py:56
  24.2 12.7 %collective-permute-start = (f32[2,64,128]{2,1,0:T(8,128)S(1)}, f32[2,64,128]{2,1,0:T(8,128)S(1)}, u32[]{:S(2)}, u32[]{:S(2)}) collective-permute-start(f32[2,64,128]{2,1,0:T(8,128)S(1)} %bitcast.53), channel_id=1, source_target_pairs={{3,0},{0,1},{1,2},{2,3},{7,4},{4,5},{5,6},{6,7},{11,8},{8,9},{9,10... | collective-permute-start | bytes 196616 | tf_op jit(solution)/shard_map/ppermute | solution.py:14
  27.3 9.6 %collective-permute-start.1 = (f32[2,64,128]{2,1,0:T(8,128)S(1)}, f32[2,64,128]{2,1,0:T(8,128)S(1)}, u32[]{:S(2)}, u32[]{:S(2)}) collective-permute-start(f32[2,64,128]{2,1,0:T(8,128)S(1)} %bitcast.54), channel_id=1, source_target_pairs={{2,0},{3,1},{0,2},{1,3},{6,4},{7,5},{4,6},{5,7},{10,8},{11,9},{8,1... | collective-permute-start | bytes 196616 | tf_op jit(solution)/shard_map/ppermute | solution.py:14
  31.6 6.3 %collective-permute-start.2 = (f32[2,64,128]{2,1,0:T(8,128)S(1)}, f32[2,64,128]{2,1,0:T(8,128)S(1)}, u32[]{:S(2)}, u32[]{:S(2)}) collective-permute-start(f32[2,64,128]{2,1,0:T(8,128)S(1)} %bitcast.55), channel_id=1, source_target_pairs={{1,0},{2,1},{3,2},{0,3},{5,4},{6,5},{7,6},{4,7},{9,8},{10,9},{11,1... | collective-permute-start | bytes 196616 | tf_op jit(solution)/shard_map/ppermute | solution.py:14
  56.7 13.8 %all-to-all-start.1 = ((f32[4,256,128]{2,1,0:T(8,128)}), f32[4,256,128]{2,1,0:T(8,128)}, u32[]{:S(2)}, u32[]{:S(2)}) async-start(f32[4,256,128]{2,1,0:T(8,128)} %broadcast_in_dim.16), calls=%async_computation.1 | async-start | bytes 1048576 | tf_op jit(solution)/shard_map/all_to_all | solution.py:20
  71.7 11.7 %collective-permute-start.3 = (f32[1024,128]{1,0:T(8,128)S(1)}, f32[1024,128]{1,0:T(8,128)S(1)}, u32[]{:S(2)}, u32[]{:S(2)}) collective-permute-start(f32[1024,128]{1,0:T(8,128)S(1)} %bitcast.47), channel_id=1, source_target_pairs={{508,0},{0,4},{4,8},{8,12},{12,16},{16,20},{20,24},{24,28},{28,32}... | collective-permute-start | bytes 1572872 | tf_op jit(solution)/shard_map/ppermute | solution.py:14
  77.3 12.6 %collective-permute-start.4 = (f32[1024,128]{1,0:T(8,128)S(1)}, f32[1024,128]{1,0:T(8,128)S(1)}, u32[]{:S(2)}, u32[]{:S(2)}) collective-permute-start(f32[1024,128]{1,0:T(8,128)S(1)} %bitcast.48), channel_id=1, source_target_pairs={{4,0},{8,4},{12,8},{16,12},{20,16},{24,20},{28,24},{32,28},{36,32}... | collective-permute-start | bytes 1572872 | tf_op jit(solution)/shard_map/ppermute | solution.py:14

commit v13 on v9

--- a/solution.py
+++ b/solution.py
@@ -59,8 +59,10 @@
     levels = shifted_copies(sensitivity[:, :, 0, :], "dom")
     quarter = jnp.einsum("mdljc,dltc->mjlt", arrived, levels, precision=HIGH)
     quarter = quarter.reshape(column_blocks * pair, leads * targets)
-    full = gathered(quarter, "dom").reshape(regions, column_blocks, pair, -1)
-    summed = jnp.transpose(full, (1, 0, 2, 3)).reshape(column_blocks * local_members, -1)
+    lanes = quarter.reshape(column_blocks, 1, -1)
+    copies = jnp.broadcast_to(lanes, (column_blocks, regions, lanes.shape[2]))
+    summed = lax.all_to_all(copies, "dom", 1, 1, tiled=True)
+    summed = summed.reshape(column_blocks * local_members, -1)
     column_index = lax.axis_index("mem")
     region_index = lax.axis_index("dom")
     owned_rows = obs_pert.shape[0]

time: 91.9 us -> 97.1 us (1.057)
  local copies, waits for them, and re-layouts: 8.13 us -> 12.9 us
  matrix products: 5.02 us -> 7.11 us
  waiting for transfers between devices: 32.3 us -> 30.4 us
    reshape x0 -> x2, local copies, waits for them, and re-layouts: none -> 4.09 us  [body(): summed = summed.reshape(column_blocks * local_members, -1)]
    all_to_all x0 -> x1, local copies, waits for them, and re-layouts: none -> 2.16 us  [body(): summed = lax.all_to_all(copies, 'dom', 1, 1, tiled=True)]
    dot_general x3, matrix products: 4.17 us -> 6.26 us  [body(): jnp.dot(rows, source, precision=HIGH).reshape(owned_blocks, OBSB, -1)]
    ppermute x5, waiting for transfers between devices: 8.57 us -> 6.68 us  [from_behind(): return lax.ppermute(block, axis, route)]
    transpose x1 -> x0, local copies, waits for them, and re-layouts: 1.22 us -> none  [body(): jnp.transpose(full, (1, 0, 2, 3)).reshape(column_blocks * local_members, -1)]
  transfers between devices with their start and end apart: 7 -> 7, of which waited for: 5 -> 4; matrix products, arithmetic and copies ran while one was open for 9% -> 12% of each run, Pallas kernels for 0% -> 0%
where the time goes in v13:
time: 97.1 us; the launch traced here: 96.4 us
  starting transfers between devices  42.5 us (44%)
  waiting for transfers between devices  30.4 us (31%)
  local copies, waits for them, and re-layouts  12.9 us (13%)
  matrix products  7.11 us (7%)
  other arithmetic  3.33 us (3%)
    all_to_all x1, starting transfers between devices, body(): arrived = lax.all_to_all(grid, ('mem', 'dom'), 0, 0, tiled=True)  21.1 us
    ppermute x5, starting transfers between devices, from_behind(): return lax.ppermute(block, axis, route)  17.3 us
    all_to_all x1, waiting for transfers between devices, body(): arrived = lax.all_to_all(grid, ('mem', 'dom'), 0, 0, tiled=True)  16.2 us
    all_to_all x1, waiting for transfers between devices, body(): summed = lax.all_to_all(copies, 'dom', 1, 1, tiled=True)  7.51 us
    ppermute x5, waiting for transfers between devices, from_behind(): return lax.ppermute(block, axis, route)  6.68 us
    dot_general x3, matrix products, body(): jnp.dot(rows, source, precision=HIGH).reshape(owned_blocks, OBSB, -1)  6.26 us
    all_to_all x1, starting transfers between devices, body(): summed = lax.all_to_all(copies, 'dom', 1, 1, tiled=True)  4.13 us
    reshape x2, local copies, waits for them, and re-layouts, body(): summed = summed.reshape(column_blocks * local_members, -1)  4.09 us
  transfers between devices with their start and end apart: 7, of which 4 were waited for; matrix products, arithmetic and copies ran while one was open for 12% of the time, Pallas kernels for 0%

profile of v13, /device:TPU:57, one launch (start us, length us, event | category | flops | bytes accessed | tf_op | source)
XLA Modules:
  0.0 96.4 jit_solution(10816625182547099765)
XLA Ops:
  0.0 0.0 copy-start
  0.0 0.0 copy-start.1
  0.0 0.0 copy-start.2
  0.0 0.0 copy-start.3
  0.0 0.0 copy-start.4
  0.0 3.1 %copy.26 = f32[2,4,2,128,128]{4,2,0,1,3:T(2,128)} copy(f32[2,4,2,128,128]{4,3,2,1,0:T(8,128)} %bitcast.44) | data formatting | bytes 2097152 | tf_op jit(solution)/shard_map/reshape | solution.py:54
  3.1 21.1 %all-to-all-start = ((f32[512,1,512]{2,1,0:T(1,128)}), f32[512,1,512]{2,1,0:T(1,128)S(1)}, u32[]{:S(2)}, u32[]{:S(2)}) async-start(f32[512,1,512]{2,1,0:T(1,128)} %bitcast.9), calls=%async_computation | async-start | bytes 2097152 | tf_op jit(solution)/shard_map/all_to_all | solution.py:56
  24.2 0.0 copy-done.1
  24.2 3.1 %collective-permute-start = (f32[2,64,128]{2,1,0:T(8,128)S(1)}, f32[2,64,128]{2,1,0:T(8,128)S(1)}, u32[]{:S(2)}, u32[]{:S(2)}) collective-permute-start(f32[2,64,128]{2,1,0:T(8,128)S(1)} %bitcast.46), channel_id=1, source_target_pairs={{3,0},{0,1},{1,2},{2,3},{7,4},{4,5},{5,6},{6,7},{11,8},{8,9},{9,10... | collective-permute-start | bytes 196616 | tf_op jit(solution)/shard_map/ppermute | solution.py:14
  27.3 4.3 %collective-permute-start.1 = (f32[2,64,128]{2,1,0:T(8,128)S(1)}, f32[2,64,128]{2,1,0:T(8,128)S(1)}, u32[]{:S(2)}, u32[]{:S(2)}) collective-permute-start(f32[2,64,128]{2,1,0:T(8,128)S(1)} %bitcast.47), channel_id=1, source_target_pairs={{2,0},{3,1},{0,2},{1,3},{6,4},{7,5},{4,6},{5,7},{10,8},{11,9},{8,1... | collective-permute-start | bytes 196616 | tf_op jit(solution)/shard_map/ppermute | solution.py:14
  31.6 3.1 %collective-permute-start.2 = (f32[2,64,128]{2,1,0:T(8,128)S(1)}, f32[2,64,128]{2,1,0:T(8,128)S(1)}, u32[]{:S(2)}, u32[]{:S(2)}) collective-permute-start(f32[2,64,128]{2,1,0:T(8,128)S(1)} %bitcast.48), channel_id=1, source_target_pairs={{1,0},{2,1},{3,2},{0,3},{5,4},{6,5},{7,6},{4,7},{9,8},{10,9},{11,1... | collective-permute-start | bytes 196616 | tf_op jit(solution)/shard_map/ppermute | solution.py:14
  34.7 0.0 copy-done.2
  34.7 0.1 copy.33
  34.8 0.0 copy-done.3
  34.8 0.1 copy.34
  35.0 0.6 gather_fusion
  35.5 0.6 gather_fusion.2
  36.1 0.0 copy-done
  36.1 0.6 gather_fusion.1
  36.7 0.1 iota_compare_fusion
  36.8 0.0 copy-done.4
  36.8 0.0 collective-permute-done
  36.8 0.0 collective-permute-done.1
  36.8 0.7 collective-permute-done.2
  37.6 0.7 scatter_fusion
  38.2 16.2 %all-to-all-done = f32[512,1,512]{2,1,0:T(1,128)S(1)} async-done(((f32[512,1,512]{2,1,0:T(1,128)}), f32[512,1,512]{2,1,0:T(1,128)S(1)}, u32[]{:S(2)}, u32[]{:S(2)}) %all-to-all-start) | async-done | bytes 1048608 | tf_op jit(solution)/shard_map/all_to_all | solution.py:56
  54.5 0.8 convolution_bitcast_fusion
  55.3 0.1 copy.31
  55.4 0.8 broadcast_in_dim.16
  56.3 4.1 %all-to-all-start.1 = ((f32[128,4,256]{2,0,1:T(8,128)}), f32[128,4,256]{2,0,1:T(8,128)}, u32[]{:S(2)}, u32[]{:S(2)}) async-start(f32[128,4,256]{2,0,1:T(8,128)} %broadcast_in_dim.16), calls=%async_computation.1 | async-start | bytes 1048576 | tf_op jit(solution)/shard_map/all_to_all | solution.py:64
  60.4 0.2 select_reduce_fusion
  60.6 2.2 %broadcast_multiply_fusion = f32[768,1024]{1,0:T(8,128)S(1)} fusion(f32[768,1024]{1,0:T(8,128)} %param.9, f32[768]{0:T(1024)S(1)} %broadcast_multiply_fusion.1), kind=kLoop, calls=%fused_computation.4 | loop fusion | flops 786432 | bytes 6294528 | tf_op jit(solution)/shard_map/mul | solution.py:76
  62.7 7.5 %all-to-all-done.1 = f32[128,4,256]{2,0,1:T(8,128)} async-done(((f32[128,4,256]{2,0,1:T(8,128)}), f32[128,4,256]{2,0,1:T(8,128)}, u32[]{:S(2)}, u32[]{:S(2)}) %all-to-all-start.1) | async-done | bytes 524320 | tf_op jit(solution)/shard_map/all_to_all | solution.py:64
  70.2 2.2 %copy.32 = f32[128,4,256]{2,1,0:T(4,128)} copy(f32[128,4,256]{2,0,1:T(8,128)} %all-to-all-done.1) | data formatting | bytes 1048576 | tf_op jit(solution)/shard_map/all_to_all | solution.py:64
  72.4 2.0 %reshape.156 = f32[1024,128]{1,0:T(8,128)} reshape(f32[128,4,256]{2,1,0:T(4,128)} %copy.32) | data formatting | bytes 1048576 | tf_op jit(solution)/shard_map/reshape | solution.py:65
  74.4 4.9 %collective-permute-start.3 = (f32[1024,128]{1,0:T(8,128)}, f32[1024,128]{1,0:T(8,128)}, u32[]{:S(2)}, u32[]{:S(2)}) collective-permute-start(f32[1024,128]{1,0:T(8,128)} %reshape.156), channel_id=1, source_target_pairs={{508,0},{0,4},{4,8},{8,12},{12,16},{16,20},{20,24},{24,28},{28,32}... | collective-permute-start | bytes 1572872 | tf_op jit(solution)/shard_map/ppermute | solution.py:14
  79.3 2.1 %reshape.194 = f32[1024,128,1]{1,0,2:T(8,128)} reshape(f32[128,4,256]{2,1,0:T(4,128)} %copy.32) | data formatting | bytes 1048576 | tf_op jit(solution)/shard_map/reshape | solution.py:65
  81.4 1.9 %collective-permute-start.4 = (f32[1024,128]{1,0:T(8,128)}, f32[1024,128]{1,0:T(8,128)S(1)}, u32[]{:S(2)}, u32[]{:S(2)}) collective-permute-start(f32[1024,128]{1,0:T(8,128)} %reshape.156), channel_id=1, source_target_pairs={{4,0},{8,4},{12,8},{16,12},{20,16},{24,20},{28,24},{32,28},{36,32}... | collective-permute-start | bytes 1572872 | tf_op jit(solution)/shard_map/ppermute | solution.py:14
  83.3 2.4 %convolution_multiply_fusion = f32[6,128,128]{2,1,0:T(8,128)S(1)} fusion(f32[6,128,1024]{2,1,0:T(8,128)S(1)} %bitcast.40, f32[1024,128,1]{1,0,2:T(8,128)} %reshape.194, f32[6]{0:T(128)S(1)} %get-tuple-element.7), kind=kOutput, calls=%fused_computation.5 | convolution fusion | flops 604078080 | bytes 4063256 | tf_op jit(solution)/shard_map/dot_general | solution.py:79
  85.7 0.0 collective-permute-done.3
  85.7 2.4 %fusion.6 = f32[768,128]{1,0:T(8,128)S(1)} fusion(f32[768,1024]{1,0:T(8,128)S(1)} %broadcast_multiply_fusion, f32[1024,128]{1,0:T(8,128)} %collective-permute-done.3), kind=kOutput, calls=%fused_computation.31 | convolution fusion | flops 603979776 | bytes 4063232 | tf_op jit(solution)/shard_map/dot_general | solution.py:79
  88.2 6.0 %collective-permute-done.4 = f32[1024,128]{1,0:T(8,128)S(1)} collective-permute-done((f32[1024,128]{1,0:T(8,128)}, f32[1024,128]{1,0:T(8,128)S(1)}, u32[]{:S(2)}, u32[]{:S(2)}) %collective-permute-start.4) | collective-permute-done | bytes 524320 | tf_op jit(solution)/shard_map/ppermute | solution.py:14
  94.2 1.4 %fusion.7 = f32[768,128]{1,0:T(8,128)S(1)} fusion(f32[768,1024]{1,0:T(8,128)S(1)} %broadcast_multiply_fusion, f32[1024,128]{1,0:T(8,128)S(1)} %collective-permute-done.4), kind=kOutput, calls=%fused_computation.32 | convolution fusion | flops 603979776 | bytes 4063232 | tf_op jit(solution)/shard_map/dot_general | solution.py:79
  95.6 0.9 multiply_add_fusion
  (9 shorter events, 0.1 us)
Async XLA Ops:
  0.0 36.1 %copy-start = (s32[128]{0:T(128)S(1)}, s32[128]{0:T(128)}, u32[]{:S(2)}) copy-start(s32[128]{0:T(128)} %param.13) | copy-start | bytes 1540
  0.0 24.2 %copy-start.1 = (f32[2,64,1,128]{3,2,1,0:T(1,128)S(1)}, f32[2,64,1,128]{3,2,1,0:T(1,128)}, u32[]{:S(2)}) copy-start(f32[2,64,1,128]{3,2,1,0:T(1,128)} %param.8) | copy-start | bytes 196612
  0.0 34.7 %copy-start.2 = (s32[128,16]{0,1:T(8,128)S(1)}, s32[128,16]{0,1:T(8,128)}, u32[]{:S(2)}) copy-start(s32[128,16]{0,1:T(8,128)} %param.11) | copy-start | bytes 24580
  0.0 34.8 %copy-start.3 = (f32[128,16]{0,1:T(8,128)S(1)}, f32[128,16]{0,1:T(8,128)}, u32[]{:S(2)}) copy-start(f32[128,16]{0,1:T(8,128)} %param.12) | copy-start | bytes 24580
  0.0 36.8 %copy-start.4 = (f32[768]{0:T(1024)S(1)}, f32[768]{0:T(1024)}, u32[]{:S(2)}) copy-start(f32[768]{0:T(1024)} %param.10) | copy-start | bytes 9220
  3.1 51.4 %all-to-all-start = ((f32[512,1,512]{2,1,0:T(1,128)}), f32[512,1,512]{2,1,0:T(1,128)S(1)}, u32[]{:S(2)}, u32[]{:S(2)}) async-start(f32[512,1,512]{2,1,0:T(1,128)} %bitcast.9), calls=%async_computation | async-start | bytes 2097152 | tf_op jit(solution)/shard_map/all_to_all | solution.py:56
  24.2 12.7 %collective-permute-start = (f32[2,64,128]{2,1,0:T(8,128)S(1)}, f32[2,64,128]{2,1,0:T(8,128)S(1)}, u32[]{:S(2)}, u32[]{:S(2)}) collective-permute-start(f32[2,64,128]{2,1,0:T(8,128)S(1)} %bitcast.46), channel_id=1, source_target_pairs={{3,0},{0,1},{1,2},{2,3},{7,4},{4,5},{5,6},{6,7},{11,8},{8,9},{9,10... | collective-permute-start | bytes 196616 | tf_op jit(solution)/shard_map/ppermute | solution.py:14
  27.3 9.6 %collective-permute-start.1 = (f32[2,64,128]{2,1,0:T(8,128)S(1)}, f32[2,64,128]{2,1,0:T(8,128)S(1)}, u32[]{:S(2)}, u32[]{:S(2)}) collective-permute-start(f32[2,64,128]{2,1,0:T(8,128)S(1)} %bitcast.47), channel_id=1, source_target_pairs={{2,0},{3,1},{0,2},{1,3},{6,4},{7,5},{4,6},{5,7},{10,8},{11,9},{8,1... | collective-permute-start | bytes 196616 | tf_op jit(solution)/shard_map/ppermute | solution.py:14
  31.6 5.9 %collective-permute-start.2 = (f32[2,64,128]{2,1,0:T(8,128)S(1)}, f32[2,64,128]{2,1,0:T(8,128)S(1)}, u32[]{:S(2)}, u32[]{:S(2)}) collective-permute-start(f32[2,64,128]{2,1,0:T(8,128)S(1)} %bitcast.48), channel_id=1, source_target_pairs={{1,0},{2,1},{3,2},{0,3},{5,4},{6,5},{7,6},{4,7},{9,8},{10,9},{11,1... | collective-permute-start | bytes 196616 | tf_op jit(solution)/shard_map/ppermute | solution.py:14
  56.3 14.0 %all-to-all-start.1 = ((f32[128,4,256]{2,0,1:T(8,128)}), f32[128,4,256]{2,0,1:T(8,128)}, u32[]{:S(2)}, u32[]{:S(2)}) async-start(f32[128,4,256]{2,0,1:T(8,128)} %broadcast_in_dim.16), calls=%async_computation.1 | async-start | bytes 1048576 | tf_op jit(solution)/shard_map/all_to_all | solution.py:64
  74.4 11.3 %collective-permute-start.3 = (f32[1024,128]{1,0:T(8,128)}, f32[1024,128]{1,0:T(8,128)}, u32[]{:S(2)}, u32[]{:S(2)}) collective-permute-start(f32[1024,128]{1,0:T(8,128)} %reshape.156), channel_id=1, source_target_pairs={{508,0},{0,4},{4,8},{8,12},{12,16},{16,20},{20,24},{24,28},{28,32}... | collective-permute-start | bytes 1572872 | tf_op jit(solution)/shard_map/ppermute | solution.py:14
  81.4 12.8 %collective-permute-start.4 = (f32[1024,128]{1,0:T(8,128)}, f32[1024,128]{1,0:T(8,128)S(1)}, u32[]{:S(2)}, u32[]{:S(2)}) collective-permute-start(f32[1024,128]{1,0:T(8,128)} %reshape.156), channel_id=1, source_target_pairs={{4,0},{8,4},{12,8},{16,12},{20,16},{24,20},{28,24},{32,28},{36,32}... | collective-permute-start | bytes 1572872 | tf_op jit(solution)/shard_map/ppermute | solution.py:14

commit v14 on v9

--- a/solution.py
+++ b/solution.py
@@ -65,10 +65,20 @@
     region_index = lax.axis_index("dom")
     owned_rows = obs_pert.shape[0]
     owned_blocks = owned_rows // OBSB
-    behind = from_behind(summed, "mem", 1)
-    ahead = from_behind(summed, "mem", -1)
+    count = lax.axis_size("mem")
+    swap = [(i, i + 1 if i % 2 == 0 else i - 1) for i in range(count)]
+    cross = [(i, (i - 1) % count if i % 2 == 0 else (i + 1) % count) for i in range(count)]
+    near = lax.ppermute(summed, "mem", swap)
+    far = lax.ppermute(summed, "mem", cross)
     weight_rows = own_weights(
         obs_lists, block_taper, counts, column_index, region_index, owned_blocks, regions
+    )
+    even = column_index % 2 == 0
+    behind, ahead = far, near
+    weight_rows = (
+        jnp.where(even, weight_rows[0], weight_rows[2]),
+        weight_rows[1],
+        jnp.where(even, weight_rows[2], weight_rows[0]),
     )
     scale = (weighted_innovation / (M - 1))[:, None]
     rows = obs_pert * scale

time: 91.9 us -> 91.1 us (level)
  the two profiles are of different devices: /device:TPU:57 before, /device:TPU:2 now
where the time goes in v14:
time: 91.1 us; the launch traced here: 90.7 us
  starting transfers between devices  44 us (48%)
  waiting for transfers between devices  30 us (33%)
  local copies, waits for them, and re-layouts  8.13 us (9%)
  matrix products  5.02 us (6%)
  other arithmetic  3.33 us (4%)
    all_to_all x1, starting transfers between devices, body(): arrived = lax.all_to_all(grid, ('mem', 'dom'), 0, 0, tiled=True)  21.2 us
    all_to_all x1, waiting for transfers between devices, body(): arrived = lax.all_to_all(grid, ('mem', 'dom'), 0, 0, tiled=True)  13.5 us
    ppermute x3, starting transfers between devices, from_behind(): return lax.ppermute(block, axis, route)  12.1 us
    ppermute x1, waiting for transfers between devices, body(): far = lax.ppermute(summed, 'mem', cross)  7.75 us
    all_to_all x1, waiting for transfers between devices, gathered(): return lax.all_to_all(copies, axis, 0, 0, tiled=True)  6.28 us
    all_to_all x1, starting transfers between devices, gathered(): return lax.all_to_all(copies, axis, 0, 0, tiled=True)  6.08 us
    dot_general x3, matrix products, body(): jnp.dot(rows, source, precision=HIGH).reshape(owned_blocks, OBSB, -1)  4.17 us
    reshape x1, local copies, waits for them, and re-layouts, body(): grid = fcst_pert.reshape(leads, regions, pair, column_blocks, width)  3.06 us
  transfers between devices with their start and end apart: 7, of which 4 were waited for; matrix products, arithmetic and copies ran while one was open for 9% of the time, Pallas kernels for 0%

profile of v14, /device:TPU:2, one launch (start us, length us, event | category | flops | bytes accessed | tf_op | source)
XLA Modules:
  0.0 90.7 jit_solution(10772894466734583481)
XLA Ops:
  0.0 0.0 copy-start
  0.0 0.0 copy-start.1
  0.0 0.0 copy-start.2
  0.0 0.0 copy-start.3
  0.0 0.0 copy-start.4
  0.0 3.1 %copy.25 = f32[2,4,2,128,128]{4,2,0,1,3:T(2,128)} copy(f32[2,4,2,128,128]{4,3,2,1,0:T(8,128)} %bitcast.52) | data formatting | bytes 2097152 | tf_op jit(solution)/shard_map/reshape | solution.py:54
  3.1 21.2 %all-to-all-start = ((f32[512,1,512]{2,1,0:T(1,128)}), f32[512,1,512]{2,1,0:T(1,128)S(1)}, u32[]{:S(2)}, u32[]{:S(2)}) async-start(f32[512,1,512]{2,1,0:T(1,128)} %bitcast.9), calls=%async_computation | async-start | bytes 2097152 | tf_op jit(solution)/shard_map/all_to_all | solution.py:56
  24.3 0.0 copy-done.1
  24.3 3.4 %collective-permute-start = (f32[2,64,128]{2,1,0:T(8,128)S(1)}, f32[2,64,128]{2,1,0:T(8,128)S(1)}, u32[]{:S(2)}, u32[]{:S(2)}) collective-permute-start(f32[2,64,128]{2,1,0:T(8,128)S(1)} %bitcast.53), channel_id=1, source_target_pairs={{3,0},{0,1},{1,2},{2,3},{7,4},{4,5},{5,6},{6,7},{11,8},{8,9},{9,10... | collective-permute-start | bytes 196616 | tf_op jit(solution)/shard_map/ppermute | solution.py:14
  27.7 6.8 %collective-permute-start.1 = (f32[2,64,128]{2,1,0:T(8,128)S(1)}, f32[2,64,128]{2,1,0:T(8,128)S(1)}, u32[]{:S(2)}, u32[]{:S(2)}) collective-permute-start(f32[2,64,128]{2,1,0:T(8,128)S(1)} %bitcast.54), channel_id=1, source_target_pairs={{2,0},{3,1},{0,2},{1,3},{6,4},{7,5},{4,6},{5,7},{10,8},{11,9},{8,1... | collective-permute-start | bytes 196616 | tf_op jit(solution)/shard_map/ppermute | solution.py:14
  34.5 1.9 %collective-permute-start.2 = (f32[2,64,128]{2,1,0:T(8,128)S(1)}, f32[2,64,128]{2,1,0:T(8,128)S(1)}, u32[]{:S(2)}, u32[]{:S(2)}) collective-permute-start(f32[2,64,128]{2,1,0:T(8,128)S(1)} %bitcast.55), channel_id=1, source_target_pairs={{1,0},{2,1},{3,2},{0,3},{5,4},{6,5},{7,6},{4,7},{9,8},{10,9},{11,1... | collective-permute-start | bytes 196616 | tf_op jit(solution)/shard_map/ppermute | solution.py:14
  36.4 0.0 copy-done.2
  36.4 0.1 copy.31
  36.5 0.0 copy-done.3
  36.5 0.1 copy.32
  36.7 0.6 gather_fusion
  37.2 0.6 gather_fusion.2
  37.8 0.0 copy-done
  37.8 0.6 gather_fusion.1
  38.5 0.1 iota_compare_fusion
  38.5 0.0 copy-done.4
  38.5 0.0 collective-permute-done
  38.5 0.0 collective-permute-done.1
  38.6 2.5 %collective-permute-done.2 = f32[2,64,128]{2,1,0:T(8,128)S(1)} collective-permute-done((f32[2,64,128]{2,1,0:T(8,128)S(1)}, f32[2,64,128]{2,1,0:T(8,128)S(1)}, u32[]{:S(2)}, u32[]{:S(2)}) %collective-permute-start.2) | collective-permute-done | bytes 65568 | tf_op jit(solution)/shard_map/ppermute | solution.py:14
  41.1 0.7 scatter_fusion
  41.7 13.5 %all-to-all-done = f32[512,1,512]{2,1,0:T(1,128)S(1)} async-done(((f32[512,1,512]{2,1,0:T(1,128)}), f32[512,1,512]{2,1,0:T(1,128)S(1)}, u32[]{:S(2)}, u32[]{:S(2)}) %all-to-all-start) | async-done | bytes 1048608 | tf_op jit(solution)/shard_map/all_to_all | solution.py:56
  55.2 0.8 convolution_bitcast_fusion
  56.1 0.2 copy.29
  56.3 0.2 broadcast_in_dim.15
  56.4 0.8 broadcast_in_dim.16
  57.3 6.1 %all-to-all-start.1 = ((f32[4,256,128]{2,1,0:T(8,128)}), f32[4,256,128]{2,1,0:T(8,128)}, u32[]{:S(2)}, u32[]{:S(2)}) async-start(f32[4,256,128]{2,1,0:T(8,128)} %broadcast_in_dim.16), calls=%async_computation.1 | async-start | bytes 1048576 | tf_op jit(solution)/shard_map/all_to_all | solution.py:20
  63.3 0.2 select_reduce_fusion
  63.5 2.2 %broadcast_multiply_fusion = f32[768,1024]{1,0:T(8,128)S(1)} fusion(f32[768,1024]{1,0:T(8,128)} %param.9, f32[768]{0:T(1024)S(1)} %broadcast_multiply_fusion.1), kind=kLoop, calls=%fused_computation.4 | loop fusion | flops 786432 | bytes 6294528 | tf_op jit(solution)/shard_map/mul | solution.py:84
  65.7 6.3 %all-to-all-done.1 = f32[4,256,128]{2,1,0:T(8,128)} async-done(((f32[4,256,128]{2,1,0:T(8,128)}), f32[4,256,128]{2,1,0:T(8,128)}, u32[]{:S(2)}, u32[]{:S(2)}) %all-to-all-start.1) | async-done | bytes 524320 | tf_op jit(solution)/shard_map/all_to_all | solution.py:20
  71.9 1.2 %copy.30 = f32[128,4,2,128]{3,2,1,0:T(2,128)S(1)} copy(f32[128,4,2,128]{3,2,0,1:T(2,128)} %bitcast.15) | data formatting | bytes 1048576 | tf_op jit(solution)/shard_map/transpose | solution.py:63
  73.2 1.9 %collective-permute-start.3 = (f32[1024,128]{1,0:T(8,128)S(1)}, f32[1024,128]{1,0:T(8,128)S(1)}, u32[]{:S(2)}, u32[]{:S(2)}) collective-permute-start(f32[1024,128]{1,0:T(8,128)S(1)} %bitcast.47), channel_id=1, source_target_pairs={{0,508},{4,8},{8,4},{12,16},{16,12},{20,24},{24,20},{28,32},{32,28... | collective-permute-start | bytes 1572872 | tf_op jit(solution)/shard_map/ppermute | solution.py:72
  75.1 2.7 %collective-permute-start.4 = (f32[1024,128]{1,0:T(8,128)S(1)}, f32[1024,128]{1,0:T(8,128)S(1)}, u32[]{:S(2)}, u32[]{:S(2)}) collective-permute-start(f32[1024,128]{1,0:T(8,128)S(1)} %bitcast.48), channel_id=1, source_target_pairs={{0,4},{4,0},{8,12},{12,8},{16,20},{20,16},{24,28},{28,24},{32,36},... | collective-permute-start | bytes 1572872 | tf_op jit(solution)/shard_map/ppermute | solution.py:71
  77.8 1.4 %convolution_multiply_fusion = f32[6,128,128]{2,1,0:T(8,128)S(1)} fusion(f32[6,128,1024]{2,1,0:T(8,128)S(1)} %bitcast.45, f32[1024,128,1]{1,0,2:T(8,128)S(1)} %bitcast.49, f32[6]{0:T(128)S(1)} %get-tuple-element.6), kind=kOutput, calls=%fused_computation.5 | convolution fusion | flops 604078080 | bytes 4063256 | tf_op jit(solution)/shard_map/dot_general | solution.py:87
  79.2 7.8 %collective-permute-done.3 = f32[1024,128]{1,0:T(8,128)S(1)} collective-permute-done((f32[1024,128]{1,0:T(8,128)S(1)}, f32[1024,128]{1,0:T(8,128)S(1)}, u32[]{:S(2)}, u32[]{:S(2)}) %collective-permute-start.3) | collective-permute-done | bytes 524320 | tf_op jit(solution)/shard_map/ppermute | solution.py:72
  87.0 1.4 %fusion.8 = f32[768,128]{1,0:T(8,128)S(1)} fusion(f32[768,1024]{1,0:T(8,128)S(1)} %broadcast_multiply_fusion, f32[1024,128]{1,0:T(8,128)S(1)} %collective-permute-done.3), kind=kOutput, calls=%fused_computation.33 | convolution fusion | flops 603979776 | bytes 4063232 | tf_op jit(solution)/shard_map/dot_general | solution.py:87
  88.4 0.0 collective-permute-done.4
  88.4 1.4 %fusion.9 = f32[768,128]{1,0:T(8,128)S(1)} fusion(f32[768,1024]{1,0:T(8,128)S(1)} %broadcast_multiply_fusion, f32[1024,128]{1,0:T(8,128)S(1)} %collective-permute-done.4), kind=kOutput, calls=%fused_computation.34 | convolution fusion | flops 603979776 | bytes 4063232 | tf_op jit(solution)/shard_map/dot_general | solution.py:87
  89.8 0.9 multiply_add_fusion
  (8 shorter events, 0.1 us)
Async XLA Ops:
  0.0 37.8 %copy-start = (s32[128]{0:T(128)S(1)}, s32[128]{0:T(128)}, u32[]{:S(2)}) copy-start(s32[128]{0:T(128)} %param.13) | copy-start | bytes 1540
  0.0 24.3 %copy-start.1 = (f32[2,64,1,128]{3,2,1,0:T(1,128)S(1)}, f32[2,64,1,128]{3,2,1,0:T(1,128)}, u32[]{:S(2)}) copy-start(f32[2,64,1,128]{3,2,1,0:T(1,128)} %param.8) | copy-start | bytes 196612
  0.0 36.4 %copy-start.2 = (s32[128,16]{0,1:T(8,128)S(1)}, s32[128,16]{0,1:T(8,128)}, u32[]{:S(2)}) copy-start(s32[128,16]{0,1:T(8,128)} %param.11) | copy-start | bytes 24580
  0.0 36.5 %copy-start.3 = (f32[128,16]{0,1:T(8,128)S(1)}, f32[128,16]{0,1:T(8,128)}, u32[]{:S(2)}) copy-start(f32[128,16]{0,1:T(8,128)} %param.12) | copy-start | bytes 24580
  0.0 38.5 %copy-start.4 = (f32[768]{0:T(1024)S(1)}, f32[768]{0:T(1024)}, u32[]{:S(2)}) copy-start(f32[768]{0:T(1024)} %param.10) | copy-start | bytes 9220
  3.1 52.1 %all-to-all-start = ((f32[512,1,512]{2,1,0:T(1,128)}), f32[512,1,512]{2,1,0:T(1,128)S(1)}, u32[]{:S(2)}, u32[]{:S(2)}) async-start(f32[512,1,512]{2,1,0:T(1,128)} %bitcast.9), calls=%async_computation | async-start | bytes 2097152 | tf_op jit(solution)/shard_map/all_to_all | solution.py:56
  24.3 14.2 %collective-permute-start = (f32[2,64,128]{2,1,0:T(8,128)S(1)}, f32[2,64,128]{2,1,0:T(8,128)S(1)}, u32[]{:S(2)}, u32[]{:S(2)}) collective-permute-start(f32[2,64,128]{2,1,0:T(8,128)S(1)} %bitcast.53), channel_id=1, source_target_pairs={{3,0},{0,1},{1,2},{2,3},{7,4},{4,5},{5,6},{6,7},{11,8},{8,9},{9,10... | collective-permute-start | bytes 196616 | tf_op jit(solution)/shard_map/ppermute | solution.py:14
  27.7 10.9 %collective-permute-start.1 = (f32[2,64,128]{2,1,0:T(8,128)S(1)}, f32[2,64,128]{2,1,0:T(8,128)S(1)}, u32[]{:S(2)}, u32[]{:S(2)}) collective-permute-start(f32[2,64,128]{2,1,0:T(8,128)S(1)} %bitcast.54), channel_id=1, source_target_pairs={{2,0},{3,1},{0,2},{1,3},{6,4},{7,5},{4,6},{5,7},{10,8},{11,9},{8,1... | collective-permute-start | bytes 196616 | tf_op jit(solution)/shard_map/ppermute | solution.py:14
  34.5 6.5 %collective-permute-start.2 = (f32[2,64,128]{2,1,0:T(8,128)S(1)}, f32[2,64,128]{2,1,0:T(8,128)S(1)}, u32[]{:S(2)}, u32[]{:S(2)}) collective-permute-start(f32[2,64,128]{2,1,0:T(8,128)S(1)} %bitcast.55), channel_id=1, source_target_pairs={{1,0},{2,1},{3,2},{0,3},{5,4},{6,5},{7,6},{4,7},{9,8},{10,9},{11,1... | collective-permute-start | bytes 196616 | tf_op jit(solution)/shard_map/ppermute | solution.py:14
  57.3 14.7 %all-to-all-start.1 = ((f32[4,256,128]{2,1,0:T(8,128)}), f32[4,256,128]{2,1,0:T(8,128)}, u32[]{:S(2)}, u32[]{:S(2)}) async-start(f32[4,256,128]{2,1,0:T(8,128)} %broadcast_in_dim.16), calls=%async_computation.1 | async-start | bytes 1048576 | tf_op jit(solution)/shard_map/all_to_all | solution.py:20
  73.2 13.8 %collective-permute-start.3 = (f32[1024,128]{1,0:T(8,128)S(1)}, f32[1024,128]{1,0:T(8,128)S(1)}, u32[]{:S(2)}, u32[]{:S(2)}) collective-permute-start(f32[1024,128]{1,0:T(8,128)S(1)} %bitcast.47), channel_id=1, source_target_pairs={{0,508},{4,8},{8,4},{12,16},{16,12},{20,24},{24,20},{28,32},{32,28... | collective-permute-start | bytes 1572872 | tf_op jit(solution)/shard_map/ppermute | solution.py:72
  75.1 13.3 %collective-permute-start.4 = (f32[1024,128]{1,0:T(8,128)S(1)}, f32[1024,128]{1,0:T(8,128)S(1)}, u32[]{:S(2)}, u32[]{:S(2)}) collective-permute-start(f32[1024,128]{1,0:T(8,128)S(1)} %bitcast.48), channel_id=1, source_target_pairs={{0,4},{4,0},{8,12},{12,8},{16,20},{20,16},{24,28},{28,24},{32,36},... | collective-permute-start | bytes 1572872 | tf_op jit(solution)/shard_map/ppermute | solution.py:71

commit v15 on v14

--- a/solution.py
+++ b/solution.py
@@ -52,7 +52,7 @@
     width = columns // column_blocks
     pair = local_members // regions
     grid = fcst_pert.reshape(leads, regions, pair, column_blocks, width)
-    grid = jnp.transpose(grid, (3, 1, 0, 2, 4)).reshape(column_blocks * regions, -1)
+    grid = jnp.transpose(grid, (3, 1, 0, 2, 4)).reshape(column_blocks * regions, leads * pair, width)
     arrived = lax.all_to_all(grid, ("mem", "dom"), 0, 0, tiled=True)
     arrived = arrived.reshape(column_blocks, regions, leads, pair, width)
     targets = sensitivity.shape[1]

time: 91.1 us -> 91.7 us (level)
    reshape x0 -> x1, local copies, waits for them, and re-layouts: none -> 1.65 us  [body(): jnp.transpose(grid, (3, 1, 0, 2, 4))]
    reshape x1, local copies, waits for them, and re-layouts: 3.06 us -> 1.95 us  [body(): grid = fcst_pert.reshape(leads, regions, pair, column_blocks, width)]
where the time goes in v15:
time: 91.7 us; the launch traced here: 91.2 us
  starting transfers between devices  44 us (48%)
  waiting for transfers between devices  30 us (33%)
  local copies, waits for them, and re-layouts  8.67 us (9%)
  matrix products  5.02 us (5%)
  other arithmetic  3.33 us (4%)
    all_to_all x1, starting transfers between devices, body(): arrived = lax.all_to_all(grid, ('mem', 'dom'), 0, 0, tiled=True)  21.2 us
    all_to_all x1, waiting for transfers between devices, body(): arrived = lax.all_to_all(grid, ('mem', 'dom'), 0, 0, tiled=True)  13.5 us
    ppermute x3, starting transfers between devices, from_behind(): return lax.ppermute(block, axis, route)  12.1 us
    ppermute x1, waiting for transfers between devices, body(): far = lax.ppermute(summed, 'mem', cross)  7.75 us
    all_to_all x1, waiting for transfers between devices, gathered(): return lax.all_to_all(copies, axis, 0, 0, tiled=True)  6.28 us
    all_to_all x1, starting transfers between devices, gathered(): return lax.all_to_all(copies, axis, 0, 0, tiled=True)  6.08 us
    dot_general x3, matrix products, body(): jnp.dot(rows, source, precision=HIGH).reshape(owned_blocks, OBSB, -1)  4.17 us
    ppermute x1, starting transfers between devices, body(): near = lax.ppermute(summed, 'mem', swap)  2.72 us
  transfers between devices with their start and end apart: 7, of which 4 were waited for; matrix products, arithmetic and copies ran while one was open for 9% of the time, Pallas kernels for 0%

profile of v15, /device:TPU:2, one launch (start us, length us, event | category | flops | bytes accessed | tf_op | source)
XLA Modules:
  0.0 91.2 jit_solution(8206317625176425802)
XLA Ops:
  0.0 0.0 copy-start
  0.0 0.0 copy-start.1
  0.0 0.0 copy-start.2
  0.0 0.0 copy-start.3
  0.0 0.0 copy-start.4
  0.0 1.9 %copy.26 = f32[2,4,2,128,128]{4,1,3,2,0:T(4,128)S(1)} copy(f32[2,4,2,128,128]{4,3,2,1,0:T(8,128)} %bitcast.53) | data formatting | bytes 2097152 | tf_op jit(solution)/shard_map/reshape | solution.py:54
  2.0 1.7 %copy.27 = f32[512,4,128]{2,1,0:T(4,128)} copy(f32[512,4,128]{2,0,1:T(8,128)S(1)} %bitcast.47) | data formatting | bytes 2097152 | tf_op jit(solution)/shard_map/reshape | solution.py:55
  3.6 21.2 %all-to-all-start = ((f32[512,4,128]{2,1,0:T(4,128)}), f32[512,4,128]{2,1,0:T(4,128)S(1)}, u32[]{:S(2)}, u32[]{:S(2)}) async-start(f32[512,4,128]{2,1,0:T(4,128)} %copy.27), calls=%async_computation | async-start | bytes 2097152 | tf_op jit(solution)/shard_map/all_to_all | solution.py:56
  24.8 0.0 copy-done.1
  24.8 3.4 %collective-permute-start = (f32[2,64,128]{2,1,0:T(8,128)S(1)}, f32[2,64,128]{2,1,0:T(8,128)S(1)}, u32[]{:S(2)}, u32[]{:S(2)}) collective-permute-start(f32[2,64,128]{2,1,0:T(8,128)S(1)} %bitcast.54), channel_id=1, source_target_pairs={{3,0},{0,1},{1,2},{2,3},{7,4},{4,5},{5,6},{6,7},{11,8},{8,9},{9,10... | collective-permute-start | bytes 196616 | tf_op jit(solution)/shard_map/ppermute | solution.py:14
  28.2 6.8 %collective-permute-start.1 = (f32[2,64,128]{2,1,0:T(8,128)S(1)}, f32[2,64,128]{2,1,0:T(8,128)S(1)}, u32[]{:S(2)}, u32[]{:S(2)}) collective-permute-start(f32[2,64,128]{2,1,0:T(8,128)S(1)} %bitcast.55), channel_id=1, source_target_pairs={{2,0},{3,1},{0,2},{1,3},{6,4},{7,5},{4,6},{5,7},{10,8},{11,9},{8,1... | collective-permute-start | bytes 196616 | tf_op jit(solution)/shard_map/ppermute | solution.py:14
  35.0 1.9 %collective-permute-start.2 = (f32[2,64,128]{2,1,0:T(8,128)S(1)}, f32[2,64,128]{2,1,0:T(8,128)S(1)}, u32[]{:S(2)}, u32[]{:S(2)}) collective-permute-start(f32[2,64,128]{2,1,0:T(8,128)S(1)} %bitcast.56), channel_id=1, source_target_pairs={{1,0},{2,1},{3,2},{0,3},{5,4},{6,5},{7,6},{4,7},{9,8},{10,9},{11,1... | collective-permute-start | bytes 196616 | tf_op jit(solution)/shard_map/ppermute | solution.py:14
  37.0 0.0 copy-done.2
  37.0 0.1 copy.33
  37.1 0.0 copy-done.3
  37.1 0.1 copy.34
  37.2 0.6 gather_fusion
  37.8 0.6 gather_fusion.2
  38.3 0.0 copy-done
  38.3 0.6 gather_fusion.1
  39.0 0.1 iota_compare_fusion
  39.1 0.0 copy-done.4
  39.1 0.0 collective-permute-done
  39.1 0.0 collective-permute-done.1
  39.1 2.5 %collective-permute-done.2 = f32[2,64,128]{2,1,0:T(8,128)S(1)} collective-permute-done((f32[2,64,128]{2,1,0:T(8,128)S(1)}, f32[2,64,128]{2,1,0:T(8,128)S(1)}, u32[]{:S(2)}, u32[]{:S(2)}) %collective-permute-start.2) | collective-permute-done | bytes 65568 | tf_op jit(solution)/shard_map/ppermute | solution.py:14
  41.6 0.7 scatter_fusion
  42.3 13.5 %all-to-all-done = f32[512,4,128]{2,1,0:T(4,128)S(1)} async-done(((f32[512,4,128]{2,1,0:T(4,128)}), f32[512,4,128]{2,1,0:T(4,128)S(1)}, u32[]{:S(2)}, u32[]{:S(2)}) %all-to-all-start) | async-done | bytes 1048608 | tf_op jit(solution)/shard_map/all_to_all | solution.py:56
  55.8 0.8 convolution_bitcast_fusion
  56.6 0.2 copy.31
  56.8 0.2 broadcast_in_dim.15
  57.0 0.8 broadcast_in_dim.16
  57.8 6.1 %all-to-all-start.1 = ((f32[4,256,128]{2,1,0:T(8,128)}), f32[4,256,128]{2,1,0:T(8,128)}, u32[]{:S(2)}, u32[]{:S(2)}) async-start(f32[4,256,128]{2,1,0:T(8,128)} %broadcast_in_dim.16), calls=%async_computation.1 | async-start | bytes 1048576 | tf_op jit(solution)/shard_map/all_to_all | solution.py:20
  63.9 0.2 select_reduce_fusion
  64.0 2.2 %broadcast_multiply_fusion = f32[768,1024]{1,0:T(8,128)S(1)} fusion(f32[768,1024]{1,0:T(8,128)} %param.9, f32[768]{0:T(1024)S(1)} %broadcast_multiply_fusion.1), kind=kLoop, calls=%fused_computation.4 | loop fusion | flops 786432 | bytes 6294528 | tf_op jit(solution)/shard_map/mul | solution.py:84
  66.2 6.3 %all-to-all-done.1 = f32[4,256,128]{2,1,0:T(8,128)} async-done(((f32[4,256,128]{2,1,0:T(8,128)}), f32[4,256,128]{2,1,0:T(8,128)}, u32[]{:S(2)}, u32[]{:S(2)}) %all-to-all-start.1) | async-done | bytes 524320 | tf_op jit(solution)/shard_map/all_to_all | solution.py:20
  72.5 1.2 %copy.32 = f32[128,4,2,128]{3,2,1,0:T(2,128)S(1)} copy(f32[128,4,2,128]{3,2,0,1:T(2,128)} %bitcast.15) | data formatting | bytes 1048576 | tf_op jit(solution)/shard_map/transpose | solution.py:63
  73.7 1.9 %collective-permute-start.3 = (f32[1024,128]{1,0:T(8,128)S(1)}, f32[1024,128]{1,0:T(8,128)S(1)}, u32[]{:S(2)}, u32[]{:S(2)}) collective-permute-start(f32[1024,128]{1,0:T(8,128)S(1)} %bitcast.48), channel_id=1, source_target_pairs={{0,508},{4,8},{8,4},{12,16},{16,12},{20,24},{24,20},{28,32},{32,28... | collective-permute-start | bytes 1572872 | tf_op jit(solution)/shard_map/ppermute | solution.py:72
  75.7 2.7 %collective-permute-start.4 = (f32[1024,128]{1,0:T(8,128)S(1)}, f32[1024,128]{1,0:T(8,128)S(1)}, u32[]{:S(2)}, u32[]{:S(2)}) collective-permute-start(f32[1024,128]{1,0:T(8,128)S(1)} %bitcast.49), channel_id=1, source_target_pairs={{0,4},{4,0},{8,12},{12,8},{16,20},{20,16},{24,28},{28,24},{32,36},... | collective-permute-start | bytes 1572872 | tf_op jit(solution)/shard_map/ppermute | solution.py:71
  78.4 1.4 %convolution_multiply_fusion = f32[6,128,128]{2,1,0:T(8,128)S(1)} fusion(f32[6,128,1024]{2,1,0:T(8,128)S(1)} %bitcast.45, f32[1024,128,1]{1,0,2:T(8,128)S(1)} %bitcast.50, f32[6]{0:T(128)S(1)} %get-tuple-element.6), kind=kOutput, calls=%fused_computation.5 | convolution fusion | flops 604078080 | bytes 4063256 | tf_op jit(solution)/shard_map/dot_general | solution.py:87
  79.8 7.8 %collective-permute-done.3 = f32[1024,128]{1,0:T(8,128)S(1)} collective-permute-done((f32[1024,128]{1,0:T(8,128)S(1)}, f32[1024,128]{1,0:T(8,128)S(1)}, u32[]{:S(2)}, u32[]{:S(2)}) %collective-permute-start.3) | collective-permute-done | bytes 524320 | tf_op jit(solution)/shard_map/ppermute | solution.py:72
  87.5 1.4 %fusion.8 = f32[768,128]{1,0:T(8,128)S(1)} fusion(f32[768,1024]{1,0:T(8,128)S(1)} %broadcast_multiply_fusion, f32[1024,128]{1,0:T(8,128)S(1)} %collective-permute-done.3), kind=kOutput, calls=%fused_computation.33 | convolution fusion | flops 603979776 | bytes 4063232 | tf_op jit(solution)/shard_map/dot_general | solution.py:87
  88.9 0.0 collective-permute-done.4
  88.9 1.4 %fusion.9 = f32[768,128]{1,0:T(8,128)S(1)} fusion(f32[768,1024]{1,0:T(8,128)S(1)} %broadcast_multiply_fusion, f32[1024,128]{1,0:T(8,128)S(1)} %collective-permute-done.4), kind=kOutput, calls=%fused_computation.34 | convolution fusion | flops 603979776 | bytes 4063232 | tf_op jit(solution)/shard_map/dot_general | solution.py:87
  90.3 0.9 multiply_add_fusion
  (8 shorter events, 0.1 us)
Async XLA Ops:
  0.0 38.3 %copy-start = (s32[128]{0:T(128)S(1)}, s32[128]{0:T(128)}, u32[]{:S(2)}) copy-start(s32[128]{0:T(128)} %param.13) | copy-start | bytes 1540
  0.0 24.8 %copy-start.1 = (f32[2,64,1,128]{3,2,1,0:T(1,128)S(1)}, f32[2,64,1,128]{3,2,1,0:T(1,128)}, u32[]{:S(2)}) copy-start(f32[2,64,1,128]{3,2,1,0:T(1,128)} %param.8) | copy-start | bytes 196612
  0.0 37.0 %copy-start.2 = (s32[128,16]{0,1:T(8,128)S(1)}, s32[128,16]{0,1:T(8,128)}, u32[]{:S(2)}) copy-start(s32[128,16]{0,1:T(8,128)} %param.11) | copy-start | bytes 24580
  0.0 37.1 %copy-start.3 = (f32[128,16]{0,1:T(8,128)S(1)}, f32[128,16]{0,1:T(8,128)}, u32[]{:S(2)}) copy-start(f32[128,16]{0,1:T(8,128)} %param.12) | copy-start | bytes 24580
  0.0 39.1 %copy-start.4 = (f32[768]{0:T(1024)S(1)}, f32[768]{0:T(1024)}, u32[]{:S(2)}) copy-start(f32[768]{0:T(1024)} %param.10) | copy-start | bytes 9220
  3.6 52.1 %all-to-all-start = ((f32[512,4,128]{2,1,0:T(4,128)}), f32[512,4,128]{2,1,0:T(4,128)S(1)}, u32[]{:S(2)}, u32[]{:S(2)}) async-start(f32[512,4,128]{2,1,0:T(4,128)} %copy.27), calls=%async_computation | async-start | bytes 2097152 | tf_op jit(solution)/shard_map/all_to_all | solution.py:56
  24.8 14.2 %collective-permute-start = (f32[2,64,128]{2,1,0:T(8,128)S(1)}, f32[2,64,128]{2,1,0:T(8,128)S(1)}, u32[]{:S(2)}, u32[]{:S(2)}) collective-permute-start(f32[2,64,128]{2,1,0:T(8,128)S(1)} %bitcast.54), channel_id=1, source_target_pairs={{3,0},{0,1},{1,2},{2,3},{7,4},{4,5},{5,6},{6,7},{11,8},{8,9},{9,10... | collective-permute-start | bytes 196616 | tf_op jit(solution)/shard_map/ppermute | solution.py:14
  28.2 10.9 %collective-permute-start.1 = (f32[2,64,128]{2,1,0:T(8,128)S(1)}, f32[2,64,128]{2,1,0:T(8,128)S(1)}, u32[]{:S(2)}, u32[]{:S(2)}) collective-permute-start(f32[2,64,128]{2,1,0:T(8,128)S(1)} %bitcast.55), channel_id=1, source_target_pairs={{2,0},{3,1},{0,2},{1,3},{6,4},{7,5},{4,6},{5,7},{10,8},{11,9},{8,1... | collective-permute-start | bytes 196616 | tf_op jit(solution)/shard_map/ppermute | solution.py:14
  35.0 6.5 %collective-permute-start.2 = (f32[2,64,128]{2,1,0:T(8,128)S(1)}, f32[2,64,128]{2,1,0:T(8,128)S(1)}, u32[]{:S(2)}, u32[]{:S(2)}) collective-permute-start(f32[2,64,128]{2,1,0:T(8,128)S(1)} %bitcast.56), channel_id=1, source_target_pairs={{1,0},{2,1},{3,2},{0,3},{5,4},{6,5},{7,6},{4,7},{9,8},{10,9},{11,1... | collective-permute-start | bytes 196616 | tf_op jit(solution)/shard_map/ppermute | solution.py:14
  57.8 14.7 %all-to-all-start.1 = ((f32[4,256,128]{2,1,0:T(8,128)}), f32[4,256,128]{2,1,0:T(8,128)}, u32[]{:S(2)}, u32[]{:S(2)}) async-start(f32[4,256,128]{2,1,0:T(8,128)} %broadcast_in_dim.16), calls=%async_computation.1 | async-start | bytes 1048576 | tf_op jit(solution)/shard_map/all_to_all | solution.py:20
  73.7 13.8 %collective-permute-start.3 = (f32[1024,128]{1,0:T(8,128)S(1)}, f32[1024,128]{1,0:T(8,128)S(1)}, u32[]{:S(2)}, u32[]{:S(2)}) collective-permute-start(f32[1024,128]{1,0:T(8,128)S(1)} %bitcast.48), channel_id=1, source_target_pairs={{0,508},{4,8},{8,4},{12,16},{16,12},{20,24},{24,20},{28,32},{32,28... | collective-permute-start | bytes 1572872 | tf_op jit(solution)/shard_map/ppermute | solution.py:72
  75.7 13.3 %collective-permute-start.4 = (f32[1024,128]{1,0:T(8,128)S(1)}, f32[1024,128]{1,0:T(8,128)S(1)}, u32[]{:S(2)}, u32[]{:S(2)}) collective-permute-start(f32[1024,128]{1,0:T(8,128)S(1)} %bitcast.49), channel_id=1, source_target_pairs={{0,4},{4,0},{8,12},{12,8},{16,20},{20,16},{24,28},{28,24},{32,36},... | collective-permute-start | bytes 1572872 | tf_op jit(solution)/shard_map/ppermute | solution.py:71

commit v16 on v14

--- a/solution.py
+++ b/solution.py
@@ -68,8 +68,8 @@
     count = lax.axis_size("mem")
     swap = [(i, i + 1 if i % 2 == 0 else i - 1) for i in range(count)]
     cross = [(i, (i - 1) % count if i % 2 == 0 else (i + 1) % count) for i in range(count)]
+    far = lax.ppermute(summed, "mem", cross)
     near = lax.ppermute(summed, "mem", swap)
-    far = lax.ppermute(summed, "mem", cross)
     weight_rows = own_weights(
         obs_lists, block_taper, counts, column_index, region_index, owned_blocks, regions
     )

time: 91.1 us -> 91.1 us (level)
  no operation moved by 1% of the time
where the time goes in v16:
time: 91.1 us; the launch traced here: 90.7 us
  starting transfers between devices  44 us (48%)
  waiting for transfers between devices  30 us (33%)
  local copies, waits for them, and re-layouts  8.13 us (9%)
  matrix products  5.02 us (6%)
  other arithmetic  3.33 us (4%)
    all_to_all x1, starting transfers between devices, body(): arrived = lax.all_to_all(grid, ('mem', 'dom'), 0, 0, tiled=True)  21.2 us
    all_to_all x1, waiting for transfers between devices, body(): arrived = lax.all_to_all(grid, ('mem', 'dom'), 0, 0, tiled=True)  13.5 us
    ppermute x3, starting transfers between devices, from_behind(): return lax.ppermute(block, axis, route)  12.1 us
    ppermute x1, waiting for transfers between devices, body(): far = lax.ppermute(summed, 'mem', cross)  7.75 us
    all_to_all x1, waiting for transfers between devices, gathered(): return lax.all_to_all(copies, axis, 0, 0, tiled=True)  6.28 us
    all_to_all x1, starting transfers between devices, gathered(): return lax.all_to_all(copies, axis, 0, 0, tiled=True)  6.08 us
    dot_general x3, matrix products, body(): jnp.dot(rows, source, precision=HIGH).reshape(owned_blocks, OBSB, -1)  4.17 us
    reshape x1, local copies, waits for them, and re-layouts, body(): grid = fcst_pert.reshape(leads, regions, pair, column_blocks, width)  3.06 us
  transfers between devices with their start and end apart: 7, of which 4 were waited for; matrix products, arithmetic and copies ran while one was open for 9% of the time, Pallas kernels for 0%

profile of v16, /device:TPU:2, one launch (start us, length us, event | category | flops | bytes accessed | tf_op | source)
XLA Modules:
  0.0 90.7 jit_solution(10772894466734583481)
XLA Ops:
  0.0 0.0 copy-start
  0.0 0.0 copy-start.1
  0.0 0.0 copy-start.2
  0.0 0.0 copy-start.3
  0.0 0.0 copy-start.4
  0.0 3.1 %copy.25 = f32[2,4,2,128,128]{4,2,0,1,3:T(2,128)} copy(f32[2,4,2,128,128]{4,3,2,1,0:T(8,128)} %bitcast.52) | data formatting | bytes 2097152 | tf_op jit(solution)/shard_map/reshape | solution.py:54
  3.1 21.2 %all-to-all-start = ((f32[512,1,512]{2,1,0:T(1,128)}), f32[512,1,512]{2,1,0:T(1,128)S(1)}, u32[]{:S(2)}, u32[]{:S(2)}) async-start(f32[512,1,512]{2,1,0:T(1,128)} %bitcast.9), calls=%async_computation | async-start | bytes 2097152 | tf_op jit(solution)/shard_map/all_to_all | solution.py:56
  24.3 0.0 copy-done.1
  24.3 3.4 %collective-permute-start = (f32[2,64,128]{2,1,0:T(8,128)S(1)}, f32[2,64,128]{2,1,0:T(8,128)S(1)}, u32[]{:S(2)}, u32[]{:S(2)}) collective-permute-start(f32[2,64,128]{2,1,0:T(8,128)S(1)} %bitcast.53), channel_id=1, source_target_pairs={{3,0},{0,1},{1,2},{2,3},{7,4},{4,5},{5,6},{6,7},{11,8},{8,9},{9,10... | collective-permute-start | bytes 196616 | tf_op jit(solution)/shard_map/ppermute | solution.py:14
  27.7 6.8 %collective-permute-start.1 = (f32[2,64,128]{2,1,0:T(8,128)S(1)}, f32[2,64,128]{2,1,0:T(8,128)S(1)}, u32[]{:S(2)}, u32[]{:S(2)}) collective-permute-start(f32[2,64,128]{2,1,0:T(8,128)S(1)} %bitcast.54), channel_id=1, source_target_pairs={{2,0},{3,1},{0,2},{1,3},{6,4},{7,5},{4,6},{5,7},{10,8},{11,9},{8,1... | collective-permute-start | bytes 196616 | tf_op jit(solution)/shard_map/ppermute | solution.py:14
  34.5 1.9 %collective-permute-start.2 = (f32[2,64,128]{2,1,0:T(8,128)S(1)}, f32[2,64,128]{2,1,0:T(8,128)S(1)}, u32[]{:S(2)}, u32[]{:S(2)}) collective-permute-start(f32[2,64,128]{2,1,0:T(8,128)S(1)} %bitcast.55), channel_id=1, source_target_pairs={{1,0},{2,1},{3,2},{0,3},{5,4},{6,5},{7,6},{4,7},{9,8},{10,9},{11,1... | collective-permute-start | bytes 196616 | tf_op jit(solution)/shard_map/ppermute | solution.py:14
  36.4 0.0 copy-done.2
  36.4 0.1 copy.31
  36.5 0.0 copy-done.3
  36.5 0.1 copy.32
  36.7 0.6 gather_fusion
  37.2 0.6 gather_fusion.2
  37.8 0.0 copy-done
  37.8 0.6 gather_fusion.1
  38.5 0.1 iota_compare_fusion
  38.5 0.0 copy-done.4
  38.5 0.0 collective-permute-done
  38.5 0.0 collective-permute-done.1
  38.6 2.5 %collective-permute-done.2 = f32[2,64,128]{2,1,0:T(8,128)S(1)} collective-permute-done((f32[2,64,128]{2,1,0:T(8,128)S(1)}, f32[2,64,128]{2,1,0:T(8,128)S(1)}, u32[]{:S(2)}, u32[]{:S(2)}) %collective-permute-start.2) | collective-permute-done | bytes 65568 | tf_op jit(solution)/shard_map/ppermute | solution.py:14
  41.1 0.7 scatter_fusion
  41.7 13.5 %all-to-all-done = f32[512,1,512]{2,1,0:T(1,128)S(1)} async-done(((f32[512,1,512]{2,1,0:T(1,128)}), f32[512,1,512]{2,1,0:T(1,128)S(1)}, u32[]{:S(2)}, u32[]{:S(2)}) %all-to-all-start) | async-done | bytes 1048608 | tf_op jit(solution)/shard_map/all_to_all | solution.py:56
  55.2 0.8 convolution_bitcast_fusion
  56.1 0.2 copy.29
  56.3 0.2 broadcast_in_dim.15
  56.4 0.8 broadcast_in_dim.16
  57.3 6.1 %all-to-all-start.1 = ((f32[4,256,128]{2,1,0:T(8,128)}), f32[4,256,128]{2,1,0:T(8,128)}, u32[]{:S(2)}, u32[]{:S(2)}) async-start(f32[4,256,128]{2,1,0:T(8,128)} %broadcast_in_dim.16), calls=%async_computation.1 | async-start | bytes 1048576 | tf_op jit(solution)/shard_map/all_to_all | solution.py:20
  63.3 0.2 select_reduce_fusion
  63.5 2.2 %broadcast_multiply_fusion = f32[768,1024]{1,0:T(8,128)S(1)} fusion(f32[768,1024]{1,0:T(8,128)} %param.9, f32[768]{0:T(1024)S(1)} %broadcast_multiply_fusion.1), kind=kLoop, calls=%fused_computation.4 | loop fusion | flops 786432 | bytes 6294528 | tf_op jit(solution)/shard_map/mul | solution.py:84
  65.7 6.3 %all-to-all-done.1 = f32[4,256,128]{2,1,0:T(8,128)} async-done(((f32[4,256,128]{2,1,0:T(8,128)}), f32[4,256,128]{2,1,0:T(8,128)}, u32[]{:S(2)}, u32[]{:S(2)}) %all-to-all-start.1) | async-done | bytes 524320 | tf_op jit(solution)/shard_map/all_to_all | solution.py:20
  71.9 1.2 %copy.30 = f32[128,4,2,128]{3,2,1,0:T(2,128)S(1)} copy(f32[128,4,2,128]{3,2,0,1:T(2,128)} %bitcast.15) | data formatting | bytes 1048576 | tf_op jit(solution)/shard_map/transpose | solution.py:63
  73.2 1.9 %collective-permute-start.3 = (f32[1024,128]{1,0:T(8,128)S(1)}, f32[1024,128]{1,0:T(8,128)S(1)}, u32[]{:S(2)}, u32[]{:S(2)}) collective-permute-start(f32[1024,128]{1,0:T(8,128)S(1)} %bitcast.47), channel_id=1, source_target_pairs={{0,508},{4,8},{8,4},{12,16},{16,12},{20,24},{24,20},{28,32},{32,28... | collective-permute-start | bytes 1572872 | tf_op jit(solution)/shard_map/ppermute | solution.py:71
  75.1 2.7 %collective-permute-start.4 = (f32[1024,128]{1,0:T(8,128)S(1)}, f32[1024,128]{1,0:T(8,128)S(1)}, u32[]{:S(2)}, u32[]{:S(2)}) collective-permute-start(f32[1024,128]{1,0:T(8,128)S(1)} %bitcast.48), channel_id=1, source_target_pairs={{0,4},{4,0},{8,12},{12,8},{16,20},{20,16},{24,28},{28,24},{32,36},... | collective-permute-start | bytes 1572872 | tf_op jit(solution)/shard_map/ppermute | solution.py:72
  77.8 1.4 %convolution_multiply_fusion = f32[6,128,128]{2,1,0:T(8,128)S(1)} fusion(f32[6,128,1024]{2,1,0:T(8,128)S(1)} %bitcast.45, f32[1024,128,1]{1,0,2:T(8,128)S(1)} %bitcast.49, f32[6]{0:T(128)S(1)} %get-tuple-element.6), kind=kOutput, calls=%fused_computation.5 | convolution fusion | flops 604078080 | bytes 4063256 | tf_op jit(solution)/shard_map/dot_general | solution.py:87
  79.2 7.8 %collective-permute-done.3 = f32[1024,128]{1,0:T(8,128)S(1)} collective-permute-done((f32[1024,128]{1,0:T(8,128)S(1)}, f32[1024,128]{1,0:T(8,128)S(1)}, u32[]{:S(2)}, u32[]{:S(2)}) %collective-permute-start.3) | collective-permute-done | bytes 524320 | tf_op jit(solution)/shard_map/ppermute | solution.py:71
  87.0 1.4 %fusion.8 = f32[768,128]{1,0:T(8,128)S(1)} fusion(f32[768,1024]{1,0:T(8,128)S(1)} %broadcast_multiply_fusion, f32[1024,128]{1,0:T(8,128)S(1)} %collective-permute-done.3), kind=kOutput, calls=%fused_computation.33 | convolution fusion | flops 603979776 | bytes 4063232 | tf_op jit(solution)/shard_map/dot_general | solution.py:87
  88.4 0.0 collective-permute-done.4
  88.4 1.4 %fusion.9 = f32[768,128]{1,0:T(8,128)S(1)} fusion(f32[768,1024]{1,0:T(8,128)S(1)} %broadcast_multiply_fusion, f32[1024,128]{1,0:T(8,128)S(1)} %collective-permute-done.4), kind=kOutput, calls=%fused_computation.34 | convolution fusion | flops 603979776 | bytes 4063232 | tf_op jit(solution)/shard_map/dot_general | solution.py:87
  89.8 0.9 multiply_add_fusion
  (8 shorter events, 0.1 us)
Async XLA Ops:
  0.0 37.8 %copy-start = (s32[128]{0:T(128)S(1)}, s32[128]{0:T(128)}, u32[]{:S(2)}) copy-start(s32[128]{0:T(128)} %param.13) | copy-start | bytes 1540
  0.0 24.3 %copy-start.1 = (f32[2,64,1,128]{3,2,1,0:T(1,128)S(1)}, f32[2,64,1,128]{3,2,1,0:T(1,128)}, u32[]{:S(2)}) copy-start(f32[2,64,1,128]{3,2,1,0:T(1,128)} %param.8) | copy-start | bytes 196612
  0.0 36.4 %copy-start.2 = (s32[128,16]{0,1:T(8,128)S(1)}, s32[128,16]{0,1:T(8,128)}, u32[]{:S(2)}) copy-start(s32[128,16]{0,1:T(8,128)} %param.11) | copy-start | bytes 24580
  0.0 36.5 %copy-start.3 = (f32[128,16]{0,1:T(8,128)S(1)}, f32[128,16]{0,1:T(8,128)}, u32[]{:S(2)}) copy-start(f32[128,16]{0,1:T(8,128)} %param.12) | copy-start | bytes 24580
  0.0 38.5 %copy-start.4 = (f32[768]{0:T(1024)S(1)}, f32[768]{0:T(1024)}, u32[]{:S(2)}) copy-start(f32[768]{0:T(1024)} %param.10) | copy-start | bytes 9220
  3.1 52.1 %all-to-all-start = ((f32[512,1,512]{2,1,0:T(1,128)}), f32[512,1,512]{2,1,0:T(1,128)S(1)}, u32[]{:S(2)}, u32[]{:S(2)}) async-start(f32[512,1,512]{2,1,0:T(1,128)} %bitcast.9), calls=%async_computation | async-start | bytes 2097152 | tf_op jit(solution)/shard_map/all_to_all | solution.py:56
  24.3 14.2 %collective-permute-start = (f32[2,64,128]{2,1,0:T(8,128)S(1)}, f32[2,64,128]{2,1,0:T(8,128)S(1)}, u32[]{:S(2)}, u32[]{:S(2)}) collective-permute-start(f32[2,64,128]{2,1,0:T(8,128)S(1)} %bitcast.53), channel_id=1, source_target_pairs={{3,0},{0,1},{1,2},{2,3},{7,4},{4,5},{5,6},{6,7},{11,8},{8,9},{9,10... | collective-permute-start | bytes 196616 | tf_op jit(solution)/shard_map/ppermute | solution.py:14
  27.7 10.9 %collective-permute-start.1 = (f32[2,64,128]{2,1,0:T(8,128)S(1)}, f32[2,64,128]{2,1,0:T(8,128)S(1)}, u32[]{:S(2)}, u32[]{:S(2)}) collective-permute-start(f32[2,64,128]{2,1,0:T(8,128)S(1)} %bitcast.54), channel_id=1, source_target_pairs={{2,0},{3,1},{0,2},{1,3},{6,4},{7,5},{4,6},{5,7},{10,8},{11,9},{8,1... | collective-permute-start | bytes 196616 | tf_op jit(solution)/shard_map/ppermute | solution.py:14
  34.5 6.5 %collective-permute-start.2 = (f32[2,64,128]{2,1,0:T(8,128)S(1)}, f32[2,64,128]{2,1,0:T(8,128)S(1)}, u32[]{:S(2)}, u32[]{:S(2)}) collective-permute-start(f32[2,64,128]{2,1,0:T(8,128)S(1)} %bitcast.55), channel_id=1, source_target_pairs={{1,0},{2,1},{3,2},{0,3},{5,4},{6,5},{7,6},{4,7},{9,8},{10,9},{11,1... | collective-permute-start | bytes 196616 | tf_op jit(solution)/shard_map/ppermute | solution.py:14
  57.3 14.7 %all-to-all-start.1 = ((f32[4,256,128]{2,1,0:T(8,128)}), f32[4,256,128]{2,1,0:T(8,128)}, u32[]{:S(2)}, u32[]{:S(2)}) async-start(f32[4,256,128]{2,1,0:T(8,128)} %broadcast_in_dim.16), calls=%async_computation.1 | async-start | bytes 1048576 | tf_op jit(solution)/shard_map/all_to_all | solution.py:20
  73.2 13.8 %collective-permute-start.3 = (f32[1024,128]{1,0:T(8,128)S(1)}, f32[1024,128]{1,0:T(8,128)S(1)}, u32[]{:S(2)}, u32[]{:S(2)}) collective-permute-start(f32[1024,128]{1,0:T(8,128)S(1)} %bitcast.47), channel_id=1, source_target_pairs={{0,508},{4,8},{8,4},{12,16},{16,12},{20,24},{24,20},{28,32},{32,28... | collective-permute-start | bytes 1572872 | tf_op jit(solution)/shard_map/ppermute | solution.py:71
  75.1 13.3 %collective-permute-start.4 = (f32[1024,128]{1,0:T(8,128)S(1)}, f32[1024,128]{1,0:T(8,128)S(1)}, u32[]{:S(2)}, u32[]{:S(2)}) collective-permute-start(f32[1024,128]{1,0:T(8,128)S(1)} %bitcast.48), channel_id=1, source_target_pairs={{0,4},{4,0},{8,12},{12,8},{16,20},{20,16},{24,28},{28,24},{32,36},... | collective-permute-start | bytes 1572872 | tf_op jit(solution)/shard_map/ppermute | solution.py:72

commit v17 on v16

--- a/solution.py
+++ b/solution.py
@@ -82,10 +82,12 @@
     )
     scale = (weighted_innovation / (M - 1))[:, None]
     rows = obs_pert * scale
-    result = 0
-    for source, weights in zip((behind, summed, ahead), weight_rows):
-        product = jnp.dot(rows, source, precision=HIGH).reshape(owned_blocks, OBSB, -1)
-        result = result + product * weights[:, None, None]
+    own = jnp.dot(rows, summed, precision=HIGH).reshape(owned_blocks, OBSB, -1)
+    rows = rows.reshape(owned_blocks, OBSB, -1)
+    others = weight_rows[0][:, None, None] * behind[None] + weight_rows[2][:, None, None] * ahead[None]
+    result = own * weight_rows[1][:, None, None] + jnp.einsum(
+        "irk,ikt->irt", rows, others, precision=HIGH
+    )
     return result.reshape(owned_rows, -1)
 
 

time: 91.1 us -> 90.3 us (level)
    all_to_all x1, waiting for transfers between devices: 13.5 us -> 15.1 us  [body(): arrived = lax.all_to_all(grid, ('mem', 'dom'), 0, 0, tiled=True)]
    ppermute x3, waiting for transfers between devices: 2.47 us -> 1.46 us  [from_behind(): return lax.ppermute(block, axis, route)]
    dot_general x3 -> x2, matrix products: 4.17 us -> 4.23 us  [the longest x1 2.84 us: body(): jnp.einsum('irk,ikt->irt', rows, others, precision=HIGH)]
  transfers between devices with their start and end apart: 7 -> 7, of which waited for: 4 -> 5; matrix products, arithmetic and copies ran while one was open for 9% -> 7% of each run, Pallas kernels for 0% -> 0%
where the time goes in v17:
time: 90.3 us; the launch traced here: 89.8 us
  starting transfers between devices  43.4 us (48%)
  waiting for transfers between devices  30.6 us (34%)
  local copies, waits for them, and re-layouts  8.15 us (9%)
  matrix products  5.08 us (6%)
  other arithmetic  2.45 us (3%)
    all_to_all x1, starting transfers between devices, body(): arrived = lax.all_to_all(grid, ('mem', 'dom'), 0, 0, tiled=True)  21.2 us
    all_to_all x1, waiting for transfers between devices, body(): arrived = lax.all_to_all(grid, ('mem', 'dom'), 0, 0, tiled=True)  15.1 us
    ppermute x3, starting transfers between devices, from_behind(): return lax.ppermute(block, axis, route)  11.5 us
    ppermute x1, waiting for transfers between devices, body(): far = lax.ppermute(summed, 'mem', cross)  7.75 us
    all_to_all x1, waiting for transfers between devices, gathered(): return lax.all_to_all(copies, axis, 0, 0, tiled=True)  6.27 us
    all_to_all x1, starting transfers between devices, gathered(): return lax.all_to_all(copies, axis, 0, 0, tiled=True)  6.08 us
    reshape x1, local copies, waits for them, and re-layouts, body(): grid = fcst_pert.reshape(leads, regions, pair, column_blocks, width)  3.07 us
    dot_general x1, matrix products, body(): jnp.einsum('irk,ikt->irt', rows, others, precision=HIGH)  2.84 us
  transfers between devices with their start and end apart: 7, of which 5 were waited for; matrix products, arithmetic and copies ran while one was open for 7% of the time, Pallas kernels for 0%

profile of v17, /device:TPU:2, one launch (start us, length us, event | category | flops | bytes accessed | tf_op | source)
XLA Modules:
  0.0 89.8 jit_solution(11659768277608475178)
XLA Ops:
  0.0 0.0 copy-start
  0.0 0.0 copy-start.1
  0.0 0.0 copy-start.2
  0.0 0.0 copy-start.3
  0.0 0.0 copy-start.4
  0.0 3.1 %copy.25 = f32[2,4,2,128,128]{4,2,0,1,3:T(2,128)} copy(f32[2,4,2,128,128]{4,3,2,1,0:T(8,128)} %bitcast.47) | data formatting | bytes 2097152 | tf_op jit(solution)/shard_map/reshape | solution.py:54
  3.1 21.2 %all-to-all-start = ((f32[512,1,512]{2,1,0:T(1,128)}), f32[512,1,512]{2,1,0:T(1,128)S(1)}, u32[]{:S(2)}, u32[]{:S(2)}) async-start(f32[512,1,512]{2,1,0:T(1,128)} %bitcast.10), calls=%async_computation | async-start | bytes 2097152 | tf_op jit(solution)/shard_map/all_to_all | solution.py:56
  24.3 0.0 copy-done.1
  24.3 6.2 %collective-permute-start.2 = (f32[2,64,128]{2,1,0:T(8,128)S(1)}, f32[2,64,128]{2,1,0:T(8,128)S(1)}, u32[]{:S(2)}, u32[]{:S(2)}) collective-permute-start(f32[2,64,128]{2,1,0:T(8,128)S(1)} %bitcast.48), channel_id=1, source_target_pairs={{1,0},{2,1},{3,2},{0,3},{5,4},{6,5},{7,6},{4,7},{9,8},{10,9},{11,1... | collective-permute-start | bytes 196616 | tf_op jit(solution)/shard_map/ppermute | solution.py:14
  30.5 1.9 %collective-permute-start.1 = (f32[2,64,128]{2,1,0:T(8,128)S(1)}, f32[2,64,128]{2,1,0:T(8,128)S(1)}, u32[]{:S(2)}, u32[]{:S(2)}) collective-permute-start(f32[2,64,128]{2,1,0:T(8,128)S(1)} %bitcast.49), channel_id=1, source_target_pairs={{2,0},{3,1},{0,2},{1,3},{6,4},{7,5},{4,6},{5,7},{10,8},{11,9},{8,1... | collective-permute-start | bytes 196616 | tf_op jit(solution)/shard_map/ppermute | solution.py:14
  32.5 3.4 %collective-permute-start = (f32[2,64,128]{2,1,0:T(8,128)S(1)}, f32[2,64,128]{2,1,0:T(8,128)S(1)}, u32[]{:S(2)}, u32[]{:S(2)}) collective-permute-start(f32[2,64,128]{2,1,0:T(8,128)S(1)} %bitcast.50), channel_id=1, source_target_pairs={{3,0},{0,1},{1,2},{2,3},{7,4},{4,5},{5,6},{6,7},{11,8},{8,9},{9,10... | collective-permute-start | bytes 196616 | tf_op jit(solution)/shard_map/ppermute | solution.py:14
  35.8 0.0 copy-done.2
  35.9 0.1 copy.31
  36.0 0.0 copy-done
  36.0 0.6 gather_fusion.1
  36.6 0.6 gather_fusion
  37.2 0.0 copy-done.3
  37.2 0.1 copy.32
  37.3 0.6 gather_fusion.2
  37.9 0.1 iota_compare_fusion
  38.0 0.0 copy-done.4
  38.0 0.0 collective-permute-done.2
  38.0 0.9 collective-permute-done.1
  38.8 0.6 collective-permute-done
  39.5 0.7 scatter_fusion
  40.2 15.1 %all-to-all-done = f32[512,1,512]{2,1,0:T(1,128)S(1)} async-done(((f32[512,1,512]{2,1,0:T(1,128)}), f32[512,1,512]{2,1,0:T(1,128)S(1)}, u32[]{:S(2)}, u32[]{:S(2)}) %all-to-all-start) | async-done | bytes 1048608 | tf_op jit(solution)/shard_map/all_to_all | solution.py:56
  55.2 0.8 convolution_bitcast_fusion
  56.1 0.2 copy.29
  56.3 0.2 broadcast_in_dim.15
  56.5 0.8 broadcast_in_dim.16
  57.3 6.1 %all-to-all-start.1 = ((f32[4,256,128]{2,1,0:T(8,128)}), f32[4,256,128]{2,1,0:T(8,128)}, u32[]{:S(2)}, u32[]{:S(2)}) async-start(f32[4,256,128]{2,1,0:T(8,128)} %broadcast_in_dim.16), calls=%async_computation.1 | async-start | bytes 1048576 | tf_op jit(solution)/shard_map/all_to_all | solution.py:20
  63.4 0.2 select_reduce_fusion
  63.5 2.2 %broadcast_multiply_fusion = f32[768,1024]{1,0:T(8,128)S(1)} fusion(f32[768,1024]{1,0:T(8,128)} %param.9, f32[768]{0:T(1024)S(1)} %broadcast_multiply_fusion.1), kind=kLoop, calls=%fused_computation.12 | loop fusion | flops 786432 | bytes 6294528 | tf_op jit(solution)/shard_map/mul | solution.py:84
  65.7 6.3 %all-to-all-done.1 = f32[4,256,128]{2,1,0:T(8,128)} async-done(((f32[4,256,128]{2,1,0:T(8,128)}), f32[4,256,128]{2,1,0:T(8,128)}, u32[]{:S(2)}, u32[]{:S(2)}) %all-to-all-start.1) | async-done | bytes 524320 | tf_op jit(solution)/shard_map/all_to_all | solution.py:20
  72.0 1.2 %copy.30 = f32[128,4,2,128]{3,2,1,0:T(2,128)S(1)} copy(f32[128,4,2,128]{3,2,0,1:T(2,128)} %bitcast.16) | data formatting | bytes 1048576 | tf_op jit(solution)/shard_map/transpose | solution.py:63
  73.2 1.9 %collective-permute-start.3 = (f32[1024,128]{1,0:T(8,128)S(1)}, f32[1024,128]{1,0:T(8,128)S(1)}, u32[]{:S(2)}, u32[]{:S(2)}) collective-permute-start(f32[1024,128]{1,0:T(8,128)S(1)} %bitcast.44), channel_id=1, source_target_pairs={{0,508},{4,8},{8,4},{12,16},{16,12},{20,24},{24,20},{28,32},{32,28... | collective-permute-start | bytes 1572872 | tf_op jit(solution)/shard_map/ppermute | solution.py:71
  75.1 2.7 %collective-permute-start.4 = (f32[1024,128]{1,0:T(8,128)S(1)}, f32[1024,128]{1,0:T(8,128)S(1)}, u32[]{:S(2)}, u32[]{:S(2)}) collective-permute-start(f32[1024,128]{1,0:T(8,128)S(1)} %bitcast.45), channel_id=1, source_target_pairs={{0,4},{4,0},{8,12},{12,8},{16,20},{20,16},{24,28},{28,24},{32,36},... | collective-permute-start | bytes 1572872 | tf_op jit(solution)/shard_map/ppermute | solution.py:72
  77.9 1.4 %convolution_multiply_fusion = f32[6,128,128]{2,1,0:T(8,128)S(1)} fusion(f32[6,128,1024]{2,1,0:T(8,128)S(1)} %bitcast.41, f32[1024,128,1]{1,0,2:T(8,128)S(1)} %bitcast.46, f32[6]{0:T(128)S(1)} %get-tuple-element.6), kind=kOutput, calls=%fused_computation.14 | convolution fusion | flops 604078080 | bytes 4063256 | tf_op jit(solution)/shard_map/dot_general | solution.py:85
  79.3 7.7 %collective-permute-done.3 = f32[1024,128]{1,0:T(8,128)S(1)} collective-permute-done((f32[1024,128]{1,0:T(8,128)S(1)}, f32[1024,128]{1,0:T(8,128)S(1)}, u32[]{:S(2)}, u32[]{:S(2)}) %collective-permute-start.3) | collective-permute-done | bytes 524320 | tf_op jit(solution)/shard_map/ppermute | solution.py:71
  87.0 0.0 collective-permute-done.4
  87.0 2.8 %fusion.8 = f32[6,128,128]{2,1,0:T(8,128)} fusion(f32[6,128,128]{2,1,0:T(8,128)S(1)} %convolution_multiply_fusion, f32[6,128,1024]{2,1,0:T(8,128)S(1)} %bitcast.42, f32[1024,128]{1,0:T(8,128)S(1)} %collective-permute-done.4, f32[6]{0:T(128)S(1)} %get-tuple-element.7, f32[1024,128]{1,0:T(8,128)S(1)} %collective-permute-done.3, f32[6]{0:T(128)S(1)} %get-tuple-element.5), kind=kOutput, calls=%fused_computation.13 | convolution fusion | flops 606437376 | bytes 4980784 | tf_op jit(solution)/shard_map/irk,ikt->irt/dot_general | solution.py:88
  (8 shorter events, 0.1 us)
Async XLA Ops:
  0.0 36.0 %copy-start = (s32[128]{0:T(128)S(1)}, s32[128]{0:T(128)}, u32[]{:S(2)}) copy-start(s32[128]{0:T(128)} %param.13) | copy-start | bytes 1540
  0.0 24.3 %copy-start.1 = (f32[2,64,1,128]{3,2,1,0:T(1,128)S(1)}, f32[2,64,1,128]{3,2,1,0:T(1,128)}, u32[]{:S(2)}) copy-start(f32[2,64,1,128]{3,2,1,0:T(1,128)} %param.8) | copy-start | bytes 196612
  0.0 35.8 %copy-start.2 = (s32[128,16]{0,1:T(8,128)S(1)}, s32[128,16]{0,1:T(8,128)}, u32[]{:S(2)}) copy-start(s32[128,16]{0,1:T(8,128)} %param.11) | copy-start | bytes 24580
  0.0 37.2 %copy-start.3 = (f32[128,16]{0,1:T(8,128)S(1)}, f32[128,16]{0,1:T(8,128)}, u32[]{:S(2)}) copy-start(f32[128,16]{0,1:T(8,128)} %param.12) | copy-start | bytes 24580
  0.0 37.9 %copy-start.4 = (f32[768]{0:T(1024)S(1)}, f32[768]{0:T(1024)}, u32[]{:S(2)}) copy-start(f32[768]{0:T(1024)} %param.10) | copy-start | bytes 9220
  3.1 52.1 %all-to-all-start = ((f32[512,1,512]{2,1,0:T(1,128)}), f32[512,1,512]{2,1,0:T(1,128)S(1)}, u32[]{:S(2)}, u32[]{:S(2)}) async-start(f32[512,1,512]{2,1,0:T(1,128)} %bitcast.10), calls=%async_computation | async-start | bytes 2097152 | tf_op jit(solution)/shard_map/all_to_all | solution.py:56
  24.3 13.7 %collective-permute-start.2 = (f32[2,64,128]{2,1,0:T(8,128)S(1)}, f32[2,64,128]{2,1,0:T(8,128)S(1)}, u32[]{:S(2)}, u32[]{:S(2)}) collective-permute-start(f32[2,64,128]{2,1,0:T(8,128)S(1)} %bitcast.48), channel_id=1, source_target_pairs={{1,0},{2,1},{3,2},{0,3},{5,4},{6,5},{7,6},{4,7},{9,8},{10,9},{11,1... | collective-permute-start | bytes 196616 | tf_op jit(solution)/shard_map/ppermute | solution.py:14
  30.5 8.3 %collective-permute-start.1 = (f32[2,64,128]{2,1,0:T(8,128)S(1)}, f32[2,64,128]{2,1,0:T(8,128)S(1)}, u32[]{:S(2)}, u32[]{:S(2)}) collective-permute-start(f32[2,64,128]{2,1,0:T(8,128)S(1)} %bitcast.49), channel_id=1, source_target_pairs={{2,0},{3,1},{0,2},{1,3},{6,4},{7,5},{4,6},{5,7},{10,8},{11,9},{8,1... | collective-permute-start | bytes 196616 | tf_op jit(solution)/shard_map/ppermute | solution.py:14
  32.5 7.0 %collective-permute-start = (f32[2,64,128]{2,1,0:T(8,128)S(1)}, f32[2,64,128]{2,1,0:T(8,128)S(1)}, u32[]{:S(2)}, u32[]{:S(2)}) collective-permute-start(f32[2,64,128]{2,1,0:T(8,128)S(1)} %bitcast.50), channel_id=1, source_target_pairs={{3,0},{0,1},{1,2},{2,3},{7,4},{4,5},{5,6},{6,7},{11,8},{8,9},{9,10... | collective-permute-start | bytes 196616 | tf_op jit(solution)/shard_map/ppermute | solution.py:14
  57.3 14.7 %all-to-all-start.1 = ((f32[4,256,128]{2,1,0:T(8,128)}), f32[4,256,128]{2,1,0:T(8,128)}, u32[]{:S(2)}, u32[]{:S(2)}) async-start(f32[4,256,128]{2,1,0:T(8,128)} %broadcast_in_dim.16), calls=%async_computation.1 | async-start | bytes 1048576 | tf_op jit(solution)/shard_map/all_to_all | solution.py:20
  73.2 13.8 %collective-permute-start.3 = (f32[1024,128]{1,0:T(8,128)S(1)}, f32[1024,128]{1,0:T(8,128)S(1)}, u32[]{:S(2)}, u32[]{:S(2)}) collective-permute-start(f32[1024,128]{1,0:T(8,128)S(1)} %bitcast.44), channel_id=1, source_target_pairs={{0,508},{4,8},{8,4},{12,16},{16,12},{20,24},{24,20},{28,32},{32,28... | collective-permute-start | bytes 1572872 | tf_op jit(solution)/shard_map/ppermute | solution.py:71
  75.1 11.9 %collective-permute-start.4 = (f32[1024,128]{1,0:T(8,128)S(1)}, f32[1024,128]{1,0:T(8,128)S(1)}, u32[]{:S(2)}, u32[]{:S(2)}) collective-permute-start(f32[1024,128]{1,0:T(8,128)S(1)} %bitcast.45), channel_id=1, source_target_pairs={{0,4},{4,0},{8,12},{12,8},{16,20},{20,16},{24,28},{28,24},{32,36},... | collective-permute-start | bytes 1572872 | tf_op jit(solution)/shard_map/ppermute | solution.py:72

commit v18 on v17

--- a/solution.py
+++ b/solution.py
@@ -52,12 +52,12 @@
     width = columns // column_blocks
     pair = local_members // regions
     grid = fcst_pert.reshape(leads, regions, pair, column_blocks, width)
-    grid = jnp.transpose(grid, (3, 1, 0, 2, 4)).reshape(column_blocks * regions, -1)
+    grid = jnp.transpose(grid, (3, 1, 2, 0, 4)).reshape(column_blocks * regions, -1)
     arrived = lax.all_to_all(grid, ("mem", "dom"), 0, 0, tiled=True)
-    arrived = arrived.reshape(column_blocks, regions, leads, pair, width)
+    arrived = arrived.reshape(column_blocks, regions, pair, leads, width)
     targets = sensitivity.shape[1]
     levels = shifted_copies(sensitivity[:, :, 0, :], "dom")
-    quarter = jnp.einsum("mdljc,dltc->mjlt", arrived, levels, precision=HIGH)
+    quarter = jnp.einsum("mdjlc,dltc->mjlt", arrived, levels, precision=HIGH)
     quarter = quarter.reshape(column_blocks * pair, leads * targets)
     full = gathered(quarter, "dom").reshape(regions, column_blocks, pair, -1)
     summed = jnp.transpose(full, (1, 0, 2, 3)).reshape(column_blocks * local_members, -1)

time: 90.3 us -> 90.3 us (level)
  no operation moved by 1% of the time
where the time goes in v18:
time: 90.3 us; the launch traced here: 89.8 us
  starting transfers between devices  43.4 us (48%)
  waiting for transfers between devices  30.6 us (34%)
  local copies, waits for them, and re-layouts  8.15 us (9%)
  matrix products  5.08 us (6%)
  other arithmetic  2.45 us (3%)
    all_to_all x1, starting transfers between devices, body(): arrived = lax.all_to_all(grid, ('mem', 'dom'), 0, 0, tiled=True)  21.2 us
    all_to_all x1, waiting for transfers between devices, body(): arrived = lax.all_to_all(grid, ('mem', 'dom'), 0, 0, tiled=True)  15.1 us
    ppermute x3, starting transfers between devices, from_behind(): return lax.ppermute(block, axis, route)  11.5 us
    ppermute x1, waiting for transfers between devices, body(): far = lax.ppermute(summed, 'mem', cross)  7.75 us
    all_to_all x1, waiting for transfers between devices, gathered(): return lax.all_to_all(copies, axis, 0, 0, tiled=True)  6.27 us
    all_to_all x1, starting transfers between devices, gathered(): return lax.all_to_all(copies, axis, 0, 0, tiled=True)  6.08 us
    reshape x1, local copies, waits for them, and re-layouts, body(): grid = fcst_pert.reshape(leads, regions, pair, column_blocks, width)  3.07 us
    dot_general x1, matrix products, body(): jnp.einsum('irk,ikt->irt', rows, others, precision=HIGH)  2.84 us
  transfers between devices with their start and end apart: 7, of which 5 were waited for; matrix products, arithmetic and copies ran while one was open for 7% of the time, Pallas kernels for 0%

profile of v18, /device:TPU:2, one launch (start us, length us, event | category | flops | bytes accessed | tf_op | source)
XLA Modules:
  0.0 89.8 jit_solution(12819788715174459283)
XLA Ops:
  0.0 0.0 copy-start
  0.0 0.0 copy-start.1
  0.0 0.0 copy-start.2
  0.0 0.0 copy-start.3
  0.0 0.0 copy-start.4
  0.0 3.1 %copy.25 = f32[2,4,2,128,128]{4,0,2,1,3:T(2,128)} copy(f32[2,4,2,128,128]{4,3,2,1,0:T(8,128)} %bitcast.47) | data formatting | bytes 2097152 | tf_op jit(solution)/shard_map/reshape | solution.py:54
  3.1 21.2 %all-to-all-start = ((f32[512,1,512]{2,1,0:T(1,128)}), f32[512,1,512]{2,1,0:T(1,128)S(1)}, u32[]{:S(2)}, u32[]{:S(2)}) async-start(f32[512,1,512]{2,1,0:T(1,128)} %bitcast.10), calls=%async_computation | async-start | bytes 2097152 | tf_op jit(solution)/shard_map/all_to_all | solution.py:56
  24.3 0.0 copy-done.1
  24.3 6.2 %collective-permute-start.2 = (f32[2,64,128]{2,1,0:T(8,128)S(1)}, f32[2,64,128]{2,1,0:T(8,128)S(1)}, u32[]{:S(2)}, u32[]{:S(2)}) collective-permute-start(f32[2,64,128]{2,1,0:T(8,128)S(1)} %bitcast.48), channel_id=1, source_target_pairs={{1,0},{2,1},{3,2},{0,3},{5,4},{6,5},{7,6},{4,7},{9,8},{10,9},{11,1... | collective-permute-start | bytes 196616 | tf_op jit(solution)/shard_map/ppermute | solution.py:14
  30.5 1.9 %collective-permute-start.1 = (f32[2,64,128]{2,1,0:T(8,128)S(1)}, f32[2,64,128]{2,1,0:T(8,128)S(1)}, u32[]{:S(2)}, u32[]{:S(2)}) collective-permute-start(f32[2,64,128]{2,1,0:T(8,128)S(1)} %bitcast.49), channel_id=1, source_target_pairs={{2,0},{3,1},{0,2},{1,3},{6,4},{7,5},{4,6},{5,7},{10,8},{11,9},{8,1... | collective-permute-start | bytes 196616 | tf_op jit(solution)/shard_map/ppermute | solution.py:14
  32.5 3.4 %collective-permute-start = (f32[2,64,128]{2,1,0:T(8,128)S(1)}, f32[2,64,128]{2,1,0:T(8,128)S(1)}, u32[]{:S(2)}, u32[]{:S(2)}) collective-permute-start(f32[2,64,128]{2,1,0:T(8,128)S(1)} %bitcast.50), channel_id=1, source_target_pairs={{3,0},{0,1},{1,2},{2,3},{7,4},{4,5},{5,6},{6,7},{11,8},{8,9},{9,10... | collective-permute-start | bytes 196616 | tf_op jit(solution)/shard_map/ppermute | solution.py:14
  35.8 0.0 copy-done.2
  35.9 0.1 copy.31
  36.0 0.0 copy-done
  36.0 0.6 gather_fusion.1
  36.6 0.6 gather_fusion
  37.2 0.0 copy-done.3
  37.2 0.1 copy.32
  37.3 0.6 gather_fusion.2
  37.9 0.1 iota_compare_fusion
  38.0 0.0 copy-done.4
  38.0 0.0 collective-permute-done.2
  38.0 0.9 collective-permute-done.1
  38.8 0.6 collective-permute-done
  39.5 0.7 scatter_fusion
  40.2 15.1 %all-to-all-done = f32[512,1,512]{2,1,0:T(1,128)S(1)} async-done(((f32[512,1,512]{2,1,0:T(1,128)}), f32[512,1,512]{2,1,0:T(1,128)S(1)}, u32[]{:S(2)}, u32[]{:S(2)}) %all-to-all-start) | async-done | bytes 1048608 | tf_op jit(solution)/shard_map/all_to_all | solution.py:56
  55.2 0.8 convolution_bitcast_fusion
  56.1 0.2 copy.29
  56.3 0.2 broadcast_in_dim.15
  56.5 0.8 broadcast_in_dim.16
  57.3 6.1 %all-to-all-start.1 = ((f32[4,256,128]{2,1,0:T(8,128)}), f32[4,256,128]{2,1,0:T(8,128)}, u32[]{:S(2)}, u32[]{:S(2)}) async-start(f32[4,256,128]{2,1,0:T(8,128)} %broadcast_in_dim.16), calls=%async_computation.1 | async-start | bytes 1048576 | tf_op jit(solution)/shard_map/all_to_all | solution.py:20
  63.4 0.2 select_reduce_fusion
  63.5 2.2 %broadcast_multiply_fusion = f32[768,1024]{1,0:T(8,128)S(1)} fusion(f32[768,1024]{1,0:T(8,128)} %param.9, f32[768]{0:T(1024)S(1)} %broadcast_multiply_fusion.1), kind=kLoop, calls=%fused_computation.12 | loop fusion | flops 786432 | bytes 6294528 | tf_op jit(solution)/shard_map/mul | solution.py:84
  65.7 6.3 %all-to-all-done.1 = f32[4,256,128]{2,1,0:T(8,128)} async-done(((f32[4,256,128]{2,1,0:T(8,128)}), f32[4,256,128]{2,1,0:T(8,128)}, u32[]{:S(2)}, u32[]{:S(2)}) %all-to-all-start.1) | async-done | bytes 524320 | tf_op jit(solution)/shard_map/all_to_all | solution.py:20
  72.0 1.2 %copy.30 = f32[128,4,2,128]{3,2,1,0:T(2,128)S(1)} copy(f32[128,4,2,128]{3,2,0,1:T(2,128)} %bitcast.16) | data formatting | bytes 1048576 | tf_op jit(solution)/shard_map/transpose | solution.py:63
  73.2 1.9 %collective-permute-start.3 = (f32[1024,128]{1,0:T(8,128)S(1)}, f32[1024,128]{1,0:T(8,128)S(1)}, u32[]{:S(2)}, u32[]{:S(2)}) collective-permute-start(f32[1024,128]{1,0:T(8,128)S(1)} %bitcast.44), channel_id=1, source_target_pairs={{0,508},{4,8},{8,4},{12,16},{16,12},{20,24},{24,20},{28,32},{32,28... | collective-permute-start | bytes 1572872 | tf_op jit(solution)/shard_map/ppermute | solution.py:71
  75.1 2.7 %collective-permute-start.4 = (f32[1024,128]{1,0:T(8,128)S(1)}, f32[1024,128]{1,0:T(8,128)S(1)}, u32[]{:S(2)}, u32[]{:S(2)}) collective-permute-start(f32[1024,128]{1,0:T(8,128)S(1)} %bitcast.45), channel_id=1, source_target_pairs={{0,4},{4,0},{8,12},{12,8},{16,20},{20,16},{24,28},{28,24},{32,36},... | collective-permute-start | bytes 1572872 | tf_op jit(solution)/shard_map/ppermute | solution.py:72
  77.9 1.4 %convolution_multiply_fusion = f32[6,128,128]{2,1,0:T(8,128)S(1)} fusion(f32[6,128,1024]{2,1,0:T(8,128)S(1)} %bitcast.41, f32[1024,128,1]{1,0,2:T(8,128)S(1)} %bitcast.46, f32[6]{0:T(128)S(1)} %get-tuple-element.6), kind=kOutput, calls=%fused_computation.14 | convolution fusion | flops 604078080 | bytes 4063256 | tf_op jit(solution)/shard_map/dot_general | solution.py:85
  79.3 7.7 %collective-permute-done.3 = f32[1024,128]{1,0:T(8,128)S(1)} collective-permute-done((f32[1024,128]{1,0:T(8,128)S(1)}, f32[1024,128]{1,0:T(8,128)S(1)}, u32[]{:S(2)}, u32[]{:S(2)}) %collective-permute-start.3) | collective-permute-done | bytes 524320 | tf_op jit(solution)/shard_map/ppermute | solution.py:71
  87.0 0.0 collective-permute-done.4
  87.0 2.8 %fusion.8 = f32[6,128,128]{2,1,0:T(8,128)} fusion(f32[6,128,128]{2,1,0:T(8,128)S(1)} %convolution_multiply_fusion, f32[6,128,1024]{2,1,0:T(8,128)S(1)} %bitcast.42, f32[1024,128]{1,0:T(8,128)S(1)} %collective-permute-done.4, f32[6]{0:T(128)S(1)} %get-tuple-element.7, f32[1024,128]{1,0:T(8,128)S(1)} %collective-permute-done.3, f32[6]{0:T(128)S(1)} %get-tuple-element.5), kind=kOutput, calls=%fused_computation.13 | convolution fusion | flops 606437376 | bytes 4980784 | tf_op jit(solution)/shard_map/irk,ikt->irt/dot_general | solution.py:88
  (8 shorter events, 0.1 us)
Async XLA Ops:
  0.0 36.0 %copy-start = (s32[128]{0:T(128)S(1)}, s32[128]{0:T(128)}, u32[]{:S(2)}) copy-start(s32[128]{0:T(128)} %param.13) | copy-start | bytes 1540
  0.0 24.3 %copy-start.1 = (f32[2,64,1,128]{3,2,1,0:T(1,128)S(1)}, f32[2,64,1,128]{3,2,1,0:T(1,128)}, u32[]{:S(2)}) copy-start(f32[2,64,1,128]{3,2,1,0:T(1,128)} %param.8) | copy-start | bytes 196612
  0.0 35.8 %copy-start.2 = (s32[128,16]{0,1:T(8,128)S(1)}, s32[128,16]{0,1:T(8,128)}, u32[]{:S(2)}) copy-start(s32[128,16]{0,1:T(8,128)} %param.11) | copy-start | bytes 24580
  0.0 37.2 %copy-start.3 = (f32[128,16]{0,1:T(8,128)S(1)}, f32[128,16]{0,1:T(8,128)}, u32[]{:S(2)}) copy-start(f32[128,16]{0,1:T(8,128)} %param.12) | copy-start | bytes 24580
  0.0 37.9 %copy-start.4 = (f32[768]{0:T(1024)S(1)}, f32[768]{0:T(1024)}, u32[]{:S(2)}) copy-start(f32[768]{0:T(1024)} %param.10) | copy-start | bytes 9220
  3.1 52.1 %all-to-all-start = ((f32[512,1,512]{2,1,0:T(1,128)}), f32[512,1,512]{2,1,0:T(1,128)S(1)}, u32[]{:S(2)}, u32[]{:S(2)}) async-start(f32[512,1,512]{2,1,0:T(1,128)} %bitcast.10), calls=%async_computation | async-start | bytes 2097152 | tf_op jit(solution)/shard_map/all_to_all | solution.py:56
  24.3 13.7 %collective-permute-start.2 = (f32[2,64,128]{2,1,0:T(8,128)S(1)}, f32[2,64,128]{2,1,0:T(8,128)S(1)}, u32[]{:S(2)}, u32[]{:S(2)}) collective-permute-start(f32[2,64,128]{2,1,0:T(8,128)S(1)} %bitcast.48), channel_id=1, source_target_pairs={{1,0},{2,1},{3,2},{0,3},{5,4},{6,5},{7,6},{4,7},{9,8},{10,9},{11,1... | collective-permute-start | bytes 196616 | tf_op jit(solution)/shard_map/ppermute | solution.py:14
  30.5 8.3 %collective-permute-start.1 = (f32[2,64,128]{2,1,0:T(8,128)S(1)}, f32[2,64,128]{2,1,0:T(8,128)S(1)}, u32[]{:S(2)}, u32[]{:S(2)}) collective-permute-start(f32[2,64,128]{2,1,0:T(8,128)S(1)} %bitcast.49), channel_id=1, source_target_pairs={{2,0},{3,1},{0,2},{1,3},{6,4},{7,5},{4,6},{5,7},{10,8},{11,9},{8,1... | collective-permute-start | bytes 196616 | tf_op jit(solution)/shard_map/ppermute | solution.py:14
  32.5 7.0 %collective-permute-start = (f32[2,64,128]{2,1,0:T(8,128)S(1)}, f32[2,64,128]{2,1,0:T(8,128)S(1)}, u32[]{:S(2)}, u32[]{:S(2)}) collective-permute-start(f32[2,64,128]{2,1,0:T(8,128)S(1)} %bitcast.50), channel_id=1, source_target_pairs={{3,0},{0,1},{1,2},{2,3},{7,4},{4,5},{5,6},{6,7},{11,8},{8,9},{9,10... | collective-permute-start | bytes 196616 | tf_op jit(solution)/shard_map/ppermute | solution.py:14
  57.3 14.7 %all-to-all-start.1 = ((f32[4,256,128]{2,1,0:T(8,128)}), f32[4,256,128]{2,1,0:T(8,128)}, u32[]{:S(2)}, u32[]{:S(2)}) async-start(f32[4,256,128]{2,1,0:T(8,128)} %broadcast_in_dim.16), calls=%async_computation.1 | async-start | bytes 1048576 | tf_op jit(solution)/shard_map/all_to_all | solution.py:20
  73.2 13.8 %collective-permute-start.3 = (f32[1024,128]{1,0:T(8,128)S(1)}, f32[1024,128]{1,0:T(8,128)S(1)}, u32[]{:S(2)}, u32[]{:S(2)}) collective-permute-start(f32[1024,128]{1,0:T(8,128)S(1)} %bitcast.44), channel_id=1, source_target_pairs={{0,508},{4,8},{8,4},{12,16},{16,12},{20,24},{24,20},{28,32},{32,28... | collective-permute-start | bytes 1572872 | tf_op jit(solution)/shard_map/ppermute | solution.py:71
  75.1 11.9 %collective-permute-start.4 = (f32[1024,128]{1,0:T(8,128)S(1)}, f32[1024,128]{1,0:T(8,128)S(1)}, u32[]{:S(2)}, u32[]{:S(2)}) collective-permute-start(f32[1024,128]{1,0:T(8,128)S(1)} %bitcast.45), channel_id=1, source_target_pairs={{0,4},{4,0},{8,12},{12,8},{16,20},{20,16},{24,28},{28,24},{32,36},... | collective-permute-start | bytes 1572872 | tf_op jit(solution)/shard_map/ppermute | solution.py:72

commit v19 on v18

--- a/solution.py
+++ b/solution.py
@@ -57,6 +57,8 @@
     arrived = arrived.reshape(column_blocks, regions, pair, leads, width)
     targets = sensitivity.shape[1]
     levels = shifted_copies(sensitivity[:, :, 0, :], "dom")
+    rows = obs_pert * (weighted_innovation / (M - 1))[:, None]
+    levels, rows = lax.optimization_barrier((levels, rows))
     quarter = jnp.einsum("mdjlc,dltc->mjlt", arrived, levels, precision=HIGH)
     quarter = quarter.reshape(column_blocks * pair, leads * targets)
     full = gathered(quarter, "dom").reshape(regions, column_blocks, pair, -1)
@@ -80,8 +82,6 @@
         weight_rows[1],
         jnp.where(even, weight_rows[2], weight_rows[0]),
     )
-    scale = (weighted_innovation / (M - 1))[:, None]
-    rows = obs_pert * scale
     own = jnp.dot(rows, summed, precision=HIGH).reshape(owned_blocks, OBSB, -1)
     rows = rows.reshape(owned_blocks, OBSB, -1)
     others = weight_rows[0][:, None, None] * behind[None] + weight_rows[2][:, None, None] * ahead[None]

time: 90.3 us -> 91.7 us (1.016)
  waiting for transfers between devices: 30.6 us -> 26.2 us
  starting transfers between devices: 43.4 us -> 45.5 us
  local copies, waits for them, and re-layouts: 8.15 us -> 9.77 us
  matrix products: 5.08 us -> 6.3 us
    all_to_all x1, waiting for transfers between devices: 15.1 us -> 11.9 us  [body(): arrived = lax.all_to_all(grid, ('mem', 'dom'), 0, 0, tiled=True)]
    all_to_all x1, starting transfers between devices: 21.2 us -> 23.3 us  [body(): arrived = lax.all_to_all(grid, ('mem', 'dom'), 0, 0, tiled=True)]
    dot_general x1, matrix products: 0.85 us -> 2.07 us  [body(): quarter = jnp.einsum('mdjlc,dltc->mjlt', arrived, levels, precision=HIGH)]
    scatter x1, local copies, waits for them, and re-layouts: 0.66 us -> 1.58 us  [shifted_copies(): return slots.at[order].set(jnp.stack(arrived))]
  transfers between devices with their start and end apart: 7 -> 7, of which waited for: 5 -> 5; matrix products, arithmetic and copies ran while one was open for 7% -> 10% of each run, Pallas kernels for 0% -> 0%
where the time goes in v19:
time: 91.7 us; the launch traced here: 91.2 us
  starting transfers between devices  45.5 us (50%)
  waiting for transfers between devices  26.2 us (29%)
  local copies, waits for them, and re-layouts  9.77 us (11%)
  matrix products  6.3 us (7%)
  other arithmetic  3.16 us (3%)
    all_to_all x1, starting transfers between devices, body(): arrived = lax.all_to_all(grid, ('mem', 'dom'), 0, 0, tiled=True)  23.3 us
    all_to_all x1, waiting for transfers between devices, body(): arrived = lax.all_to_all(grid, ('mem', 'dom'), 0, 0, tiled=True)  11.9 us
    ppermute x3, starting transfers between devices, from_behind(): return lax.ppermute(block, axis, route)  11.6 us
    ppermute x1, waiting for transfers between devices, body(): far = lax.ppermute(summed, 'mem', cross)  7.75 us
    all_to_all x1, starting transfers between devices, gathered(): return lax.all_to_all(copies, axis, 0, 0, tiled=True)  6.07 us
    all_to_all x1, waiting for transfers between devices, gathered(): return lax.all_to_all(copies, axis, 0, 0, tiled=True)  5.71 us
    reshape x1, local copies, waits for them, and re-layouts, body(): grid = fcst_pert.reshape(leads, regions, pair, column_blocks, width)  3.09 us
    dot_general x1, matrix products, body(): jnp.einsum('irk,ikt->irt', rows, others, precision=HIGH)  2.84 us
  transfers between devices with their start and end apart: 7, of which 5 were waited for; matrix products, arithmetic and copies ran while one was open for 10% of the time, Pallas kernels for 0%

profile of v19, /device:TPU:2, one launch (start us, length us, event | category | flops | bytes accessed | tf_op | source)
XLA Modules:
  0.0 91.2 jit_solution(9947312462930427375)
XLA Ops:
  0.0 0.0 copy-start
  0.0 0.0 copy-start.1
  0.0 0.0 copy-start.3
  0.0 3.1 %copy.25 = f32[2,4,2,128,128]{4,0,2,1,3:T(2,128)} copy(f32[2,4,2,128,128]{4,3,2,1,0:T(8,128)} %bitcast.46) | data formatting | bytes 2097152 | tf_op jit(solution)/shard_map/reshape | solution.py:54
  3.1 23.3 %all-to-all-start = ((f32[512,1,512]{2,1,0:T(1,128)}), f32[512,1,512]{2,1,0:T(1,128)}, u32[]{:S(2)}, u32[]{:S(2)}) async-start(f32[512,1,512]{2,1,0:T(1,128)} %bitcast.10), calls=%async_computation | async-start | bytes 2097152 | tf_op jit(solution)/shard_map/all_to_all | solution.py:56
  26.4 0.0 copy-done.1
  26.4 6.3 %collective-permute-start.2 = (f32[2,64,128]{2,1,0:T(8,128)S(1)}, f32[2,64,128]{2,1,0:T(8,128)S(1)}, u32[]{:S(2)}, u32[]{:S(2)}) collective-permute-start(f32[2,64,128]{2,1,0:T(8,128)S(1)} %bitcast.47), channel_id=1, source_target_pairs={{1,0},{2,1},{3,2},{0,3},{5,4},{6,5},{7,6},{4,7},{9,8},{10,9},{11,1... | collective-permute-start | bytes 196616 | tf_op jit(solution)/shard_map/ppermute | solution.py:14
  32.7 1.9 %collective-permute-start.1 = (f32[2,64,128]{2,1,0:T(8,128)S(1)}, f32[2,64,128]{2,1,0:T(8,128)S(1)}, u32[]{:S(2)}, u32[]{:S(2)}) collective-permute-start(f32[2,64,128]{2,1,0:T(8,128)S(1)} %bitcast.48), channel_id=1, source_target_pairs={{2,0},{3,1},{0,2},{1,3},{6,4},{7,5},{4,6},{5,7},{10,8},{11,9},{8,1... | collective-permute-start | bytes 196616 | tf_op jit(solution)/shard_map/ppermute | solution.py:14
  34.6 3.4 %collective-permute-start = (f32[2,64,128]{2,1,0:T(8,128)S(1)}, f32[2,64,128]{2,1,0:T(8,128)S(1)}, u32[]{:S(2)}, u32[]{:S(2)}) collective-permute-start(f32[2,64,128]{2,1,0:T(8,128)S(1)} %bitcast.49), channel_id=1, source_target_pairs={{3,0},{0,1},{1,2},{2,3},{7,4},{4,5},{5,6},{6,7},{11,8},{8,9},{9,10... | collective-permute-start | bytes 196616 | tf_op jit(solution)/shard_map/ppermute | solution.py:14
  38.0 0.0 copy-done.3
  38.0 2.2 %broadcast_multiply_fusion = f32[768,1024]{1,0:T(8,128)S(1)} fusion(f32[768,1024]{1,0:T(8,128)} %param.9, f32[768]{0:T(1024)S(1)} %broadcast_multiply_fusion.1), kind=kLoop, calls=%fused_computation.12 | loop fusion | flops 786432 | bytes 6294528 | tf_op jit(solution)/shard_map/mul | solution.py:60
  40.2 0.0 copy-start.2
  40.2 0.0 collective-permute-done.2
  40.3 0.7 collective-permute-done.1
  40.9 0.2 collective-permute-done
  41.1 0.7 pad_maximum_fusion
  41.9 1.6 %scatter_fusion = f32[4,2,64,128]{3,2,1,0:T(8,128)S(1)} fusion(f32[4,2,64,128]{3,2,1,0:T(8,128)S(1)} %broadcast_in_dim.14, s32[4]{0:T(128)S(1)} %fusion.17, f32[4,2,64,128]{3,2,1,0:T(8,128)} %pad_maximum_fusion), kind=kCustom, calls=%fused_computation.3 | custom fusion | bytes 786448 | tf_op jit(solution)/shard_map/scatter | solution.py:29
  43.4 11.9 %all-to-all-done = f32[512,1,512]{2,1,0:T(1,128)} async-done(((f32[512,1,512]{2,1,0:T(1,128)}), f32[512,1,512]{2,1,0:T(1,128)}, u32[]{:S(2)}, u32[]{:S(2)}) %all-to-all-start) | async-done | bytes 1048608 | tf_op jit(solution)/shard_map/all_to_all | solution.py:56
  55.3 2.1 %convolution_bitcast_fusion = f32[128,2,2,64]{0,3,1,2:T(8,128)S(1)} fusion(f32[128,4,2,2,128]{4,3,2,1,0:T(2,128)} %bitcast.11, f32[4,2,64,128]{3,2,1,0:T(8,128)S(1)} %scatter_fusion), kind=kOutput, calls=%fused_computation.15 | convolution fusion | flops 100663296 | bytes 1441792 | tf_op jit(solution)/shard_map/mdjlc,dltc->mjlt/dot_general | solution.py:62
  57.4 0.2 copy.29
  57.6 0.2 broadcast_in_dim.15
  57.8 0.8 broadcast_in_dim.16
  58.6 6.1 %all-to-all-start.1 = ((f32[4,256,128]{2,1,0:T(8,128)}), f32[4,256,128]{2,1,0:T(8,128)}, u32[]{:S(2)}, u32[]{:S(2)}) async-start(f32[4,256,128]{2,1,0:T(8,128)} %broadcast_in_dim.16), calls=%async_computation.1 | async-start | bytes 1048576 | tf_op jit(solution)/shard_map/all_to_all | solution.py:20
  64.7 0.0 copy-done.2
  64.7 0.1 copy.31
  64.8 0.0 copy-done
  64.8 0.6 gather_fusion.1
  65.4 0.6 gather_fusion
  66.0 0.8 copy.32
  66.8 0.6 gather_fusion.2
  67.3 0.1 iota_compare_fusion
  67.4 0.2 select_reduce_fusion
  67.6 5.7 %all-to-all-done.1 = f32[4,256,128]{2,1,0:T(8,128)} async-done(((f32[4,256,128]{2,1,0:T(8,128)}), f32[4,256,128]{2,1,0:T(8,128)}, u32[]{:S(2)}, u32[]{:S(2)}) %all-to-all-start.1) | async-done | bytes 524320 | tf_op jit(solution)/shard_map/all_to_all | solution.py:20
  73.3 1.2 %copy.30 = f32[128,4,2,128]{3,2,1,0:T(2,128)S(1)} copy(f32[128,4,2,128]{3,2,0,1:T(2,128)} %bitcast.16) | data formatting | bytes 1048576 | tf_op jit(solution)/shard_map/transpose | solution.py:65
  74.5 1.9 %collective-permute-start.3 = (f32[1024,128]{1,0:T(8,128)S(1)}, f32[1024,128]{1,0:T(8,128)S(1)}, u32[]{:S(2)}, u32[]{:S(2)}) collective-permute-start(f32[1024,128]{1,0:T(8,128)S(1)} %bitcast.43), channel_id=1, source_target_pairs={{0,508},{4,8},{8,4},{12,16},{16,12},{20,24},{24,20},{28,32},{32,28... | collective-permute-start | bytes 1572872 | tf_op jit(solution)/shard_map/ppermute | solution.py:73
  76.4 2.7 %collective-permute-start.4 = (f32[1024,128]{1,0:T(8,128)S(1)}, f32[1024,128]{1,0:T(8,128)S(1)}, u32[]{:S(2)}, u32[]{:S(2)}) collective-permute-start(f32[1024,128]{1,0:T(8,128)S(1)} %bitcast.44), channel_id=1, source_target_pairs={{0,4},{4,0},{8,12},{12,8},{16,20},{20,16},{24,28},{28,24},{32,36},... | collective-permute-start | bytes 1572872 | tf_op jit(solution)/shard_map/ppermute | solution.py:74
  79.2 1.4 %convolution_multiply_fusion = f32[6,128,128]{2,1,0:T(8,128)S(1)} fusion(f32[6,128,1024]{2,1,0:T(8,128)S(1)} %bitcast.41, f32[1024,128,1]{1,0,2:T(8,128)S(1)} %bitcast.45, f32[6]{0:T(128)S(1)} %get-tuple-element.10), kind=kOutput, calls=%fused_computation.14 | convolution fusion | flops 604078080 | bytes 4063256 | tf_op jit(solution)/shard_map/dot_general | solution.py:85
  80.6 7.8 %collective-permute-done.3 = f32[1024,128]{1,0:T(8,128)S(1)} collective-permute-done((f32[1024,128]{1,0:T(8,128)S(1)}, f32[1024,128]{1,0:T(8,128)S(1)}, u32[]{:S(2)}, u32[]{:S(2)}) %collective-permute-start.3) | collective-permute-done | bytes 524320 | tf_op jit(solution)/shard_map/ppermute | solution.py:73
  88.3 0.0 collective-permute-done.4
  88.3 2.8 %fusion.8 = f32[6,128,128]{2,1,0:T(8,128)} fusion(f32[6,128,128]{2,1,0:T(8,128)S(1)} %convolution_multiply_fusion, f32[6,128,1024]{2,1,0:T(8,128)S(1)} %bitcast.42, f32[1024,128]{1,0:T(8,128)S(1)} %collective-permute-done.4, f32[6]{0:T(128)S(1)} %get-tuple-element.11, f32[1024,128]{1,0:T(8,128)S(1)} %collective-permute-done.3, f32[6]{0:T(128)S(1)} %get-tuple-element.9), kind=kOutput, calls=%fused_computation.13 | convolution fusion | flops 606437376 | bytes 4980784 | tf_op jit(solution)/shard_map/irk,ikt->irt/dot_general | solution.py:88
  (7 shorter events, 0.1 us)
Async XLA Ops:
  0.0 64.8 %copy-start = (s32[128]{0:T(128)S(1)}, s32[128]{0:T(128)}, u32[]{:S(2)}) copy-start(s32[128]{0:T(128)} %param.13) | copy-start | bytes 1540
  0.0 26.4 %copy-start.1 = (f32[2,64,1,128]{3,2,1,0:T(1,128)S(1)}, f32[2,64,1,128]{3,2,1,0:T(1,128)}, u32[]{:S(2)}) copy-start(f32[2,64,1,128]{3,2,1,0:T(1,128)} %param.8) | copy-start | bytes 196612
  0.0 38.0 %copy-start.3 = (f32[768]{0:T(1024)S(1)}, f32[768]{0:T(1024)}, u32[]{:S(2)}) copy-start(f32[768]{0:T(1024)} %param.10) | copy-start | bytes 9220
  3.1 52.2 %all-to-all-start = ((f32[512,1,512]{2,1,0:T(1,128)}), f32[512,1,512]{2,1,0:T(1,128)}, u32[]{:S(2)}, u32[]{:S(2)}) async-start(f32[512,1,512]{2,1,0:T(1,128)} %bitcast.10), calls=%async_computation | async-start | bytes 2097152 | tf_op jit(solution)/shard_map/all_to_all | solution.py:56
  26.4 13.9 %collective-permute-start.2 = (f32[2,64,128]{2,1,0:T(8,128)S(1)}, f32[2,64,128]{2,1,0:T(8,128)S(1)}, u32[]{:S(2)}, u32[]{:S(2)}) collective-permute-start(f32[2,64,128]{2,1,0:T(8,128)S(1)} %bitcast.47), channel_id=1, source_target_pairs={{1,0},{2,1},{3,2},{0,3},{5,4},{6,5},{7,6},{4,7},{9,8},{10,9},{11,1... | collective-permute-start | bytes 196616 | tf_op jit(solution)/shard_map/ppermute | solution.py:14
  32.7 8.3 %collective-permute-start.1 = (f32[2,64,128]{2,1,0:T(8,128)S(1)}, f32[2,64,128]{2,1,0:T(8,128)S(1)}, u32[]{:S(2)}, u32[]{:S(2)}) collective-permute-start(f32[2,64,128]{2,1,0:T(8,128)S(1)} %bitcast.48), channel_id=1, source_target_pairs={{2,0},{3,1},{0,2},{1,3},{6,4},{7,5},{4,6},{5,7},{10,8},{11,9},{8,1... | collective-permute-start | bytes 196616 | tf_op jit(solution)/shard_map/ppermute | solution.py:14
  34.6 6.5 %collective-permute-start = (f32[2,64,128]{2,1,0:T(8,128)S(1)}, f32[2,64,128]{2,1,0:T(8,128)S(1)}, u32[]{:S(2)}, u32[]{:S(2)}) collective-permute-start(f32[2,64,128]{2,1,0:T(8,128)S(1)} %bitcast.49), channel_id=1, source_target_pairs={{3,0},{0,1},{1,2},{2,3},{7,4},{4,5},{5,6},{6,7},{11,8},{8,9},{9,10... | collective-permute-start | bytes 196616 | tf_op jit(solution)/shard_map/ppermute | solution.py:14
  40.2 24.5 %copy-start.2 = (s32[128,16]{0,1:T(8,128)S(1)}, s32[128,16]{0,1:T(8,128)}, u32[]{:S(2)}) copy-start(s32[128,16]{0,1:T(8,128)} %param.11) | copy-start | bytes 24580
  58.6 14.7 %all-to-all-start.1 = ((f32[4,256,128]{2,1,0:T(8,128)}), f32[4,256,128]{2,1,0:T(8,128)}, u32[]{:S(2)}, u32[]{:S(2)}) async-start(f32[4,256,128]{2,1,0:T(8,128)} %broadcast_in_dim.16), calls=%async_computation.1 | async-start | bytes 1048576 | tf_op jit(solution)/shard_map/all_to_all | solution.py:20
  74.5 13.8 %collective-permute-start.3 = (f32[1024,128]{1,0:T(8,128)S(1)}, f32[1024,128]{1,0:T(8,128)S(1)}, u32[]{:S(2)}, u32[]{:S(2)}) collective-permute-start(f32[1024,128]{1,0:T(8,128)S(1)} %bitcast.43), channel_id=1, source_target_pairs={{0,508},{4,8},{8,4},{12,16},{16,12},{20,24},{24,20},{28,32},{32,28... | collective-permute-start | bytes 1572872 | tf_op jit(solution)/shard_map/ppermute | solution.py:73
  76.4 11.9 %collective-permute-start.4 = (f32[1024,128]{1,0:T(8,128)S(1)}, f32[1024,128]{1,0:T(8,128)S(1)}, u32[]{:S(2)}, u32[]{:S(2)}) collective-permute-start(f32[1024,128]{1,0:T(8,128)S(1)} %bitcast.44), channel_id=1, source_target_pairs={{0,4},{4,0},{8,12},{12,8},{16,20},{20,16},{24,28},{28,24},{32,36},... | collective-permute-start | bytes 1572872 | tf_op jit(solution)/shard_map/ppermute | solution.py:74
